TPU v7x, 512 devices: a whole 4x4x16 slice. The times are simulated.
512 devices in a mesh: rows: 32 (over x, y, core), cols: 16 (over z).
Axes of the slice: x: 4, y: 4, z: 16, core: 2. Of those that a mesh axis runs over, the one named last changes fastest.
Arguments:
- panel_t: float32 [256, 65536], P('cols', 'rows'), as said below
- trailing: float32 [65536, 4096], P('rows', 'cols'), may hold values from -6 to 6
- prev_lower_t: float32 [256, 65536], P('cols', 'rows'), may hold values from -6 to 6
- prev_upper: float32 [256, 4096], P(None, 'cols'), may hold values from -0.375 to 0.375
- leaf_picks: int32 [32, 256], P('rows'), may hold values from 0 to 2047, as said below
- merge_picks: int32 [31, 256], replicated, may hold values from 0 to 511, as said below
Outputs:
- lower_t: float32 [256, 65536], P('cols', 'rows')
- upper_left: float32 [256, 256], replicated
- upper_right: float32 [256, 4096], P(None, 'cols')
- updated: float32 [65536, 4096], P('rows', 'cols')
- gram: float32 [256, 256], P('cols')
Inputs may be any that keep to these rules, and one draw needn't show every extreme that they name: `leaf_picks`: each row lists 256 different row numbers within the 2048 rows of one index of rows. `merge_picks`: each row lists 256 different positions in a stack of two candidate lists. `panel_t`: the rows of the panel at the pivots form a strictly diagonally dominant block.
All inputs are finite; a program needn't handle non-finite values.
Results may differ from a plain program's by a relative error of at most 0.0003.
Values sent between devices are 32-bit elements; how exact they have to be, the bound alone decides.
No kernel may reach another device: no remote copies, remote signals or barrier semaphores. Data moves between devices by JAX's collectives and lax.ppermute only.
A program may use at most 64 MiB of HBM per device.

v0:
```python
import jax
import jax.numpy as jnp
from jax import lax
from jax.sharding import PartitionSpec as P

full_precision = lax.Precision.HIGHEST


def from_partner(shard, axis, apart):
    return lax.ppermute(shard, axis, [(i, i ^ 1 << apart) for i in range(lax.axis_size(axis))])


def trace_pivots(merge_picks, row_devices):
    list_width = merge_picks.shape[1]
    leaf_group = jnp.zeros((list_width,), jnp.int32)
    leaf_slot = jnp.arange(list_width, dtype=jnp.int32)
    levels = row_devices.bit_length() - 1
    for section in reversed(range(levels)):
        offset_rows = row_devices - (row_devices >> section)
        position = merge_picks[offset_rows + leaf_group, leaf_slot]
        right_side = (position >= list_width).astype(jnp.int32)
        leaf_group = 2 * leaf_group + right_side
        leaf_slot = position - list_width * right_side
    return (leaf_group, leaf_slot)


def product(left_side, right_side):
    return jnp.dot(left_side, right_side, precision=full_precision)


def unit_lower_inverse(lower):
    order = lower.shape[0]
    identity = jnp.eye(order, dtype=jnp.float32)
    power = identity - lower
    result = identity + power
    covered = 1
    while covered < order - 1:
        power = product(power, power)
        result = product(result, identity + power)
        covered = 2 * covered + 1
    return result


def upper_inverse(upper):
    diagonal = jnp.diagonal(upper)
    scaled = upper / diagonal[:, None]
    unit_inverse = unit_lower_inverse(scaled.T).T
    return unit_inverse / diagonal[None, :]


def small_factor(matrix):
    order = matrix.shape[0]
    row_index = lax.broadcasted_iota(jnp.int32, (order, order), 0)
    col_index = lax.broadcasted_iota(jnp.int32, (order, order), 1)
    line_index = jnp.arange(order, dtype=jnp.int32)
    reduced = matrix
    for column_index in range(order - 1):
        pivot_line = jnp.sum(jnp.where(row_index == column_index, reduced, 0.0), 0)
        pivot_column = jnp.sum(jnp.where(col_index == column_index, reduced, 0.0), 1)
        pivot_value = jnp.sum(jnp.where(line_index == column_index, pivot_line, 0.0))
        factors = jnp.where(line_index > column_index, pivot_column / pivot_value, 0.0)
        below = row_index > column_index
        reduced = jnp.where(
            below & (col_index > column_index),
            reduced - factors[:, None] * pivot_line[None, :],
            reduced,
        )
        reduced = jnp.where(below & (col_index == column_index), factors[:, None], reduced)
    return (jnp.tril(reduced, -1) + jnp.eye(order, dtype=matrix.dtype), jnp.triu(reduced))


def factor(matrix):
    order = matrix.shape[0]
    if order <= 32:
        return small_factor(matrix)
    middle_index = order // 2
    lower_head, upper_head = factor(matrix[:middle_index, :middle_index])
    upper_side = product(unit_lower_inverse(lower_head), matrix[:middle_index, middle_index:])
    lower_side = product(matrix[middle_index:, :middle_index], upper_inverse(upper_head))
    schur_block = matrix[middle_index:, middle_index:] - product(lower_side, upper_side)
    lower_tail, upper_tail = factor(schur_block)
    zero_upper = jnp.zeros((middle_index, order - middle_index), matrix.dtype)
    zero_lower = jnp.zeros((order - middle_index, middle_index), matrix.dtype)
    lower_full = jnp.concatenate(
        [
            jnp.concatenate([lower_head, zero_upper], 1),
            jnp.concatenate([lower_side, lower_tail], 1),
        ],
        0,
    )
    upper_full = jnp.concatenate(
        [
            jnp.concatenate([upper_head, upper_side], 1),
            jnp.concatenate([zero_lower, upper_tail], 1),
        ],
        0,
    )
    return (lower_full, upper_full)


def contract_first(left_side, right_side):
    return lax.dot_general(
        left_side, right_side, (((0,), (0,)), ((), ())), precision=full_precision
    )


def contract_second(left_side, right_side):
    return lax.dot_general(
        left_side, right_side, (((1,), (1,)), ((), ())), precision=full_precision
    )


def body(panel_t, trailing, prev_lower_t, prev_upper, leaf_picks, merge_picks):
    slab_rows = panel_t.shape[0]
    rows_here = panel_t.shape[1]
    row_devices = lax.axis_size("rows")
    own_row = lax.axis_index("rows")
    own_column = lax.axis_index("cols")
    leaf_group, leaf_slot = trace_pivots(merge_picks, row_devices)
    owner_mask = leaf_group == own_row
    local_rows = jnp.take(leaf_picks[0], leaf_slot)
    middle = trailing
    middle = middle - contract_first(
        lax.all_gather(prev_lower_t, "cols", axis=0, tiled=True), prev_upper
    )
    panel_full = lax.all_gather(panel_t, "cols", axis=0, tiled=True)
    middle, panel_full = (middle, panel_full)
    candidates = jnp.take(panel_t, leaf_picks[0], axis=1)
    levels = row_devices.bit_length() - 1
    for section in range(levels):
        partner = from_partner(candidates, "rows", section)
        upper_half = own_row >> section & 1
        stacked = jnp.where(
            upper_half == 0,
            jnp.concatenate([candidates, partner], 1),
            jnp.concatenate([partner, candidates], 1),
        )
        merge_index = row_devices - (row_devices >> section) + (own_row >> section + 1)
        selection = lax.dynamic_index_in_dim(merge_picks, merge_index, 0, keepdims=False)
        candidates = jnp.take(stacked, selection, axis=1)
    block_t = lax.all_gather(candidates, "cols", axis=0, tiled=True)
    lower_left, upper_left = factor(block_t.T)
    inverse = upper_inverse(upper_left)
    chosen_rows = jnp.take(middle, local_rows, axis=0)
    pivot_trailing = lax.psum(jnp.where(owner_mask[:, None], chosen_rows, 0.0), "rows")
    upper_right = product(unit_lower_inverse(lower_left), pivot_trailing)
    lower_full = jnp.dot(inverse.T, panel_full, precision=full_precision)
    lower_tile = lax.dynamic_slice_in_dim(lower_full, own_column * slab_rows, slab_rows, 0)
    updated = middle - contract_first(lower_full, upper_right)
    gram_rows = contract_second(lower_tile, lower_full)
    gram = lax.psum(gram_rows, "rows") / (rows_here * row_devices)
    return (lower_tile, upper_left, upper_right, updated, gram)


def solution(mesh):
    return jax.shard_map(
        body,
        mesh=mesh,
        in_specs=(
            P("cols", "rows"),
            P("rows", "cols"),
            P("cols", "rows"),
            P(None, "cols"),
            P("rows", None),
            P(),
        ),
        out_specs=(P("cols", "rows"), P(), P(None, "cols"), P("rows", "cols"), P("cols", None)),
        check_vma=False,
    )
```

profile of v0, /device:TPU:1, one launch (start us, length us, event | category | flops | bytes accessed | tf_op | source)
XLA Modules:
  0.0 666.7 jit_solution(18420080270595223450)
XLA Ops:
  8.0 1.2 copy.357
  9.2 2.5 gather_fusion.9
  11.8 2.3 gather_fusion.10
  14.1 2.3 gather_fusion.11
  16.5 2.3 gather_fusion.12
  18.9 2.3 gather_fusion.13
  22.2 8.8 %collective-permute-start = (f32[16,256]{0,1:T(8,128)S(1)}, f32[16,256]{0,1:T(8,128)S(1)}, u32[]{:S(2)}, u32[]{:S(2)}) collective-permute-start(f32[16,256]{0,1:T(8,128)S(1)} %select_bitcast_fusion.4), channel_id=1, source_target_pairs={{0,16},{16,0},{32,48},{48,32},{64,80},{80,64},{96,112},{112,96},{1... | collective-permute-start | bytes 49160 | tf_op jit(solution)/shard_map/ppermute | solution.py:10
  31.8 1.9 gather_fusion.14
  34.8 1.9 collective-permute-start.1
  36.7 5.1 collective-permute-done.1
  42.6 1.9 collective-permute-start.2
  44.6 5.7 collective-permute-done.2
  50.3 0.7 gather_fusion.18
  51.1 1.9 collective-permute-start.3
  53.1 3.8 collective-permute-done.3
  57.7 1.9 collective-permute-start.4
  60.2 4.8 collective-permute-done.4
  65.8 27.0 %all_gather.9 = f32[256,256]{1,0:T(8,128)S(1)} all-gather(f32[16,256]{1,0:T(8,128)S(1)} %select_bitcast_fusion.5), channel_id=1, replica_groups=mesh['rows'=32,'cols'=16] {'cols'}, dimensions={0}, use_global_device_ids=true | all-gather | bytes 278528 | tf_op jit(solution)/shard_map/all_gather | solution.py:141
  187.0 0.8 gather_fusion.2
  288.1 1.3 gather_fusion.4
  390.3 0.8 gather_fusion.6
  492.6 2.5 gather_fusion.8
  496.3 0.8 copy.464
  507.7 6.1 convolution_subtract_fusion.1
  513.8 1.0 gather_fusion.15
  514.8 0.8 select_select_fusion
  515.7 3.5 fusion.224
  519.2 1.7 fusion.232
  521.0 127.3 %psum.15 = f32[16,256]{1,0:T(8,128)S(1)} all-reduce(f32[16,256]{1,0:T(8,128)S(1)} %fusion.232), channel_id=1, replica_groups=mesh['rows'=32,'cols'=16] {'rows'}, use_global_device_ids=true, to_apply=%region_745.747 | all-reduce | flops 4096 | bytes 32768 | tf_op jit(solution)/shard_map/psum | solution.py:151
  648.9 3.1 all-reduce.16.cloned.1.call-done
  652.0 1.3 fusion.231
  653.4 6.6 convolution_subtract_fusion
  (1105 shorter events, 412.3 us)
Async XLA Ops:
  7.2 500.5 %copy-start = (f32[256,256]{1,0:T(8,128)S(1)}, f32[256,256]{1,0:T(8,128)}, u32[]{:S(2)}) copy-start(f32[256,256]{1,0:T(8,128)} %param.11) | copy-start | bytes 786436
  7.2 4.6 copy-start.2
  7.2 500.5 %all-gather.5.cloned.1.call-start = ((), (), s32[]{:S(2)}) async-start(), calls=%async_computation.1 | async-start | bytes 2228224 | tf_op jit(solution)/shard_map/all_gather | solution.py:124
  7.9 507.7 %all-gather.3.cloned.1.call-start = ((), (), s32[]{:S(2)}) async-start(), calls=%async_computation | async-start | bytes 2228224 | tf_op jit(solution)/shard_map/all_gather | solution.py:126
  14.1 7.1 %copy-start.1 = (s32[1,256]{1,0:T(1,128)S(1)}, s32[1,256]{1,0:T(1,128)}, u32[]{:S(2)}) copy-start(s32[1,256]{1,0:T(1,128)} %param.12) | copy-start | bytes 3076
  22.2 11.7 %collective-permute-start = (f32[16,256]{0,1:T(8,128)S(1)}, f32[16,256]{0,1:T(8,128)S(1)}, u32[]{:S(2)}, u32[]{:S(2)}) collective-permute-start(f32[16,256]{0,1:T(8,128)S(1)} %select_bitcast_fusion.4), channel_id=1, source_target_pairs={{0,16},{16,0},{32,48},{48,32},{64,80},{80,64},{96,112},{112,96},{1... | collective-permute-start | bytes 49160 | tf_op jit(solution)/shard_map/ppermute | solution.py:10
  31.0 621.0 %all-reduce.16.cloned.1.call-start = ((), (), s32[]{:S(2)}) async-start(), calls=%async_computation.2 | async-start | bytes 524288 | tf_op jit(solution)/shard_map/psum | solution.py:145
  34.8 7.0 %collective-permute-start.1 = (f32[16,256]{0,1:T(8,128)S(1)}, f32[16,256]{0,1:T(8,128)S(1)}, u32[]{:S(2)}, u32[]{:S(2)}) collective-permute-start(f32[16,256]{0,1:T(8,128)S(1)} %select_bitcast_fusion.3), channel_id=1, source_target_pairs={{0,32},{16,48},{32,0},{48,16},{64,96},{80,112},{96,64},{112,80},{1... | collective-permute-start | bytes 49160 | tf_op jit(solution)/shard_map/ppermute | solution.py:10
  42.6 7.6 %collective-permute-start.2 = (f32[16,256]{0,1:T(8,128)S(1)}, f32[16,256]{0,1:T(8,128)S(1)}, u32[]{:S(2)}, u32[]{:S(2)}) collective-permute-start(f32[16,256]{0,1:T(8,128)S(1)} %select_bitcast_fusion.2), channel_id=1, source_target_pairs={{0,64},{16,80},{32,96},{48,112},{64,0},{80,16},{96,32},{112,48},{1... | collective-permute-start | bytes 49160 | tf_op jit(solution)/shard_map/ppermute | solution.py:10
  51.1 5.7 collective-permute-start.3
  57.7 7.3 %collective-permute-start.4 = (f32[16,256]{0,1:T(8,128)S(1)}, f32[16,256]{0,1:T(8,128)S(1)}, u32[]{:S(2)}, u32[]{:S(2)}) collective-permute-start(f32[16,256]{0,1:T(8,128)S(1)} %select_bitcast_fusion), channel_id=1, source_target_pairs={{0,256},{16,272},{32,288},{48,304},{64,320},{80,336},{96,352},{112... | collective-permute-start | bytes 49160 | tf_op jit(solution)/shard_map/ppermute | solution.py:10
  513.8 1.9 copy-start.3
  519.2 140.8 %copy-start.5 = (f32[16,2048]{1,0:T(8,128)}, f32[16,2048]{1,0:T(8,128)S(1)}, u32[]{:S(2)}) copy-start(f32[16,2048]{1,0:T(8,128)S(1)} %constant_dynamic-slice_fusion) | copy-start | bytes 393220
  653.3 6.6 copy-start.4
Sparse Core Ops, SparseCore 0:
  10.1 69.6 all-gather.4
  81.9 70.6 all-gather.2
  515.7 136.2 all-reduce.15
where the time goes:
time: 674 us; the launch traced here: 667 us
  other arithmetic  362 us (54%)
  blocking collectives  154 us (23%)
  matrix products  59.6 us (9%)
  local copies, waits for them, and re-layouts  33.2 us (5%)
  waiting for transfers between devices  23.2 us (3%)
  between operations  18.1 us (3%)
  starting transfers between devices  16.6 us (2%)
    select_n x248, other arithmetic, small_factor(): jnp.where(line_index > column_index, pivot_column / pivot_value, 0.0)  161 us
    reduce_sum x248, other arithmetic, small_factor(): jnp.sum(jnp.where(line_index == column_index, pivot_line, 0.0))  151 us
    psum x1, blocking collectives, body(): gram = lax.psum(gram_rows, 'rows') / (rows_here * row_devices)  127 us
    reduce_sum x244, other arithmetic, small_factor(): jnp.sum(jnp.where(col_index == column_index, reduced, 0.0), 1)  45.1 us
    dot_general x178, matrix products, product(): return jnp.dot(left_side, right_side, precision=full_precision)  41.6 us
    all_gather x1, blocking collectives, body(): block_t = lax.all_gather(candidates, 'cols', axis=0, tiled=True)  27 us
    ppermute x5, waiting for transfers between devices, from_partner(): lax.ppermute(shard, axis, [(i, i ^ 1 << apart) for i in range(lax.axis_si...  19.3 us
    ppermute x5, starting transfers between devices, from_partner(): lax.ppermute(shard, axis, [(i, i ^ 1 << apart) for i in range(lax.axis_si...  16.5 us
  transfers between devices with their start and end apart: 8, of which 5 were waited for; matrix products, arithmetic and copies ran while one was open for 67% of the time, Pallas kernels for 0%

commit v1 on v0

--- a/solution.py
+++ b/solution.py
@@ -1,6 +1,8 @@
 import jax
 import jax.numpy as jnp
 from jax import lax
+from jax.experimental import pallas as pl
+from jax.experimental.pallas import tpu as pltpu
 from jax.sharding import PartitionSpec as P
 
 full_precision = lax.Precision.HIGHEST
@@ -48,54 +50,45 @@
     return unit_inverse / diagonal[None, :]
 
 
-def small_factor(matrix):
-    order = matrix.shape[0]
-    row_index = lax.broadcasted_iota(jnp.int32, (order, order), 0)
-    col_index = lax.broadcasted_iota(jnp.int32, (order, order), 1)
-    line_index = jnp.arange(order, dtype=jnp.int32)
-    reduced = matrix
-    for column_index in range(order - 1):
-        pivot_line = jnp.sum(jnp.where(row_index == column_index, reduced, 0.0), 0)
-        pivot_column = jnp.sum(jnp.where(col_index == column_index, reduced, 0.0), 1)
-        pivot_value = jnp.sum(jnp.where(line_index == column_index, pivot_line, 0.0))
-        factors = jnp.where(line_index > column_index, pivot_column / pivot_value, 0.0)
-        below = row_index > column_index
-        reduced = jnp.where(
-            below & (col_index > column_index),
-            reduced - factors[:, None] * pivot_line[None, :],
-            reduced,
-        )
-        reduced = jnp.where(below & (col_index == column_index), factors[:, None], reduced)
-    return (jnp.tril(reduced, -1) + jnp.eye(order, dtype=matrix.dtype), jnp.triu(reduced))
+def elimination_kernel(matrix_ref, reduced_ref):
+    order = matrix_ref.shape[0]
+    reduced_ref[...] = matrix_ref[...]
+    phase = 32
+    for first_row in range(0, order - 1, phase):
+        first_col = (first_row // 128) * 128
+        height = order - first_row
+        width = order - first_col
+        row_index = lax.broadcasted_iota(jnp.int32, (height, width), 0) + first_row
+        col_index = lax.broadcasted_iota(jnp.int32, (height, width), 1) + first_col
+
+        def step(column_index, carry):
+            window = reduced_ref[first_row:, first_col:]
+            pivot_line = reduced_ref[pl.ds(column_index, 1), :][:, first_col:]
+            on_column = col_index == column_index
+            pivot_column = jnp.sum(jnp.where(on_column, window, 0.0), axis=1, keepdims=True)
+            pivot_value = jnp.sum(
+                jnp.where(on_column[0:1], pivot_line, 0.0), axis=1, keepdims=True
+            )
+            factors = pivot_column / pivot_value
+            below = row_index > column_index
+            window = jnp.where(
+                below & (col_index > column_index), window - factors * pivot_line, window
+            )
+            window = jnp.where(below & on_column, factors, window)
+            reduced_ref[first_row:, first_col:] = window
+            return carry
+
+        lax.fori_loop(first_row, min(first_row + phase, order - 1), step, 0)
 
 
 def factor(matrix):
     order = matrix.shape[0]
-    if order <= 32:
-        return small_factor(matrix)
-    middle_index = order // 2
-    lower_head, upper_head = factor(matrix[:middle_index, :middle_index])
-    upper_side = product(unit_lower_inverse(lower_head), matrix[:middle_index, middle_index:])
-    lower_side = product(matrix[middle_index:, :middle_index], upper_inverse(upper_head))
-    schur_block = matrix[middle_index:, middle_index:] - product(lower_side, upper_side)
-    lower_tail, upper_tail = factor(schur_block)
-    zero_upper = jnp.zeros((middle_index, order - middle_index), matrix.dtype)
-    zero_lower = jnp.zeros((order - middle_index, middle_index), matrix.dtype)
-    lower_full = jnp.concatenate(
-        [
-            jnp.concatenate([lower_head, zero_upper], 1),
-            jnp.concatenate([lower_side, lower_tail], 1),
-        ],
-        0,
-    )
-    upper_full = jnp.concatenate(
-        [
-            jnp.concatenate([upper_head, upper_side], 1),
-            jnp.concatenate([zero_lower, upper_tail], 1),
-        ],
-        0,
-    )
-    return (lower_full, upper_full)
+    reduced = pl.pallas_call(
+        elimination_kernel,
+        out_shape=jax.ShapeDtypeStruct(matrix.shape, matrix.dtype),
+    )(matrix)
+    lower = jnp.tril(reduced, -1) + jnp.eye(order, dtype=matrix.dtype)
+    return (lower, jnp.triu(reduced))
 
 
 def contract_first(left_side, right_side):

time: 674 us -> 309 us (0.46)
  other arithmetic: 362 us -> 2.4 us
  Pallas kernels: 0 us -> 32.9 us
  matrix products: 59.6 us -> 30.1 us
  waiting for transfers between devices: 23.2 us -> 32.7 us
  local copies, waits for them, and re-layouts: 33.2 us -> 26.1 us
    reduce_sum x493 -> x0, other arithmetic: 196 us -> none  [the longest x248 151 us: small_factor(): jnp.sum(jnp.where(line_index == column_index, pivot_line, 0.0))]
    select_n x255 -> x1, other arithmetic: 161 us -> 0.03 us  [factor(): return (lower, jnp.triu(reduced))]
    pallas_call x0 -> x1, Pallas kernels: none -> 32.9 us  [factor(): pl.pallas_call(elimination_kernel, out_shape=jax.ShapeDtypeStruct(matrix....]
    dot_general x178 -> x29, matrix products: 41.6 us -> 12.5 us  [product(): return jnp.dot(left_side, right_side, precision=full_precision)]
  transfers between devices with their start and end apart: 8 -> 8, of which waited for: 5 -> 6; matrix products, arithmetic and copies ran while one was open for 67% -> 16% of each run, Pallas kernels for 0% -> 11%
where the time goes in v1:
time: 309 us; the launch traced here: 308 us
  blocking collectives  153 us (50%)
  Pallas kernels  32.9 us (11%)
  waiting for transfers between devices  32.7 us (11%)
  matrix products  30.1 us (10%)
  local copies, waits for them, and re-layouts  26.1 us (8%)
  starting transfers between devices  16.6 us (5%)
  between operations  14.6 us (5%)
    psum x1, blocking collectives, body(): gram = lax.psum(gram_rows, 'rows') / (rows_here * row_devices)  128 us
    pallas_call x1, Pallas kernels, factor(): pl.pallas_call(elimination_kernel, out_shape=jax.ShapeDtypeStruct(matrix....  32.9 us
    all_gather x1, blocking collectives, body(): block_t = lax.all_gather(candidates, 'cols', axis=0, tiled=True)  25 us
    ppermute x5, waiting for transfers between devices, from_partner(): lax.ppermute(shard, axis, [(i, i ^ 1 << apart) for i in range(lax.axis_si...  20 us
    ppermute x5, starting transfers between devices, from_partner(): lax.ppermute(shard, axis, [(i, i ^ 1 << apart) for i in range(lax.axis_si...  16.5 us
    dot_general x29, matrix products, product(): return jnp.dot(left_side, right_side, precision=full_precision)  12.5 us
    dot_general x2, matrix products, contract_first(): lax.dot_general(left_side, right_side, (((0,), (0,)), ((), ())), precisio...  12.4 us
    gather x5, local copies, waits for them, and re-layouts, trace_pivots(): position = merge_picks[offset_rows + leaf_group, leaf_slot]  11.9 us
  transfers between devices with their start and end apart: 8, of which 6 were waited for; matrix products, arithmetic and copies ran while one was open for 16% of the time, Pallas kernels for 11%

profile of v1, /device:TPU:1, one launch (start us, length us, event | category | flops | bytes accessed | tf_op | source)
XLA Modules:
  0.0 308.4 jit_solution(2810393766573232160)
XLA Ops:
  8.0 1.2 copy.61
  9.2 2.5 gather_fusion.2
  11.8 2.3 gather_fusion.3
  14.1 2.3 gather_fusion.4
  16.5 2.3 gather_fusion.5
  18.9 2.3 gather_fusion.6
  21.3 0.7 gather_fusion
  22.1 8.8 %collective-permute-start = (f32[16,256]{0,1:T(8,128)S(1)}, f32[16,256]{0,1:T(8,128)S(1)}, u32[]{:S(2)}, u32[]{:S(2)}) collective-permute-start(f32[16,256]{0,1:T(8,128)S(1)} %select_bitcast_fusion.5), channel_id=1, source_target_pairs={{0,16},{16,0},{32,48},{48,32},{64,80},{80,64},{96,112},{112,96},{1... | collective-permute-start | bytes 49160 | tf_op jit(solution)/shard_map/ppermute | solution.py:12
  31.3 1.9 gather_fusion.7
  34.2 1.9 collective-permute-start.1
  36.1 5.2 %collective-permute-done.1 = f32[16,256]{0,1:T(8,128)S(1)} collective-permute-done((f32[16,256]{0,1:T(8,128)S(1)}, f32[16,256]{0,1:T(8,128)S(1)}, u32[]{:S(2)}, u32[]{:S(2)}) %collective-permute-start.1) | collective-permute-done | bytes 16416 | tf_op jit(solution)/shard_map/ppermute | solution.py:12
  42.2 1.9 collective-permute-start.2
  44.1 5.8 %collective-permute-done.2 = f32[16,256]{0,1:T(8,128)S(1)} collective-permute-done((f32[16,256]{0,1:T(8,128)S(1)}, f32[16,256]{0,1:T(8,128)S(1)}, u32[]{:S(2)}, u32[]{:S(2)}) %collective-permute-start.2) | collective-permute-done | bytes 16416 | tf_op jit(solution)/shard_map/ppermute | solution.py:12
  50.8 1.9 collective-permute-start.3
  52.7 3.9 %collective-permute-done.3 = f32[16,256]{0,1:T(8,128)S(1)} collective-permute-done((f32[16,256]{0,1:T(8,128)S(1)}, f32[16,256]{0,1:T(8,128)S(1)}, u32[]{:S(2)}, u32[]{:S(2)}) %collective-permute-start.3) | collective-permute-done | bytes 16416 | tf_op jit(solution)/shard_map/ppermute | solution.py:12
  57.5 1.9 collective-permute-start.4
  59.6 5.1 %collective-permute-done.4 = f32[16,256]{0,1:T(8,128)S(1)} collective-permute-done((f32[16,256]{0,1:T(8,128)S(1)}, f32[16,256]{0,1:T(8,128)S(1)}, u32[]{:S(2)}, u32[]{:S(2)}) %collective-permute-start.4) | collective-permute-done | bytes 16416 | tf_op jit(solution)/shard_map/ppermute | solution.py:12
  65.7 25.0 %all_gather.9 = f32[256,256]{1,0:T(8,128)S(1)} all-gather(f32[16,256]{1,0:T(8,128)S(1)} %copy.62), channel_id=1, replica_groups=mesh['rows'=32,'cols'=16] {'cols'}, dimensions={0}, use_global_device_ids=true | all-gather | bytes 278528 | tf_op jit(solution)/shard_map/all_gather | solution.py:134
  90.6 0.8 copy.63
  91.5 32.9 %shard_map.101 = f32[256,256]{1,0:T(8,128)} custom-call(f32[256,256]{1,0:T(8,128)} %bitcast.96), custom_call_target="tpu_custom_call" | custom-call | tf_op jit(solution)/shard_map/pallas_call | solution.py:86
  124.4 1.1 copy.64
  125.5 2.5 gather_fusion.1
  129.3 0.8 copy.68
  140.4 5.9 %convolution_subtract_fusion.1 = f32[2048,256]{1,0:T(8,128)S(1)} fusion(f32[2048,256]{1,0:T(8,128)} %param.9, f32[256,2048]{1,0:T(8,128)} %all-gather.5.cloned.1.call-done, f32[256,256]{1,0:T(8,128)S(1)} %copy-done), kind=kOutput, calls=%fused_computation.15 | convolution fusion | flops 1611137024 | bytes 6553600 | tf_op jit(solution)/shard_map/dot_general | solution.py:95
  146.3 1.0 gather_fusion.8
  148.2 4.0 %all-gather.3.cloned.1.call-done = f32[256,2048]{1,0:T(8,128)} async-done(((f32[16,2048]{1,0:T(8,128)}), f32[256,2048]{1,0:T(8,128)}) %all-gather.3.cloned.1.call-update) | async-done | bytes 2097168 | tf_op jit(solution)/shard_map/all_gather | solution.py:119
  152.2 3.5 %fusion.52 = f32[256,2048]{1,0:T(8,128)S(1)} fusion(f32[256,256]{1,0:T(8,128)S(1)} %convolution_divide_fusion, f32[256,2048]{1,0:T(8,128)} %all-gather.3.cloned.1.call-done), kind=kOutput, calls=%fused_computation.160 | convolution fusion | flops 1610612736 | bytes 4456448 | tf_op jit(solution)/shard_map/dot_general | solution.py:140
  155.7 1.7 fusion.60
  157.4 127.9 %psum.15 = f32[16,256]{1,0:T(8,128)S(1)} all-reduce(f32[16,256]{1,0:T(8,128)S(1)} %fusion.60), channel_id=1, replica_groups=mesh['rows'=32,'cols'=16] {'rows'}, use_global_device_ids=true, to_apply=%region_1.3 | all-reduce | flops 4096 | bytes 32768 | tf_op jit(solution)/shard_map/psum | solution.py:144
  285.9 8.0 %all-reduce.2.cloned.1.call-done = f32[256,256]{0,1:T(8,128)} async-done(((f32[256,256]{0,1:T(8,128)}), f32[256,256]{0,1:T(8,128)}) %all-reduce.2.cloned.1.call-update) | async-done | bytes 262160 | tf_op jit(solution)/shard_map/psum | solution.py:138
  294.0 1.4 fusion.59
  295.4 6.5 %convolution_subtract_fusion = f32[2048,256]{1,0:T(8,128)} fusion(f32[2048,256]{1,0:T(8,128)} %copy-done.3, f32[256,2048]{1,0:T(8,128)S(1)} %fusion.52, f32[256,256]{1,0:T(8,128)S(1)} %fusion.59), kind=kOutput, calls=%fused_computation.14 | convolution fusion | flops 1611137024 | bytes 6553600 | tf_op jit(solution)/shard_map/dot_general | solution.py:95
  (103 shorter events, 18.5 us)
Async XLA Ops:
  7.2 133.2 %copy-start = (f32[256,256]{1,0:T(8,128)S(1)}, f32[256,256]{1,0:T(8,128)}, u32[]{:S(2)}) copy-start(f32[256,256]{1,0:T(8,128)} %param.11) | copy-start | bytes 786436
  7.2 4.6 %copy-start.2 = (s32[31,256]{1,0:T(8,128)S(1)}, s32[31,256]{1,0:T(8,128)}, u32[]{:S(2)}) copy-start(s32[31,256]{1,0:T(8,128)} %param.13) | copy-start | bytes 95236
  7.2 133.2 %all-gather.5.cloned.1.call-start = ((), (), s32[]{:S(2)}) async-start(), calls=%async_computation.1 | async-start | bytes 2228224 | tf_op jit(solution)/shard_map/all_gather | solution.py:117
  7.9 144.2 %all-gather.3.cloned.1.call-start = ((), (), s32[]{:S(2)}) async-start(), calls=%async_computation | async-start | bytes 2228224 | tf_op jit(solution)/shard_map/all_gather | solution.py:119
  11.8 9.5 %copy-start.1 = (s32[1,256]{1,0:T(1,128)S(1)}, s32[1,256]{1,0:T(1,128)}, u32[]{:S(2)}) copy-start(s32[1,256]{1,0:T(1,128)} %param.12) | copy-start | bytes 3076
  22.1 11.1 %collective-permute-start = (f32[16,256]{0,1:T(8,128)S(1)}, f32[16,256]{0,1:T(8,128)S(1)}, u32[]{:S(2)}, u32[]{:S(2)}) collective-permute-start(f32[16,256]{0,1:T(8,128)S(1)} %select_bitcast_fusion.5), channel_id=1, source_target_pairs={{0,16},{16,0},{32,48},{48,32},{64,80},{80,64},{96,112},{112,96},{1... | collective-permute-start | bytes 49160 | tf_op jit(solution)/shard_map/ppermute | solution.py:12
  31.0 263.0 %all-reduce.2.cloned.1.call-start = ((), (), s32[]{:S(2)}) async-start(), calls=%async_computation.2 | async-start | bytes 524288 | tf_op jit(solution)/shard_map/psum | solution.py:138
  34.2 7.1 %collective-permute-start.1 = (f32[16,256]{0,1:T(8,128)S(1)}, f32[16,256]{0,1:T(8,128)S(1)}, u32[]{:S(2)}, u32[]{:S(2)}) collective-permute-start(f32[16,256]{0,1:T(8,128)S(1)} %select_bitcast_fusion.4), channel_id=1, source_target_pairs={{0,32},{16,48},{32,0},{48,16},{64,96},{80,112},{96,64},{112,80},{1... | collective-permute-start | bytes 49160 | tf_op jit(solution)/shard_map/ppermute | solution.py:12
  42.2 7.7 %collective-permute-start.2 = (f32[16,256]{0,1:T(8,128)S(1)}, f32[16,256]{0,1:T(8,128)S(1)}, u32[]{:S(2)}, u32[]{:S(2)}) collective-permute-start(f32[16,256]{0,1:T(8,128)S(1)} %select_bitcast_fusion.3), channel_id=1, source_target_pairs={{0,64},{16,80},{32,96},{48,112},{64,0},{80,16},{96,32},{112,48},{1... | collective-permute-start | bytes 49160 | tf_op jit(solution)/shard_map/ppermute | solution.py:12
  50.8 5.9 %collective-permute-start.3 = (f32[16,256]{0,1:T(8,128)S(1)}, f32[16,256]{0,1:T(8,128)S(1)}, u32[]{:S(2)}, u32[]{:S(2)}) collective-permute-start(f32[16,256]{0,1:T(8,128)S(1)} %select_bitcast_fusion.2), channel_id=1, source_target_pairs={{0,128},{16,144},{32,160},{48,176},{64,192},{80,208},{96,224},{112... | collective-permute-start | bytes 49160 | tf_op jit(solution)/shard_map/ppermute | solution.py:12
  57.5 7.2 %collective-permute-start.4 = (f32[16,256]{0,1:T(8,128)S(1)}, f32[16,256]{0,1:T(8,128)S(1)}, u32[]{:S(2)}, u32[]{:S(2)}) collective-permute-start(f32[16,256]{0,1:T(8,128)S(1)} %select_bitcast_fusion.1), channel_id=1, source_target_pairs={{0,256},{16,272},{32,288},{48,304},{64,320},{80,336},{96,352},{112... | collective-permute-start | bytes 49160 | tf_op jit(solution)/shard_map/ppermute | solution.py:12
  128.1 2.1 copy-start.4
  146.3 1.9 copy-start.3
  155.7 146.2 %copy-start.6 = (f32[16,2048]{1,0:T(8,128)}, f32[16,2048]{1,0:T(8,128)S(1)}, u32[]{:S(2)}) copy-start(f32[16,2048]{1,0:T(8,128)S(1)} %constant_dynamic-slice_fusion) | copy-start | bytes 393220
  295.4 6.5 %copy-start.5 = (f32[256,256]{1,0:T(8,128)}, f32[256,256]{1,0:T(8,128)S(1)}, u32[]{:S(2)}) copy-start(f32[256,256]{1,0:T(8,128)S(1)} %fusion.59) | copy-start | bytes 786436
Sparse Core Ops, SparseCore 0:
  10.1 69.6 all-gather.4
  81.9 70.1 all-gather.2
  156.0 137.9 all-reduce.1

commit v2 on v1

--- a/solution.py
+++ b/solution.py
@@ -103,45 +103,46 @@
     )
 
 
+def butterfly_sum(value, axis):
+    levels = lax.axis_size(axis).bit_length() - 1
+    for section in range(levels):
+        value = value + from_partner(value, axis, section)
+    return value
+
+
 def body(panel_t, trailing, prev_lower_t, prev_upper, leaf_picks, merge_picks):
     slab_rows = panel_t.shape[0]
     rows_here = panel_t.shape[1]
+    order = merge_picks.shape[1]
     row_devices = lax.axis_size("rows")
     own_row = lax.axis_index("rows")
     own_column = lax.axis_index("cols")
     leaf_group, leaf_slot = trace_pivots(merge_picks, row_devices)
     owner_mask = leaf_group == own_row
     local_rows = jnp.take(leaf_picks[0], leaf_slot)
-    middle = trailing
-    middle = middle - contract_first(
+    own_trailing = jnp.take(trailing, local_rows, axis=0)
+    own_columns = jnp.take(jnp.concatenate([panel_t, prev_lower_t], 0), local_rows, axis=1)
+    own_pivots = jnp.concatenate([own_trailing, own_columns.T], 1)
+    pivot_data = butterfly_sum(jnp.where(owner_mask[:, None], own_pivots, 0.0), "rows")
+    pivot_trailing = pivot_data[:, : own_trailing.shape[1]]
+    pivot_columns = lax.all_gather(
+        pivot_data[:, own_trailing.shape[1] :].T, "cols", axis=0, tiled=False
+    )
+    block_t = pivot_columns[:, :slab_rows].reshape(order, order)
+    prev_pivots = pivot_columns[:, slab_rows:].reshape(order, order)
+    middle_pivots = pivot_trailing - contract_first(prev_pivots, prev_upper)
+    middle = trailing - contract_first(
         lax.all_gather(prev_lower_t, "cols", axis=0, tiled=True), prev_upper
     )
     panel_full = lax.all_gather(panel_t, "cols", axis=0, tiled=True)
-    middle, panel_full = (middle, panel_full)
-    candidates = jnp.take(panel_t, leaf_picks[0], axis=1)
-    levels = row_devices.bit_length() - 1
-    for section in range(levels):
-        partner = from_partner(candidates, "rows", section)
-        upper_half = own_row >> section & 1
-        stacked = jnp.where(
-            upper_half == 0,
-            jnp.concatenate([candidates, partner], 1),
-            jnp.concatenate([partner, candidates], 1),
-        )
-        merge_index = row_devices - (row_devices >> section) + (own_row >> section + 1)
-        selection = lax.dynamic_index_in_dim(merge_picks, merge_index, 0, keepdims=False)
-        candidates = jnp.take(stacked, selection, axis=1)
-    block_t = lax.all_gather(candidates, "cols", axis=0, tiled=True)
     lower_left, upper_left = factor(block_t.T)
     inverse = upper_inverse(upper_left)
-    chosen_rows = jnp.take(middle, local_rows, axis=0)
-    pivot_trailing = lax.psum(jnp.where(owner_mask[:, None], chosen_rows, 0.0), "rows")
-    upper_right = product(unit_lower_inverse(lower_left), pivot_trailing)
+    upper_right = product(unit_lower_inverse(lower_left), middle_pivots)
     lower_full = jnp.dot(inverse.T, panel_full, precision=full_precision)
     lower_tile = lax.dynamic_slice_in_dim(lower_full, own_column * slab_rows, slab_rows, 0)
     updated = middle - contract_first(lower_full, upper_right)
     gram_rows = contract_second(lower_tile, lower_full)
-    gram = lax.psum(gram_rows, "rows") / (rows_here * row_devices)
+    gram = butterfly_sum(gram_rows, "rows") / (rows_here * row_devices)
     return (lower_tile, upper_left, upper_right, updated, gram)
 
 

time: 309 us -> 219 us (0.71)
  blocking collectives: 153 us -> 26.8 us
  starting transfers between devices: 16.6 us -> 45.9 us
  waiting for transfers between devices: 32.7 us -> 41.8 us
  local copies, waits for them, and re-layouts: 26.1 us -> 22.8 us
    psum x1 -> x0, blocking collectives: 128 us -> none  [body(): gram = lax.psum(gram_rows, 'rows') / (rows_here * row_devices)]
    ppermute x5 -> x10, starting transfers between devices: 16.5 us -> 45.8 us  [from_partner(): lax.ppermute(shard, axis, [(i, i ^ 1 << apart) for i in range(lax.axis_si...]
    ppermute x5 -> x10, waiting for transfers between devices: 20 us -> 41.1 us  [from_partner(): lax.ppermute(shard, axis, [(i, i ^ 1 << apart) for i in range(lax.axis_si...]
    psum x1 -> x0, waiting for transfers between devices: 8.05 us -> none  [body(): lax.psum(jnp.where(owner_mask[:, None], chosen_rows, 0.0), 'rows')]
    all_gather x1, waiting for transfers between devices: 3.96 us -> 0.01 us  [body(): panel_full = lax.all_gather(panel_t, 'cols', axis=0, tiled=True)]
    gather x8 -> x2, local copies, waits for them, and re-layouts: 5.48 us -> 2.31 us  [the longest x1 1.34 us: body(): jnp.take(jnp.concatenate([panel_t, prev_lower_t], 0), local_rows, axis=1)]
    dot_general x2 -> x3, matrix products: 12.4 us -> 11.3 us  [contract_first(): lax.dot_general(left_side, right_side, (((0,), (0,)), ((), ())), precisio...]
  transfers between devices with their start and end apart: 8 -> 12, of which waited for: 6 -> 7; matrix products, arithmetic and copies ran while one was open for 16% -> 25% of each run, Pallas kernels for 11% -> 15%
where the time goes in v2:
time: 219 us; the launch traced here: 216 us
  starting transfers between devices  45.9 us (21%)
  waiting for transfers between devices  41.8 us (19%)
  Pallas kernels  33 us (15%)
  matrix products  29.1 us (13%)
  blocking collectives  26.8 us (12%)
  local copies, waits for them, and re-layouts  22.8 us (10%)
  between operations  14.8 us (7%)
  other arithmetic  2.31 us (1%)
    ppermute x10, starting transfers between devices, from_partner(): lax.ppermute(shard, axis, [(i, i ^ 1 << apart) for i in range(lax.axis_si...  45.8 us
    ppermute x10, waiting for transfers between devices, from_partner(): lax.ppermute(shard, axis, [(i, i ^ 1 << apart) for i in range(lax.axis_si...  41.1 us
    pallas_call x1, Pallas kernels, factor(): pl.pallas_call(elimination_kernel, out_shape=jax.ShapeDtypeStruct(matrix....  33 us
    all_gather x1, blocking collectives, body(): lax.all_gather(pivot_data[:, own_trailing.shape[1]:].T, 'cols', axis=0, t...  26.8 us
    dot_general x29, matrix products, product(): return jnp.dot(left_side, right_side, precision=full_precision)  12.3 us
    gather x5, local copies, waits for them, and re-layouts, trace_pivots(): position = merge_picks[offset_rows + leaf_group, leaf_slot]  11.9 us
    dot_general x3, matrix products, contract_first(): lax.dot_general(left_side, right_side, (((0,), (0,)), ((), ())), precisio...  11.3 us
  transfers between devices with their start and end apart: 12, of which 7 were waited for; matrix products, arithmetic and copies ran while one was open for 25% of the time, Pallas kernels for 15%

profile of v2, /device:TPU:1, one launch (start us, length us, event | category | flops | bytes accessed | tf_op | source)
XLA Modules:
  0.0 216.3 jit_solution(3277355454260794995)
XLA Ops:
  8.0 1.0 pad_maximum_fusion
  9.3 2.5 %gather_fusion = s32[256]{0:T(256)S(1)} fusion(s32[31,256]{1,0:T(8,128)S(1)} %copy-done.2, s32[256]{0:T(256)} %constant.187), kind=kCustom, calls=%fused_computation | custom fusion | bytes 4096 | tf_op jit(solution)/shard_map/gather | solution.py:22
  11.8 2.3 %gather_fusion.1 = s32[256]{0:T(256)S(1)} fusion(s32[31,256]{1,0:T(8,128)S(1)} %copy-done.2, s32[256]{0:T(256)S(1)} %bitcast.78), kind=kCustom, calls=%fused_computation.1 | custom fusion | bytes 4096 | tf_op jit(solution)/shard_map/gather | solution.py:22
  14.2 2.3 %gather_fusion.2 = s32[256]{0:T(256)S(1)} fusion(s32[31,256]{1,0:T(8,128)S(1)} %copy-done.2, s32[256]{0:T(256)S(1)} %bitcast.76), kind=kCustom, calls=%fused_computation.2 | custom fusion | bytes 4096 | tf_op jit(solution)/shard_map/gather | solution.py:22
  16.6 2.3 %gather_fusion.3 = s32[256]{0:T(256)S(1)} fusion(s32[31,256]{1,0:T(8,128)S(1)} %copy-done.2, s32[256]{0:T(256)S(1)} %bitcast.79), kind=kCustom, calls=%fused_computation.3 | custom fusion | bytes 4096 | tf_op jit(solution)/shard_map/gather | solution.py:22
  19.0 2.3 %gather_fusion.4 = s32[256]{0:T(256)S(1)} fusion(s32[31,256]{1,0:T(8,128)S(1)} %copy-done.2, s32[256]{0:T(256)S(1)} %bitcast.77), kind=kCustom, calls=%fused_computation.4 | custom fusion | bytes 4096 | tf_op jit(solution)/shard_map/gather | solution.py:22
  21.4 1.9 gather_fusion.5
  23.3 1.3 gather_fusion.7
  26.0 8.8 %collective-permute-start = (f32[256,288]{1,0:T(8,128)S(1)}, f32[256,288]{1,0:T(8,128)S(1)}, u32[]{:S(2)}, u32[]{:S(2)}) collective-permute-start(f32[256,288]{1,0:T(8,128)S(1)} %maximum_select_fusion), channel_id=1, source_target_pairs={{0,16},{16,0},{32,48},{48,32},{64,80},{80,64},{96,112},{112,96},{1... | collective-permute-start | bytes 884744 | tf_op jit(solution)/shard_map/ppermute | solution.py:12
  34.8 1.3 collective-permute-done
  36.2 1.9 collective-permute-start.1
  38.1 10.4 %collective-permute-done.1 = f32[256,288]{1,0:T(8,128)S(1)} collective-permute-done((f32[256,288]{1,0:T(8,128)S(1)}, f32[256,288]{1,0:T(8,128)S(1)}, u32[]{:S(2)}, u32[]{:S(2)}) %collective-permute-start.1) | collective-permute-done | bytes 294944 | tf_op jit(solution)/shard_map/ppermute | solution.py:12
  48.6 1.9 collective-permute-start.2
  50.5 11.0 %collective-permute-done.2 = f32[256,288]{1,0:T(8,128)S(1)} collective-permute-done((f32[256,288]{1,0:T(8,128)S(1)}, f32[256,288]{1,0:T(8,128)S(1)}, u32[]{:S(2)}, u32[]{:S(2)}) %collective-permute-start.2) | collective-permute-done | bytes 294944 | tf_op jit(solution)/shard_map/ppermute | solution.py:12
  61.5 1.9 collective-permute-start.3
  63.5 8.5 %collective-permute-done.3 = f32[256,288]{1,0:T(8,128)S(1)} collective-permute-done((f32[256,288]{1,0:T(8,128)S(1)}, f32[256,288]{1,0:T(8,128)S(1)}, u32[]{:S(2)}, u32[]{:S(2)}) %collective-permute-start.3) | collective-permute-done | bytes 294944 | tf_op jit(solution)/shard_map/ppermute | solution.py:12
  72.0 1.9 collective-permute-start.4
  74.2 8.9 %collective-permute-done.4 = f32[256,288]{1,0:T(8,128)S(1)} collective-permute-done((f32[256,288]{1,0:T(8,128)S(1)}, f32[256,288]{1,0:T(8,128)S(1)}, u32[]{:S(2)}, u32[]{:S(2)}) %collective-permute-start.4) | collective-permute-done | bytes 294944 | tf_op jit(solution)/shard_map/ppermute | solution.py:12
  83.2 26.8 %all-gather = f32[512,256]{1,0:T(8,128)S(1)} all-gather(f32[32,256]{1,0:T(8,128)S(1)} %copy.26), channel_id=2, replica_groups=mesh['rows'=32,'cols'=16] {'cols'}, dimensions={0}, use_global_device_ids=true | all-gather | bytes 557056 | tf_op jit(solution)/shard_map/all_gather | solution.py:128
  111.6 33.0 %shard_map.101 = f32[256,256]{1,0:T(8,128)} custom-call(f32[256,256]{1,0:T(8,128)} %bitcast.83), custom_call_target="tpu_custom_call" | custom-call | tf_op jit(solution)/shard_map/pallas_call | solution.py:86
  144.5 1.1 copy.28
  145.7 2.5 %gather_fusion.8 = f32[256]{0:T(256)S(1)} fusion(f32[256,256]{0,1:T(8,128)S(1)} %broadcast_select_fusion.1, s32[256]{0:T(256)S(1)} %bitcast.80), kind=kCustom, calls=%fused_computation.8 | custom fusion | bytes 4096 | tf_op jit(solution)/shard_map/jit(diagonal)/cond/branch_0_fun/gather | solution.py:47
  158.7 1.3 convolution_divide_fusion
  160.0 3.6 %fusion.54 = f32[256,2048]{1,0:T(8,128)S(1)} fusion(f32[256,256]{1,0:T(8,128)} %convolution_divide_fusion, f32[256,2048]{1,0:T(8,128)} %all-gather.4.cloned.1.call-done), kind=kOutput, calls=%fused_computation.127 | convolution fusion | flops 1610612736 | bytes 4456448 | tf_op jit(solution)/shard_map/dot_general | solution.py:141
  163.6 1.9 fusion.62
  165.5 13.6 %collective-permute-start.5 = (f32[16,256]{1,0:T(8,128)S(1)}, f32[16,256]{1,0:T(8,128)S(1)}, u32[]{:S(2)}, u32[]{:S(2)}) collective-permute-start(f32[16,256]{1,0:T(8,128)S(1)} %fusion.62), channel_id=1, source_target_pairs={{0,16},{16,0},{32,48},{48,32},{64,80},{80,64},{96,112},{112,96},{1... | collective-permute-start | bytes 49160 | tf_op jit(solution)/shard_map/ppermute | solution.py:12
  180.0 3.5 %collective-permute-start.6 = (f32[16,256]{1,0:T(8,128)S(1)}, f32[16,256]{1,0:T(8,128)S(1)}, u32[]{:S(2)}, u32[]{:S(2)}) collective-permute-start(f32[16,256]{1,0:T(8,128)S(1)} %add.402), channel_id=1, source_target_pairs={{0,32},{16,48},{32,0},{48,16},{64,96},{80,112},{96,64},{112,80},{1... | collective-permute-start | bytes 49160 | tf_op jit(solution)/shard_map/ppermute | solution.py:12
  184.6 4.9 %collective-permute-start.7 = (f32[16,256]{1,0:T(8,128)S(1)}, f32[16,256]{1,0:T(8,128)S(1)}, u32[]{:S(2)}, u32[]{:S(2)}) collective-permute-start(f32[16,256]{1,0:T(8,128)S(1)} %add.403), channel_id=1, source_target_pairs={{0,64},{16,80},{32,96},{48,112},{64,0},{80,16},{96,32},{112,48},{1... | collective-permute-start | bytes 49160 | tf_op jit(solution)/shard_map/ppermute | solution.py:12
  190.8 3.3 %collective-permute-start.8 = (f32[16,256]{1,0:T(8,128)S(1)}, f32[16,256]{1,0:T(8,128)S(1)}, u32[]{:S(2)}, u32[]{:S(2)}) collective-permute-start(f32[16,256]{1,0:T(8,128)S(1)} %add.404), channel_id=1, source_target_pairs={{0,128},{16,144},{32,160},{48,176},{64,192},{80,208},{96,224},{112... | collective-permute-start | bytes 49160 | tf_op jit(solution)/shard_map/ppermute | solution.py:12
  194.2 5.9 %convolution_subtract_fusion.1 = f32[2048,256]{1,0:T(8,128)S(1)} fusion(f32[2048,256]{1,0:T(8,128)} %param.7, f32[256,2048]{1,0:T(8,128)} %all-gather.6.cloned.1.call-done, f32[256,256]{1,0:T(8,128)S(1)} %copy-done), kind=kOutput, calls=%fused_computation.10 | convolution fusion | flops 1611137024 | bytes 6553600 | tf_op jit(solution)/shard_map/dot_general | solution.py:95
  200.1 4.0 %collective-permute-start.9 = (f32[16,256]{1,0:T(8,128)S(1)}, f32[16,256]{1,0:T(8,128)S(1)}, u32[]{:S(2)}, u32[]{:S(2)}) collective-permute-start(f32[16,256]{1,0:T(8,128)S(1)} %add.405), channel_id=1, source_target_pairs={{0,256},{16,272},{32,288},{48,304},{64,320},{80,336},{96,352},{112... | collective-permute-start | bytes 49160 | tf_op jit(solution)/shard_map/ppermute | solution.py:12
  204.1 4.8 %convolution_subtract_fusion = f32[2048,256]{1,0:T(8,128)} fusion(f32[2048,256]{1,0:T(8,128)S(1)} %convolution_subtract_fusion.1, f32[256,2048]{1,0:T(8,128)S(1)} %fusion.54, f32[256,256]{1,0:T(8,128)S(1)} %fusion.12), kind=kOutput, calls=%fused_computation.9 | convolution fusion | flops 1611137024 | bytes 6553600 | tf_op jit(solution)/shard_map/dot_general | solution.py:95
  (93 shorter events, 18.6 us)
Async XLA Ops:
  7.2 176.3 %copy-start = (f32[256,256]{1,0:T(8,128)S(1)}, f32[256,256]{1,0:T(8,128)}, u32[]{:S(2)}) copy-start(f32[256,256]{1,0:T(8,128)} %param.9) | copy-start | bytes 786436
  7.2 2.1 copy-start.2
  7.2 152.8 %all-gather.4.cloned.1.call-start = ((), (), s32[]{:S(2)}) async-start(), calls=%async_computation | async-start | bytes 2228224 | tf_op jit(solution)/shard_map/all_gather | solution.py:137
  7.9 186.2 %all-gather.6.cloned.1.call-start = ((), (), s32[]{:S(2)}) async-start(), calls=%async_computation.1 | async-start | bytes 2228224 | tf_op jit(solution)/shard_map/all_gather | solution.py:135
  11.8 9.5 %copy-start.1 = (s32[1,256]{1,0:T(1,128)S(1)}, s32[1,256]{1,0:T(1,128)}, u32[]{:S(2)}) copy-start(s32[1,256]{1,0:T(1,128)} %param.10) | copy-start | bytes 3076
  16.6 8.1 %copy-start.3 = (f32[2048,256]{1,0:T(8,128)S(1)}, f32[2048,256]{1,0:T(8,128)}, u32[]{:S(2)}) copy-start(f32[2048,256]{1,0:T(8,128)} %param.7) | copy-start | bytes 6291460
  24.7 1.0 copy-start.8
  26.0 10.1 %collective-permute-start = (f32[256,288]{1,0:T(8,128)S(1)}, f32[256,288]{1,0:T(8,128)S(1)}, u32[]{:S(2)}, u32[]{:S(2)}) collective-permute-start(f32[256,288]{1,0:T(8,128)S(1)} %maximum_select_fusion), channel_id=1, source_target_pairs={{0,16},{16,0},{32,48},{48,32},{64,80},{80,64},{96,112},{112,96},{1... | collective-permute-start | bytes 884744 | tf_op jit(solution)/shard_map/ppermute | solution.py:12
  36.2 12.3 %collective-permute-start.1 = (f32[256,288]{1,0:T(8,128)S(1)}, f32[256,288]{1,0:T(8,128)S(1)}, u32[]{:S(2)}, u32[]{:S(2)}) collective-permute-start(f32[256,288]{1,0:T(8,128)S(1)} %add.379), channel_id=1, source_target_pairs={{0,32},{16,48},{32,0},{48,16},{64,96},{80,112},{96,64},{112,80},{1... | collective-permute-start | bytes 884744 | tf_op jit(solution)/shard_map/ppermute | solution.py:12
  48.6 12.9 %collective-permute-start.2 = (f32[256,288]{1,0:T(8,128)S(1)}, f32[256,288]{1,0:T(8,128)S(1)}, u32[]{:S(2)}, u32[]{:S(2)}) collective-permute-start(f32[256,288]{1,0:T(8,128)S(1)} %add.380), channel_id=1, source_target_pairs={{0,64},{16,80},{32,96},{48,112},{64,0},{80,16},{96,32},{112,48},{1... | collective-permute-start | bytes 884744 | tf_op jit(solution)/shard_map/ppermute | solution.py:12
  61.5 10.5 %collective-permute-start.3 = (f32[256,288]{1,0:T(8,128)S(1)}, f32[256,288]{1,0:T(8,128)S(1)}, u32[]{:S(2)}, u32[]{:S(2)}) collective-permute-start(f32[256,288]{1,0:T(8,128)S(1)} %add.381), channel_id=1, source_target_pairs={{0,128},{16,144},{32,160},{48,176},{64,192},{80,208},{96,224},{112... | collective-permute-start | bytes 884744 | tf_op jit(solution)/shard_map/ppermute | solution.py:12
  72.0 11.1 %collective-permute-start.4 = (f32[256,288]{1,0:T(8,128)S(1)}, f32[256,288]{1,0:T(8,128)S(1)}, u32[]{:S(2)}, u32[]{:S(2)}) collective-permute-start(f32[256,288]{1,0:T(8,128)S(1)} %add.382), channel_id=1, source_target_pairs={{0,256},{16,272},{32,288},{48,304},{64,320},{80,336},{96,352},{112... | collective-permute-start | bytes 884744 | tf_op jit(solution)/shard_map/ppermute | solution.py:12
  145.7 3.8 %copy-start.4 = (f32[256,256]{1,0:T(8,128)S(1)}, f32[256,256]{1,0:T(8,128)}, u32[]{:S(2)}) copy-start(f32[256,256]{1,0:T(8,128)} %shard_map.101) | copy-start | bytes 786436
  163.5 20.0 %copy-start.5 = (f32[16,16,256]{2,1,0:T(8,128)S(1)}, f32[16,16,256]{2,1,0:T(8,128)}, u32[]{:S(2)}) copy-start(f32[16,16,256]{2,1,0:T(8,128)} %get-tuple-element.20) | copy-start | bytes 786436
  163.6 21.0 %copy-start.7 = (f32[16,2048]{1,0:T(8,128)}, f32[16,2048]{1,0:T(8,128)S(1)}, u32[]{:S(2)}) copy-start(f32[16,2048]{1,0:T(8,128)S(1)} %constant_dynamic-slice_fusion) | copy-start | bytes 393220
  165.5 14.4 %collective-permute-start.5 = (f32[16,256]{1,0:T(8,128)S(1)}, f32[16,256]{1,0:T(8,128)S(1)}, u32[]{:S(2)}, u32[]{:S(2)}) collective-permute-start(f32[16,256]{1,0:T(8,128)S(1)} %fusion.62), channel_id=1, source_target_pairs={{0,16},{16,0},{32,48},{48,32},{64,80},{80,64},{96,112},{112,96},{1... | collective-permute-start | bytes 49160 | tf_op jit(solution)/shard_map/ppermute | solution.py:12
  180.0 4.6 %collective-permute-start.6 = (f32[16,256]{1,0:T(8,128)S(1)}, f32[16,256]{1,0:T(8,128)S(1)}, u32[]{:S(2)}, u32[]{:S(2)}) collective-permute-start(f32[16,256]{1,0:T(8,128)S(1)} %add.402), channel_id=1, source_target_pairs={{0,32},{16,48},{32,0},{48,16},{64,96},{80,112},{96,64},{112,80},{1... | collective-permute-start | bytes 49160 | tf_op jit(solution)/shard_map/ppermute | solution.py:12
  184.6 6.2 %collective-permute-start.7 = (f32[16,256]{1,0:T(8,128)S(1)}, f32[16,256]{1,0:T(8,128)S(1)}, u32[]{:S(2)}, u32[]{:S(2)}) collective-permute-start(f32[16,256]{1,0:T(8,128)S(1)} %add.403), channel_id=1, source_target_pairs={{0,64},{16,80},{32,96},{48,112},{64,0},{80,16},{96,32},{112,48},{1... | collective-permute-start | bytes 49160 | tf_op jit(solution)/shard_map/ppermute | solution.py:12
  189.9 14.1 %copy-start.6 = (f32[256,256]{1,0:T(8,128)}, f32[256,256]{1,0:T(8,128)S(1)}, u32[]{:S(2)}) copy-start(f32[256,256]{1,0:T(8,128)S(1)} %fusion.12) | copy-start | bytes 786436
  190.8 9.2 %collective-permute-start.8 = (f32[16,256]{1,0:T(8,128)S(1)}, f32[16,256]{1,0:T(8,128)S(1)}, u32[]{:S(2)}, u32[]{:S(2)}) collective-permute-start(f32[16,256]{1,0:T(8,128)S(1)} %add.404), channel_id=1, source_target_pairs={{0,128},{16,144},{32,160},{48,176},{64,192},{80,208},{96,224},{112... | collective-permute-start | bytes 49160 | tf_op jit(solution)/shard_map/ppermute | solution.py:12
  200.1 8.8 %collective-permute-start.9 = (f32[16,256]{1,0:T(8,128)S(1)}, f32[16,256]{1,0:T(8,128)S(1)}, u32[]{:S(2)}, u32[]{:S(2)}) collective-permute-start(f32[16,256]{1,0:T(8,128)S(1)} %add.405), channel_id=1, source_target_pairs={{0,256},{16,272},{32,288},{48,304},{64,320},{80,336},{96,352},{112... | collective-permute-start | bytes 49160 | tf_op jit(solution)/shard_map/ppermute | solution.py:12
Sparse Core Ops, SparseCore 0:
  10.1 69.3 all-gather.3
  81.6 70.5 all-gather.5

commit v3 on v2

--- a/solution.py
+++ b/solution.py
@@ -110,6 +110,20 @@
     return value
 
 
+def butterfly_gather(value, axis):
+    levels = lax.axis_size(axis).bit_length() - 1
+    own = lax.axis_index(axis)
+    value = value[None]
+    for section in range(levels):
+        partner = from_partner(value, axis, section)
+        value = jnp.where(
+            own >> section & 1 == 0,
+            jnp.concatenate([value, partner], 0),
+            jnp.concatenate([partner, value], 0),
+        )
+    return value
+
+
 def body(panel_t, trailing, prev_lower_t, prev_upper, leaf_picks, merge_picks):
     slab_rows = panel_t.shape[0]
     rows_here = panel_t.shape[1]
@@ -120,16 +134,13 @@
     leaf_group, leaf_slot = trace_pivots(merge_picks, row_devices)
     owner_mask = leaf_group == own_row
     local_rows = jnp.take(leaf_picks[0], leaf_slot)
-    own_trailing = jnp.take(trailing, local_rows, axis=0)
     own_columns = jnp.take(jnp.concatenate([panel_t, prev_lower_t], 0), local_rows, axis=1)
-    own_pivots = jnp.concatenate([own_trailing, own_columns.T], 1)
-    pivot_data = butterfly_sum(jnp.where(owner_mask[:, None], own_pivots, 0.0), "rows")
-    pivot_trailing = pivot_data[:, : own_trailing.shape[1]]
-    pivot_columns = lax.all_gather(
-        pivot_data[:, own_trailing.shape[1] :].T, "cols", axis=0, tiled=False
-    )
+    pivot_part = butterfly_sum(jnp.where(owner_mask[None, :], own_columns, 0.0), "rows")
+    pivot_columns = butterfly_gather(pivot_part, "cols")
     block_t = pivot_columns[:, :slab_rows].reshape(order, order)
     prev_pivots = pivot_columns[:, slab_rows:].reshape(order, order)
+    own_trailing = jnp.take(trailing, local_rows, axis=0)
+    pivot_trailing = butterfly_sum(jnp.where(owner_mask[:, None], own_trailing, 0.0), "rows")
     middle_pivots = pivot_trailing - contract_first(prev_pivots, prev_upper)
     middle = trailing - contract_first(
         lax.all_gather(prev_lower_t, "cols", axis=0, tiled=True), prev_upper

time: 219 us -> 247 us (1.13)
  starting transfers between devices: 45.9 us -> 80.4 us
  blocking collectives: 26.8 us -> 0 us
  waiting for transfers between devices: 41.8 us -> 59.1 us
  other arithmetic: 2.31 us -> 4.91 us
    ppermute x10 -> x19, starting transfers between devices: 45.8 us -> 80.3 us  [from_partner(): lax.ppermute(shard, axis, [(i, i ^ 1 << apart) for i in range(lax.axis_si...]
    all_gather x1 -> x0, blocking collectives: 26.8 us -> none  [body(): lax.all_gather(pivot_data[:, own_trailing.shape[1]:].T, 'cols', axis=0, t...]
    ppermute x10 -> x19, waiting for transfers between devices: 41.1 us -> 58.4 us  [from_partner(): lax.ppermute(shard, axis, [(i, i ^ 1 << apart) for i in range(lax.axis_si...]
  transfers between devices with their start and end apart: 12 -> 21, of which waited for: 7 -> 10; matrix products, arithmetic and copies ran while one was open for 25% -> 23% of each run, Pallas kernels for 15% -> 13%
where the time goes in v3:
time: 247 us; the launch traced here: 245 us
  starting transfers between devices  80.4 us (33%)
  waiting for transfers between devices  59.1 us (24%)
  Pallas kernels  32.9 us (13%)
  matrix products  29.7 us (12%)
  local copies, waits for them, and re-layouts  22.8 us (9%)
  between operations  15 us (6%)
  other arithmetic  4.91 us (2%)
    ppermute x19, starting transfers between devices, from_partner(): lax.ppermute(shard, axis, [(i, i ^ 1 << apart) for i in range(lax.axis_si...  80.3 us
    ppermute x19, waiting for transfers between devices, from_partner(): lax.ppermute(shard, axis, [(i, i ^ 1 << apart) for i in range(lax.axis_si...  58.4 us
    pallas_call x1, Pallas kernels, factor(): pl.pallas_call(elimination_kernel, out_shape=jax.ShapeDtypeStruct(matrix....  32.9 us
    dot_general x29, matrix products, product(): return jnp.dot(left_side, right_side, precision=full_precision)  13.3 us
    gather x5, local copies, waits for them, and re-layouts, trace_pivots(): position = merge_picks[offset_rows + leaf_group, leaf_slot]  11.9 us
    dot_general x3, matrix products, contract_first(): lax.dot_general(left_side, right_side, (((0,), (0,)), ((), ())), precisio...  11.3 us
  transfers between devices with their start and end apart: 21, of which 10 were waited for; matrix products, arithmetic and copies ran while one was open for 23% of the time, Pallas kernels for 13%

profile of v3, /device:TPU:1, one launch (start us, length us, event | category | flops | bytes accessed | tf_op | source)
XLA Modules:
  0.0 244.8 jit_solution(15705554031505977355)
XLA Ops:
  9.3 2.5 %gather_fusion = s32[256]{0:T(256)S(1)} fusion(s32[31,256]{1,0:T(8,128)S(1)} %copy-done.2, s32[256]{0:T(256)} %constant.192), kind=kCustom, calls=%fused_computation | custom fusion | bytes 4096 | tf_op jit(solution)/shard_map/gather | solution.py:22
  11.8 2.3 gather_fusion.1
  14.2 2.3 gather_fusion.2
  16.6 2.3 gather_fusion.3
  19.0 2.3 gather_fusion.4
  21.4 1.9 gather_fusion.5
  25.7 8.8 %collective-permute-start = (f32[32,256]{0,1:T(8,128)S(1)}, f32[32,256]{0,1:T(8,128)S(1)}, u32[]{:S(2)}, u32[]{:S(2)}) collective-permute-start(f32[32,256]{0,1:T(8,128)S(1)} %select_bitcast_fusion), channel_id=1, source_target_pairs={{0,16},{16,0},{32,48},{48,32},{64,80},{80,64},{96,112},{112,96},{1... | collective-permute-start | bytes 98312 | tf_op jit(solution)/shard_map/ppermute | solution.py:12
  38.5 4.8 %collective-permute-done.1 = f32[32,256]{0,1:T(8,128)S(1)} collective-permute-done((f32[32,256]{0,1:T(8,128)S(1)}, f32[32,256]{0,1:T(8,128)S(1)}, u32[]{:S(2)}, u32[]{:S(2)}) %collective-permute-start.1) | collective-permute-done | bytes 32800 | tf_op jit(solution)/shard_map/ppermute | solution.py:12
  45.2 5.3 %collective-permute-done.2 = f32[32,256]{0,1:T(8,128)S(1)} collective-permute-done((f32[32,256]{0,1:T(8,128)S(1)}, f32[32,256]{0,1:T(8,128)S(1)}, u32[]{:S(2)}, u32[]{:S(2)}) %collective-permute-start.2) | collective-permute-done | bytes 32800 | tf_op jit(solution)/shard_map/ppermute | solution.py:12
  52.5 4.2 %collective-permute-done.3 = f32[32,256]{0,1:T(8,128)S(1)} collective-permute-done((f32[32,256]{0,1:T(8,128)S(1)}, f32[32,256]{0,1:T(8,128)S(1)}, u32[]{:S(2)}, u32[]{:S(2)}) %collective-permute-start.3) | collective-permute-done | bytes 32800 | tf_op jit(solution)/shard_map/ppermute | solution.py:12
  59.7 4.2 %collective-permute-done.4 = f32[32,256]{0,1:T(8,128)S(1)} collective-permute-done((f32[32,256]{0,1:T(8,128)S(1)}, f32[32,256]{0,1:T(8,128)S(1)}, u32[]{:S(2)}, u32[]{:S(2)}) %collective-permute-start.4) | collective-permute-done | bytes 32800 | tf_op jit(solution)/shard_map/ppermute | solution.py:12
  65.9 6.0 %collective-permute-start.9 = (f32[256,256]{0,1:T(8,128)S(1)}, f32[256,256]{0,1:T(8,128)S(1)}, u32[]{:S(2)}, u32[]{:S(2)}) collective-permute-start(f32[256,256]{0,1:T(8,128)S(1)} %select_select_fusion), channel_id=1, source_target_pairs={{0,16},{16,0},{32,48},{48,32},{64,80},{80,64},{96,112},{112,96},{1... | collective-permute-start | bytes 786440 | tf_op jit(solution)/shard_map/ppermute | solution.py:12
  74.1 4.9 %collective-permute-done.6 = f32[2,32,256]{2,1,0:T(8,128)S(1)} collective-permute-done((f32[2,32,256]{2,1,0:T(8,128)S(1)}, f32[2,32,256]{2,1,0:T(8,128)S(1)}, u32[]{:S(2)}, u32[]{:S(2)}) %collective-permute-start.6) | collective-permute-done | bytes 65568 | tf_op jit(solution)/shard_map/ppermute | solution.py:12
  79.0 6.3 %collective-permute-start.7 = (f32[4,32,256]{2,1,0:T(8,128)S(1)}, f32[4,32,256]{2,1,0:T(8,128)S(1)}, u32[]{:S(2)}, u32[]{:S(2)}) collective-permute-start(f32[4,32,256]{2,1,0:T(8,128)S(1)} %maximum_select_fusion.2), channel_id=1, source_target_pairs={{0,4},{1,5},{2,6},{3,7},{4,0},{5,1},{6,2},{7,3},{8,12},{9,13},{10,... | collective-permute-start | bytes 393224 | tf_op jit(solution)/shard_map/ppermute | solution.py:12
  85.3 3.1 %collective-permute-start.10 = (f32[256,256]{0,1:T(8,128)S(1)}, f32[256,256]{0,1:T(8,128)S(1)}, u32[]{:S(2)}, u32[]{:S(2)}) collective-permute-start(f32[256,256]{0,1:T(8,128)S(1)} %fusion.114), channel_id=1, source_target_pairs={{0,32},{16,48},{32,0},{48,16},{64,96},{80,112},{96,64},{112,80},{1... | collective-permute-start | bytes 786440 | tf_op jit(solution)/shard_map/ppermute | solution.py:12
  88.5 10.5 %collective-permute-done.7 = f32[4,32,256]{2,1,0:T(8,128)S(1)} collective-permute-done((f32[4,32,256]{2,1,0:T(8,128)S(1)}, f32[4,32,256]{2,1,0:T(8,128)S(1)}, u32[]{:S(2)}, u32[]{:S(2)}) %collective-permute-start.7) | collective-permute-done | bytes 131104 | tf_op jit(solution)/shard_map/ppermute | solution.py:12
  98.9 10.0 %collective-permute-start.8 = (f32[8,32,256]{2,1,0:T(8,128)S(1)}, f32[8,32,256]{2,1,0:T(8,128)S(1)}, u32[]{:S(2)}, u32[]{:S(2)}) collective-permute-start(f32[8,32,256]{2,1,0:T(8,128)S(1)} %maximum_select_fusion.1), channel_id=1, source_target_pairs={{0,8},{1,9},{2,10},{3,11},{4,12},{5,13},{6,14},{7,15},{8,0},{9,1},... | collective-permute-start | bytes 786440 | tf_op jit(solution)/shard_map/ppermute | solution.py:12
  109.2 8.4 %collective-permute-start.11 = (f32[256,256]{0,1:T(8,128)S(1)}, f32[256,256]{0,1:T(8,128)S(1)}, u32[]{:S(2)}, u32[]{:S(2)}) collective-permute-start(f32[256,256]{0,1:T(8,128)S(1)} %add.434), channel_id=1, source_target_pairs={{0,64},{16,80},{32,96},{48,112},{64,0},{80,16},{96,32},{112,48},{1... | collective-permute-start | bytes 786440 | tf_op jit(solution)/shard_map/ppermute | solution.py:12
  117.6 18.9 %collective-permute-done.8 = f32[8,32,256]{2,1,0:T(8,128)S(1)} collective-permute-done((f32[8,32,256]{2,1,0:T(8,128)S(1)}, f32[8,32,256]{2,1,0:T(8,128)S(1)}, u32[]{:S(2)}, u32[]{:S(2)}) %collective-permute-start.8) | collective-permute-done | bytes 262176 | tf_op jit(solution)/shard_map/ppermute | solution.py:12
  138.1 32.9 %shard_map.101 = f32[256,256]{1,0:T(8,128)} custom-call(f32[256,256]{1,0:T(8,128)} %bitcast.85), custom_call_target="tpu_custom_call" | custom-call | tf_op jit(solution)/shard_map/pallas_call | solution.py:86
  172.2 2.4 gather_fusion.7
  184.6 3.1 %collective-permute-start.12 = (f32[256,256]{0,1:T(8,128)S(1)}, f32[256,256]{0,1:T(8,128)S(1)}, u32[]{:S(2)}, u32[]{:S(2)}) collective-permute-start(f32[256,256]{0,1:T(8,128)S(1)} %add.435), channel_id=1, source_target_pairs={{0,128},{16,144},{32,160},{48,176},{64,192},{80,208},{96,224},{112... | collective-permute-start | bytes 786440 | tf_op jit(solution)/shard_map/ppermute | solution.py:12
  189.4 4.2 %collective-permute-done.12 = f32[256,256]{0,1:T(8,128)S(1)} collective-permute-done((f32[256,256]{0,1:T(8,128)S(1)}, f32[256,256]{0,1:T(8,128)S(1)}, u32[]{:S(2)}, u32[]{:S(2)}) %collective-permute-start.12) | collective-permute-done | bytes 262176 | tf_op jit(solution)/shard_map/ppermute | solution.py:12
  193.7 5.2 %collective-permute-start.13 = (f32[256,256]{0,1:T(8,128)S(1)}, f32[256,256]{0,1:T(8,128)}, u32[]{:S(2)}, u32[]{:S(2)}) collective-permute-start(f32[256,256]{0,1:T(8,128)S(1)} %add.436), channel_id=1, source_target_pairs={{0,256},{16,272},{32,288},{48,304},{64,320},{80,336},{96,352},{112... | collective-permute-start | bytes 786440 | tf_op jit(solution)/shard_map/ppermute | solution.py:12
  198.9 3.5 %fusion.56 = f32[256,2048]{1,0:T(8,128)S(1)} fusion(f32[256,256]{1,0:T(8,128)S(1)} %convolution_divide_fusion, f32[256,2048]{1,0:T(8,128)} %all-gather.3.cloned.1.call-done), kind=kOutput, calls=%fused_computation.131 | convolution fusion | flops 1610612736 | bytes 4456448 | tf_op jit(solution)/shard_map/dot_general | solution.py:152
  204.2 3.7 %collective-permute-start.14 = (f32[16,256]{1,0:T(8,128)S(1)}, f32[16,256]{1,0:T(8,128)S(1)}, u32[]{:S(2)}, u32[]{:S(2)}) collective-permute-start(f32[16,256]{1,0:T(8,128)S(1)} %fusion.64), channel_id=1, source_target_pairs={{0,16},{16,0},{32,48},{48,32},{64,80},{80,64},{96,112},{112,96},{1... | collective-permute-start | bytes 49160 | tf_op jit(solution)/shard_map/ppermute | solution.py:12
  208.7 3.1 %collective-permute-start.15 = (f32[16,256]{1,0:T(8,128)S(1)}, f32[16,256]{1,0:T(8,128)}, u32[]{:S(2)}, u32[]{:S(2)}) collective-permute-start(f32[16,256]{1,0:T(8,128)S(1)} %add.438), channel_id=1, source_target_pairs={{0,32},{16,48},{32,0},{48,16},{64,96},{80,112},{96,64},{112,80},{1... | collective-permute-start | bytes 49160 | tf_op jit(solution)/shard_map/ppermute | solution.py:12
  214.0 5.0 %collective-permute-start.16 = (f32[16,256]{1,0:T(8,128)S(1)}, f32[16,256]{1,0:T(8,128)S(1)}, u32[]{:S(2)}, u32[]{:S(2)}) collective-permute-start(f32[16,256]{1,0:T(8,128)S(1)} %add.439), channel_id=1, source_target_pairs={{0,64},{16,80},{32,96},{48,112},{64,0},{80,16},{96,32},{112,48},{1... | collective-permute-start | bytes 49160 | tf_op jit(solution)/shard_map/ppermute | solution.py:12
  220.4 2.1 collective-permute-start.17
  222.6 5.9 %convolution_subtract_fusion.1 = f32[2048,256]{1,0:T(8,128)S(1)} fusion(f32[2048,256]{1,0:T(8,128)} %param.7, f32[256,2048]{1,0:T(8,128)} %all-gather.5.cloned.1.call-done, f32[256,256]{1,0:T(8,128)S(1)} %copy-done), kind=kOutput, calls=%fused_computation.10 | convolution fusion | flops 1611137024 | bytes 6553600 | tf_op jit(solution)/shard_map/dot_general | solution.py:95
  228.5 4.0 %collective-permute-start.18 = (f32[16,256]{1,0:T(8,128)S(1)}, f32[16,256]{1,0:T(8,128)S(1)}, u32[]{:S(2)}, u32[]{:S(2)}) collective-permute-start(f32[16,256]{1,0:T(8,128)S(1)} %add.441), channel_id=1, source_target_pairs={{0,256},{16,272},{32,288},{48,304},{64,320},{80,336},{96,352},{112... | collective-permute-start | bytes 49160 | tf_op jit(solution)/shard_map/ppermute | solution.py:12
  232.6 4.8 %convolution_subtract_fusion = f32[2048,256]{1,0:T(8,128)} fusion(f32[2048,256]{1,0:T(8,128)S(1)} %convolution_subtract_fusion.1, f32[256,2048]{1,0:T(8,128)S(1)} %fusion.56, f32[256,256]{1,0:T(8,128)S(1)} %fusion.12), kind=kOutput, calls=%fused_computation.9 | convolution fusion | flops 1611137024 | bytes 6553600 | tf_op jit(solution)/shard_map/dot_general | solution.py:95
  (118 shorter events, 40.8 us)
Async XLA Ops:
  7.2 204.7 %copy-start = (f32[256,256]{1,0:T(8,128)S(1)}, f32[256,256]{1,0:T(8,128)}, u32[]{:S(2)}) copy-start(f32[256,256]{1,0:T(8,128)} %param.9) | copy-start | bytes 786436
  7.2 2.1 copy-start.2
  7.2 191.7 %all-gather.3.cloned.1.call-start = ((), (), s32[]{:S(2)}) async-start(), calls=%async_computation | async-start | bytes 2228224 | tf_op jit(solution)/shard_map/all_gather | solution.py:148
  7.9 214.7 %all-gather.5.cloned.1.call-start = ((), (), s32[]{:S(2)}) async-start(), calls=%async_computation.1 | async-start | bytes 2228224 | tf_op jit(solution)/shard_map/all_gather | solution.py:146
  11.8 9.5 %copy-start.1 = (s32[1,256]{1,0:T(1,128)S(1)}, s32[1,256]{1,0:T(1,128)}, u32[]{:S(2)}) copy-start(s32[1,256]{1,0:T(1,128)} %param.10) | copy-start | bytes 3076
  19.0 39.6 %copy-start.3 = (f32[2048,256]{1,0:T(8,128)S(1)}, f32[2048,256]{1,0:T(8,128)}, u32[]{:S(2)}) copy-start(f32[2048,256]{1,0:T(8,128)} %param.7) | copy-start | bytes 6291460
  25.7 9.8 %collective-permute-start = (f32[32,256]{0,1:T(8,128)S(1)}, f32[32,256]{0,1:T(8,128)S(1)}, u32[]{:S(2)}, u32[]{:S(2)}) collective-permute-start(f32[32,256]{0,1:T(8,128)S(1)} %select_bitcast_fusion), channel_id=1, source_target_pairs={{0,16},{16,0},{32,48},{48,32},{64,80},{80,64},{96,112},{112,96},{1... | collective-permute-start | bytes 98312 | tf_op jit(solution)/shard_map/ppermute | solution.py:12
  36.6 6.7 %collective-permute-start.1 = (f32[32,256]{0,1:T(8,128)S(1)}, f32[32,256]{0,1:T(8,128)S(1)}, u32[]{:S(2)}, u32[]{:S(2)}) collective-permute-start(f32[32,256]{0,1:T(8,128)S(1)} %fusion.115), channel_id=1, source_target_pairs={{0,32},{16,48},{32,0},{48,16},{64,96},{80,112},{96,64},{112,80},{1... | collective-permute-start | bytes 98312 | tf_op jit(solution)/shard_map/ppermute | solution.py:12
  43.3 7.2 %collective-permute-start.2 = (f32[32,256]{0,1:T(8,128)S(1)}, f32[32,256]{0,1:T(8,128)S(1)}, u32[]{:S(2)}, u32[]{:S(2)}) collective-permute-start(f32[32,256]{0,1:T(8,128)S(1)} %add.411), channel_id=1, source_target_pairs={{0,64},{16,80},{32,96},{48,112},{64,0},{80,16},{96,32},{112,48},{1... | collective-permute-start | bytes 98312 | tf_op jit(solution)/shard_map/ppermute | solution.py:12
  50.5 6.1 %collective-permute-start.3 = (f32[32,256]{0,1:T(8,128)S(1)}, f32[32,256]{0,1:T(8,128)S(1)}, u32[]{:S(2)}, u32[]{:S(2)}) collective-permute-start(f32[32,256]{0,1:T(8,128)S(1)} %add.412), channel_id=1, source_target_pairs={{0,128},{16,144},{32,160},{48,176},{64,192},{80,208},{96,224},{112... | collective-permute-start | bytes 98312 | tf_op jit(solution)/shard_map/ppermute | solution.py:12
  56.7 7.3 %collective-permute-start.4 = (f32[32,256]{0,1:T(8,128)S(1)}, f32[32,256]{0,1:T(8,128)S(1)}, u32[]{:S(2)}, u32[]{:S(2)}) collective-permute-start(f32[32,256]{0,1:T(8,128)S(1)} %add.413), channel_id=1, source_target_pairs={{0,256},{16,272},{32,288},{48,304},{64,320},{80,336},{96,352},{112... | collective-permute-start | bytes 98312 | tf_op jit(solution)/shard_map/ppermute | solution.py:12
  63.9 8.1 %collective-permute-start.5 = (f32[1,32,256]{1,2,0:T(8,128)S(1)}, f32[1,32,256]{1,2,0:T(8,128)S(1)}, u32[]{:S(2)}, u32[]{:S(2)}) collective-permute-start(f32[1,32,256]{1,2,0:T(8,128)S(1)} %add_bitcast_fusion), channel_id=1, source_target_pairs={{0,1},{1,0},{2,3},{3,2},{4,5},{5,4},{6,7},{7,6},{8,9},{9,8},{10,11... | collective-permute-start | bytes 98312 | tf_op jit(solution)/shard_map/ppermute | solution.py:12
  65.9 19.4 %collective-permute-start.9 = (f32[256,256]{0,1:T(8,128)S(1)}, f32[256,256]{0,1:T(8,128)S(1)}, u32[]{:S(2)}, u32[]{:S(2)}) collective-permute-start(f32[256,256]{0,1:T(8,128)S(1)} %select_select_fusion), channel_id=1, source_target_pairs={{0,16},{16,0},{32,48},{48,32},{64,80},{80,64},{96,112},{112,96},{1... | collective-permute-start | bytes 786440 | tf_op jit(solution)/shard_map/ppermute | solution.py:12
  72.1 6.8 %collective-permute-start.6 = (f32[2,32,256]{2,1,0:T(8,128)S(1)}, f32[2,32,256]{2,1,0:T(8,128)S(1)}, u32[]{:S(2)}, u32[]{:S(2)}) collective-permute-start(f32[2,32,256]{2,1,0:T(8,128)S(1)} %maximum_select_fusion.3), channel_id=1, source_target_pairs={{0,2},{1,3},{2,0},{3,1},{4,6},{5,7},{6,4},{7,5},{8,10},{9,11},{10,... | collective-permute-start | bytes 196616 | tf_op jit(solution)/shard_map/ppermute | solution.py:12
  79.0 19.9 %collective-permute-start.7 = (f32[4,32,256]{2,1,0:T(8,128)S(1)}, f32[4,32,256]{2,1,0:T(8,128)S(1)}, u32[]{:S(2)}, u32[]{:S(2)}) collective-permute-start(f32[4,32,256]{2,1,0:T(8,128)S(1)} %maximum_select_fusion.2), channel_id=1, source_target_pairs={{0,4},{1,5},{2,6},{3,7},{4,0},{5,1},{6,2},{7,3},{8,12},{9,13},{10,... | collective-permute-start | bytes 393224 | tf_op jit(solution)/shard_map/ppermute | solution.py:12
  85.3 23.8 %collective-permute-start.10 = (f32[256,256]{0,1:T(8,128)S(1)}, f32[256,256]{0,1:T(8,128)S(1)}, u32[]{:S(2)}, u32[]{:S(2)}) collective-permute-start(f32[256,256]{0,1:T(8,128)S(1)} %fusion.114), channel_id=1, source_target_pairs={{0,32},{16,48},{32,0},{48,16},{64,96},{80,112},{96,64},{112,80},{1... | collective-permute-start | bytes 786440 | tf_op jit(solution)/shard_map/ppermute | solution.py:12
  98.9 37.5 %collective-permute-start.8 = (f32[8,32,256]{2,1,0:T(8,128)S(1)}, f32[8,32,256]{2,1,0:T(8,128)S(1)}, u32[]{:S(2)}, u32[]{:S(2)}) collective-permute-start(f32[8,32,256]{2,1,0:T(8,128)S(1)} %maximum_select_fusion.1), channel_id=1, source_target_pairs={{0,8},{1,9},{2,10},{3,11},{4,12},{5,13},{6,14},{7,15},{8,0},{9,1},... | collective-permute-start | bytes 786440 | tf_op jit(solution)/shard_map/ppermute | solution.py:12
  109.2 75.4 %collective-permute-start.11 = (f32[256,256]{0,1:T(8,128)S(1)}, f32[256,256]{0,1:T(8,128)S(1)}, u32[]{:S(2)}, u32[]{:S(2)}) collective-permute-start(f32[256,256]{0,1:T(8,128)S(1)} %add.434), channel_id=1, source_target_pairs={{0,64},{16,80},{32,96},{48,112},{64,0},{80,16},{96,32},{112,48},{1... | collective-permute-start | bytes 786440 | tf_op jit(solution)/shard_map/ppermute | solution.py:12
  172.2 3.6 %copy-start.4 = (f32[256,256]{1,0:T(8,128)S(1)}, f32[256,256]{1,0:T(8,128)}, u32[]{:S(2)}) copy-start(f32[256,256]{1,0:T(8,128)} %shard_map.101) | copy-start | bytes 786436
  184.6 9.1 %collective-permute-start.12 = (f32[256,256]{0,1:T(8,128)S(1)}, f32[256,256]{0,1:T(8,128)S(1)}, u32[]{:S(2)}, u32[]{:S(2)}) collective-permute-start(f32[256,256]{0,1:T(8,128)S(1)} %add.435), channel_id=1, source_target_pairs={{0,128},{16,144},{32,160},{48,176},{64,192},{80,208},{96,224},{112... | collective-permute-start | bytes 786440 | tf_op jit(solution)/shard_map/ppermute | solution.py:12
  193.7 25.3 %collective-permute-start.13 = (f32[256,256]{0,1:T(8,128)S(1)}, f32[256,256]{0,1:T(8,128)}, u32[]{:S(2)}, u32[]{:S(2)}) collective-permute-start(f32[256,256]{0,1:T(8,128)S(1)} %add.436), channel_id=1, source_target_pairs={{0,256},{16,272},{32,288},{48,304},{64,320},{80,336},{96,352},{112... | collective-permute-start | bytes 786440 | tf_op jit(solution)/shard_map/ppermute | solution.py:12
  202.4 5.5 %copy-start.6 = (f32[256,256]{1,0:T(8,128)S(1)}, f32[256,256]{1,0:T(8,128)}, u32[]{:S(2)}) copy-start(f32[256,256]{1,0:T(8,128)} %fusion.11) | copy-start | bytes 786436
  202.4 9.5 %copy-start.7 = (f32[16,16,256]{2,1,0:T(8,128)S(1)}, f32[16,16,256]{2,1,0:T(8,128)}, u32[]{:S(2)}) copy-start(f32[16,16,256]{2,1,0:T(8,128)} %get-tuple-element.20) | copy-start | bytes 786436
  202.4 10.9 %copy-start.8 = (f32[16,2048]{1,0:T(8,128)}, f32[16,2048]{1,0:T(8,128)S(1)}, u32[]{:S(2)}) copy-start(f32[16,2048]{1,0:T(8,128)S(1)} %constant_dynamic-slice_fusion) | copy-start | bytes 393220
  204.2 4.5 %collective-permute-start.14 = (f32[16,256]{1,0:T(8,128)S(1)}, f32[16,256]{1,0:T(8,128)S(1)}, u32[]{:S(2)}, u32[]{:S(2)}) collective-permute-start(f32[16,256]{1,0:T(8,128)S(1)} %fusion.64), channel_id=1, source_target_pairs={{0,16},{16,0},{32,48},{48,32},{64,80},{80,64},{96,112},{112,96},{1... | collective-permute-start | bytes 49160 | tf_op jit(solution)/shard_map/ppermute | solution.py:12
  208.7 4.6 %collective-permute-start.15 = (f32[16,256]{1,0:T(8,128)S(1)}, f32[16,256]{1,0:T(8,128)}, u32[]{:S(2)}, u32[]{:S(2)}) collective-permute-start(f32[16,256]{1,0:T(8,128)S(1)} %add.438), channel_id=1, source_target_pairs={{0,32},{16,48},{32,0},{48,16},{64,96},{80,112},{96,64},{112,80},{1... | collective-permute-start | bytes 49160 | tf_op jit(solution)/shard_map/ppermute | solution.py:12
  214.0 6.4 %collective-permute-start.16 = (f32[16,256]{1,0:T(8,128)S(1)}, f32[16,256]{1,0:T(8,128)S(1)}, u32[]{:S(2)}, u32[]{:S(2)}) collective-permute-start(f32[16,256]{1,0:T(8,128)S(1)} %add.439), channel_id=1, source_target_pairs={{0,64},{16,80},{32,96},{48,112},{64,0},{80,16},{96,32},{112,48},{1... | collective-permute-start | bytes 49160 | tf_op jit(solution)/shard_map/ppermute | solution.py:12
  220.4 12.1 %copy-start.5 = (f32[256,256]{1,0:T(8,128)}, f32[256,256]{1,0:T(8,128)S(1)}, u32[]{:S(2)}) copy-start(f32[256,256]{1,0:T(8,128)S(1)} %fusion.12) | copy-start | bytes 786436
  220.4 8.0 %collective-permute-start.17 = (f32[16,256]{1,0:T(8,128)S(1)}, f32[16,256]{1,0:T(8,128)S(1)}, u32[]{:S(2)}, u32[]{:S(2)}) collective-permute-start(f32[16,256]{1,0:T(8,128)S(1)} %add.440), channel_id=1, source_target_pairs={{0,128},{16,144},{32,160},{48,176},{64,192},{80,208},{96,224},{112... | collective-permute-start | bytes 49160 | tf_op jit(solution)/shard_map/ppermute | solution.py:12
  228.5 8.9 %collective-permute-start.18 = (f32[16,256]{1,0:T(8,128)S(1)}, f32[16,256]{1,0:T(8,128)S(1)}, u32[]{:S(2)}, u32[]{:S(2)}) collective-permute-start(f32[16,256]{1,0:T(8,128)S(1)} %add.441), channel_id=1, source_target_pairs={{0,256},{16,272},{32,288},{48,304},{64,320},{80,336},{96,352},{112... | collective-permute-start | bytes 49160 | tf_op jit(solution)/shard_map/ppermute | solution.py:12
Sparse Core Ops, SparseCore 0:
  10.1 69.7 all-gather.2
  82.0 84.2 all-gather.4

commit v4 on v2

--- a/solution.py
+++ b/solution.py
@@ -53,7 +53,7 @@
 def elimination_kernel(matrix_ref, reduced_ref):
     order = matrix_ref.shape[0]
     reduced_ref[...] = matrix_ref[...]
-    phase = 32
+    phase = 64
     for first_row in range(0, order - 1, phase):
         first_col = (first_row // 128) * 128
         height = order - first_row
@@ -110,6 +110,49 @@
     return value
 
 
+def digit_exchange(value, axis, shift, width):
+    size = lax.axis_size(axis)
+    digit = lax.axis_index(axis) >> shift & (1 << width) - 1
+    received = [value]
+    for offset in range(1, 1 << width):
+        pairs = [(i, i ^ offset << shift) for i in range(size)]
+        received.append(lax.ppermute(value, axis, pairs))
+    stacked = jnp.stack(received)
+    return [
+        lax.dynamic_index_in_dim(stacked, position ^ digit, 0, keepdims=False)
+        for position in range(1 << width)
+    ]
+
+
+def digit_plan(size):
+    plan = []
+    shift = 0
+    if size.bit_length() % 2 == 0:
+        plan.append((0, 1))
+        shift = 1
+    while 1 << shift < size:
+        plan.append((shift, 2))
+        shift += 2
+    return plan
+
+
+def exchange_sum(value, axis):
+    for shift, width in digit_plan(lax.axis_size(axis)):
+        parts = digit_exchange(value, axis, shift, width)
+        total = parts[0]
+        for part in parts[1:]:
+            total = total + part
+        value = total
+    return value
+
+
+def exchange_gather(value, axis):
+    value = value[None]
+    for shift, width in digit_plan(lax.axis_size(axis)):
+        value = jnp.concatenate(digit_exchange(value, axis, shift, width), 0)
+    return value
+
+
 def body(panel_t, trailing, prev_lower_t, prev_upper, leaf_picks, merge_picks):
     slab_rows = panel_t.shape[0]
     rows_here = panel_t.shape[1]
@@ -120,14 +163,13 @@
     leaf_group, leaf_slot = trace_pivots(merge_picks, row_devices)
     owner_mask = leaf_group == own_row
     local_rows = jnp.take(leaf_picks[0], leaf_slot)
+    own_columns = jnp.take(jnp.concatenate([panel_t, prev_lower_t], 0), local_rows, axis=1)
+    pivot_part = exchange_sum(jnp.where(owner_mask[None, :], own_columns, 0.0), "rows")
+    pivot_columns = exchange_gather(pivot_part, "cols")
     own_trailing = jnp.take(trailing, local_rows, axis=0)
-    own_columns = jnp.take(jnp.concatenate([panel_t, prev_lower_t], 0), local_rows, axis=1)
-    own_pivots = jnp.concatenate([own_trailing, own_columns.T], 1)
-    pivot_data = butterfly_sum(jnp.where(owner_mask[:, None], own_pivots, 0.0), "rows")
-    pivot_trailing = pivot_data[:, : own_trailing.shape[1]]
-    pivot_columns = lax.all_gather(
-        pivot_data[:, own_trailing.shape[1] :].T, "cols", axis=0, tiled=False
-    )
+    own_trailing = jnp.where(owner_mask[:, None], own_trailing, 0.0)
+    own_trailing, pivot_columns = lax.optimization_barrier((own_trailing, pivot_columns))
+    pivot_trailing = exchange_sum(own_trailing, "rows")
     block_t = pivot_columns[:, :slab_rows].reshape(order, order)
     prev_pivots = pivot_columns[:, slab_rows:].reshape(order, order)
     middle_pivots = pivot_trailing - contract_first(prev_pivots, prev_upper)

time: 219 us -> 244 us (1.11)
  starting transfers between devices: 45.9 us -> 95.1 us
  blocking collectives: 26.8 us -> 0 us
  waiting for transfers between devices: 41.8 us -> 38.3 us
  other arithmetic: 2.31 us -> 5.57 us
    ppermute x0 -> x20, starting transfers between devices: none -> 76 us  [digit_exchange(): received.append(lax.ppermute(value, axis, pairs))]
    ppermute x10 -> x5, waiting for transfers between devices: 41.1 us -> 1.62 us  [from_partner(): lax.ppermute(shard, axis, [(i, i ^ 1 << apart) for i in range(lax.axis_si...]
    ppermute x0 -> x20, waiting for transfers between devices: none -> 36 us  [digit_exchange(): received.append(lax.ppermute(value, axis, pairs))]
    ppermute x10 -> x5, starting transfers between devices: 45.8 us -> 19 us  [from_partner(): lax.ppermute(shard, axis, [(i, i ^ 1 << apart) for i in range(lax.axis_si...]
    all_gather x1 -> x0, blocking collectives: 26.8 us -> none  [body(): lax.all_gather(pivot_data[:, own_trailing.shape[1]:].T, 'cols', axis=0, t...]
  transfers between devices with their start and end apart: 12 -> 27, of which waited for: 7 -> 12; matrix products, arithmetic and copies ran while one was open for 25% -> 23% of each run, Pallas kernels for 15% -> 14%
where the time goes in v4:
time: 244 us; the launch traced here: 239 us
  starting transfers between devices  95.1 us (39%)
  waiting for transfers between devices  38.3 us (16%)
  Pallas kernels  33.6 us (14%)
  matrix products  28 us (11%)
  local copies, waits for them, and re-layouts  23.6 us (10%)
  between operations  15.2 us (6%)
  other arithmetic  5.57 us (2%)
    ppermute x20, starting transfers between devices, digit_exchange(): received.append(lax.ppermute(value, axis, pairs))  76 us
    ppermute x20, waiting for transfers between devices, digit_exchange(): received.append(lax.ppermute(value, axis, pairs))  36 us
    pallas_call x1, Pallas kernels, factor(): pl.pallas_call(elimination_kernel, out_shape=jax.ShapeDtypeStruct(matrix....  33.6 us
    ppermute x5, starting transfers between devices, from_partner(): lax.ppermute(shard, axis, [(i, i ^ 1 << apart) for i in range(lax.axis_si...  19 us
    gather x5, local copies, waits for them, and re-layouts, trace_pivots(): position = merge_picks[offset_rows + leaf_group, leaf_slot]  12 us
    dot_general x29, matrix products, product(): return jnp.dot(left_side, right_side, precision=full_precision)  11.6 us
    dot_general x3, matrix products, contract_first(): lax.dot_general(left_side, right_side, (((0,), (0,)), ((), ())), precisio...  11.2 us
  transfers between devices with their start and end apart: 27, of which 12 were waited for; matrix products, arithmetic and copies ran while one was open for 23% of the time, Pallas kernels for 14%

profile of v4, /device:TPU:1, one launch (start us, length us, event | category | flops | bytes accessed | tf_op | source)
XLA Modules:
  0.0 239.4 jit_solution(11705703436856108721)
XLA Ops:
  8.0 2.5 %gather_fusion = s32[256]{0:T(256)S(1)} fusion(s32[31,256]{1,0:T(8,128)} %param.11, s32[256]{0:T(256)} %constant.261), kind=kCustom, calls=%fused_computation | custom fusion | bytes 4096 | tf_op jit(solution)/shard_map/gather | solution.py:22
  10.5 2.4 %gather_fusion.1 = s32[256]{0:T(256)S(1)} fusion(s32[31,256]{1,0:T(8,128)} %param.11, s32[256]{0:T(256)S(1)} %bitcast.135), kind=kCustom, calls=%fused_computation.1 | custom fusion | bytes 4096 | tf_op jit(solution)/shard_map/gather | solution.py:22
  13.0 2.3 gather_fusion.2
  15.4 2.3 gather_fusion.3
  27.2 8.8 %collective-permute-start = (f32[32,256]{0,1:T(8,128)S(1)}, f32[32,256]{0,1:T(8,128)S(1)}, u32[]{:S(2)}, u32[]{:S(2)}) collective-permute-start(f32[32,256]{0,1:T(8,128)S(1)} %fusion.19), channel_id=1, source_target_pairs={{0,16},{16,0},{32,48},{48,32},{64,80},{80,64},{96,112},{112,96},{1... | collective-permute-start | bytes 98312 | tf_op jit(solution)/shard_map/ppermute | solution.py:119
  40.9 5.1 %collective-permute-start.1 = (f32[32,256]{1,0:T(8,128)S(1)}, f32[32,256]{1,0:T(8,128)S(1)}, u32[]{:S(2)}, u32[]{:S(2)}) collective-permute-start(f32[32,256]{1,0:T(8,128)S(1)} %bitcast.151), channel_id=1, source_target_pairs={{0,32},{16,48},{32,0},{48,16},{64,96},{80,112},{96,64},{112,80},{1... | collective-permute-start | bytes 98312 | tf_op jit(solution)/shard_map/ppermute | solution.py:119
  51.7 5.1 %collective-permute-start.4 = (f32[32,256]{1,0:T(8,128)S(1)}, f32[32,256]{1,0:T(8,128)S(1)}, u32[]{:S(2)}, u32[]{:S(2)}) collective-permute-start(f32[32,256]{1,0:T(8,128)S(1)} %fusion.123), channel_id=1, source_target_pairs={{0,128},{16,144},{32,160},{48,176},{64,192},{80,208},{96,224},{112... | collective-permute-start | bytes 98312 | tf_op jit(solution)/shard_map/ppermute | solution.py:119
  58.7 2.8 %collective-permute-start.9 = (f32[1,32,256]{2,1,0:T(8,128)S(1)}, f32[1,32,256]{2,1,0:T(8,128)S(1)}, u32[]{:S(2)}, u32[]{:S(2)}) collective-permute-start(f32[1,32,256]{2,1,0:T(8,128)S(1)} %dynamic-slice_add_fusion.1), channel_id=1, source_target_pairs={{0,3},{1,2},{2,1},{3,0},{4,7},{5,6},{6,5},{7,4},{8,11},{9,10},{10,... | collective-permute-start | bytes 98312 | tf_op jit(solution)/shard_map/ppermute | solution.py:119
  63.4 4.5 %collective-permute-start.7 = (f32[1,32,256]{2,1,0:T(8,128)S(1)}, f32[1,32,256]{2,1,0:T(8,128)S(1)}, u32[]{:S(2)}, u32[]{:S(2)}) collective-permute-start(f32[1,32,256]{2,1,0:T(8,128)S(1)} %dynamic-slice_add_fusion.1), channel_id=1, source_target_pairs={{0,1},{1,0},{2,3},{3,2},{4,5},{5,4},{6,7},{7,6},{8,9},{9,8},{10,11... | collective-permute-start | bytes 98312 | tf_op jit(solution)/shard_map/ppermute | solution.py:119
  69.7 9.8 %collective-permute-start.12 = (f32[4,32,256]{2,1,0:T(8,128)S(1)}, f32[4,32,256]{2,1,0:T(8,128)S(1)}, u32[]{:S(2)}, u32[]{:S(2)}) collective-permute-start(f32[4,32,256]{2,1,0:T(8,128)S(1)} %get-tuple-element.31), channel_id=1, source_target_pairs={{0,12},{1,13},{2,14},{3,15},{4,8},{5,9},{6,10},{7,11},{8,4},{9,5},... | collective-permute-start | bytes 393224 | tf_op jit(solution)/shard_map/ppermute | solution.py:119
  79.5 5.5 %collective-permute-start.11 = (f32[4,32,256]{2,1,0:T(8,128)S(1)}, f32[4,32,256]{2,1,0:T(8,128)S(1)}, u32[]{:S(2)}, u32[]{:S(2)}) collective-permute-start(f32[4,32,256]{2,1,0:T(8,128)S(1)} %get-tuple-element.31), channel_id=1, source_target_pairs={{0,8},{1,9},{2,10},{3,11},{4,12},{5,13},{6,14},{7,15},{8,0},{9,1},... | collective-permute-start | bytes 393224 | tf_op jit(solution)/shard_map/ppermute | solution.py:119
  85.0 3.6 %collective-permute-start.10 = (f32[4,32,256]{2,1,0:T(8,128)S(1)}, f32[4,32,256]{2,1,0:T(8,128)S(1)}, u32[]{:S(2)}, u32[]{:S(2)}) collective-permute-start(f32[4,32,256]{2,1,0:T(8,128)S(1)} %get-tuple-element.31), channel_id=1, source_target_pairs={{0,4},{1,5},{2,6},{3,7},{4,0},{5,1},{6,2},{7,3},{8,12},{9,13},{10,... | collective-permute-start | bytes 393224 | tf_op jit(solution)/shard_map/ppermute | solution.py:119
  88.6 6.6 %collective-permute-done.12 = f32[4,32,256]{2,1,0:T(8,128)S(1)} collective-permute-done((f32[4,32,256]{2,1,0:T(8,128)S(1)}, f32[4,32,256]{2,1,0:T(8,128)S(1)}, u32[]{:S(2)}, u32[]{:S(2)}) %collective-permute-start.12) | collective-permute-done | bytes 131104 | tf_op jit(solution)/shard_map/ppermute | solution.py:119
  95.2 3.8 %collective-permute-done.11 = f32[4,32,256]{2,1,0:T(8,128)S(1)} collective-permute-done((f32[4,32,256]{2,1,0:T(8,128)S(1)}, f32[4,32,256]{2,1,0:T(8,128)S(1)}, u32[]{:S(2)}, u32[]{:S(2)}) %collective-permute-start.11) | collective-permute-done | bytes 131104 | tf_op jit(solution)/shard_map/ppermute | solution.py:119
  99.0 13.5 %collective-permute-done.10 = f32[4,32,256]{2,1,0:T(8,128)S(1)} collective-permute-done((f32[4,32,256]{2,1,0:T(8,128)S(1)}, f32[4,32,256]{2,1,0:T(8,128)S(1)}, u32[]{:S(2)}, u32[]{:S(2)}) %collective-permute-start.10) | collective-permute-done | bytes 131104 | tf_op jit(solution)/shard_map/ppermute | solution.py:119
  113.6 33.6 %shard_map.101 = f32[256,256]{1,0:T(8,128)} custom-call(f32[256,256]{1,0:T(8,128)} %bitcast.138), custom_call_target="tpu_custom_call" | custom-call | tf_op jit(solution)/shard_map/pallas_call | solution.py:86
  148.3 2.4 gather_fusion.8
  158.7 2.9 %collective-permute-start.13 = (f32[256,256]{0,1:T(8,128)S(1)}, f32[256,256]{0,1:T(8,128)S(1)}, u32[]{:S(2)}, u32[]{:S(2)}) collective-permute-start(f32[256,256]{0,1:T(8,128)S(1)} %select_select_fusion), channel_id=1, source_target_pairs={{0,16},{16,0},{32,48},{48,32},{64,80},{80,64},{96,112},{112,96},{1... | collective-permute-start | bytes 786440 | tf_op jit(solution)/shard_map/ppermute | solution.py:119
  164.1 3.7 %collective-permute-start.16 = (f32[256,256]{0,1:T(8,128)S(1)}, f32[256,256]{0,1:T(8,128)S(1)}, u32[]{:S(2)}, u32[]{:S(2)}) collective-permute-start(f32[256,256]{0,1:T(8,128)S(1)} %bitcast.141), channel_id=1, source_target_pairs={{0,96},{16,112},{32,64},{48,80},{64,32},{80,48},{96,0},{112,16},{1... | collective-permute-start | bytes 786440 | tf_op jit(solution)/shard_map/ppermute | solution.py:119
  167.8 2.9 %collective-permute-start.15 = (f32[256,256]{0,1:T(8,128)S(1)}, f32[256,256]{0,1:T(8,128)S(1)}, u32[]{:S(2)}, u32[]{:S(2)}) collective-permute-start(f32[256,256]{0,1:T(8,128)S(1)} %bitcast.142), channel_id=1, source_target_pairs={{0,64},{16,80},{32,96},{48,112},{64,0},{80,16},{96,32},{112,48},{1... | collective-permute-start | bytes 786440 | tf_op jit(solution)/shard_map/ppermute | solution.py:119
  170.7 2.7 %collective-permute-start.14 = (f32[256,256]{0,1:T(8,128)S(1)}, f32[256,256]{0,1:T(8,128)S(1)}, u32[]{:S(2)}, u32[]{:S(2)}) collective-permute-start(f32[256,256]{0,1:T(8,128)S(1)} %bitcast.143), channel_id=1, source_target_pairs={{0,32},{16,48},{32,0},{48,16},{64,96},{80,112},{96,64},{112,80},{1... | collective-permute-start | bytes 786440 | tf_op jit(solution)/shard_map/ppermute | solution.py:119
  175.2 5.6 %collective-permute-done.16 = f32[256,256]{0,1:T(8,128)S(1)} collective-permute-done((f32[256,256]{0,1:T(8,128)S(1)}, f32[256,256]{0,1:T(8,128)S(1)}, u32[]{:S(2)}, u32[]{:S(2)}) %collective-permute-start.16) | collective-permute-done | bytes 262176 | tf_op jit(solution)/shard_map/ppermute | solution.py:119
  183.8 4.0 %collective-permute-start.19 = (f32[256,256]{0,1:T(8,128)}, f32[256,256]{0,1:T(8,128)}, u32[]{:S(2)}, u32[]{:S(2)}) collective-permute-start(f32[256,256]{0,1:T(8,128)} %fusion.121), channel_id=1, source_target_pairs={{0,384},{16,400},{32,416},{48,432},{64,448},{80,464},{96,480},{112... | collective-permute-start | bytes 786440 | tf_op jit(solution)/shard_map/ppermute | solution.py:119
  189.8 3.0 %collective-permute-start.17 = (f32[256,256]{0,1:T(8,128)}, f32[256,256]{0,1:T(8,128)}, u32[]{:S(2)}, u32[]{:S(2)}) collective-permute-start(f32[256,256]{0,1:T(8,128)} %fusion.121), channel_id=1, source_target_pairs={{0,128},{16,144},{32,160},{48,176},{64,192},{80,208},{96,224},{112... | collective-permute-start | bytes 786440 | tf_op jit(solution)/shard_map/ppermute | solution.py:119
  192.9 3.5 %fusion.62 = f32[256,2048]{1,0:T(8,128)S(1)} fusion(f32[256,256]{1,0:T(8,128)S(1)} %convolution_divide_fusion, f32[256,2048]{1,0:T(8,128)} %all-gather.3.cloned.1.call-done), kind=kOutput, calls=%fused_computation.161 | convolution fusion | flops 1610612736 | bytes 4456448 | tf_op jit(solution)/shard_map/dot_general | solution.py:183
  198.2 3.9 %collective-permute-start.20 = (f32[16,256]{1,0:T(8,128)S(1)}, f32[16,256]{1,0:T(8,128)S(1)}, u32[]{:S(2)}, u32[]{:S(2)}) collective-permute-start(f32[16,256]{1,0:T(8,128)S(1)} %fusion.70), channel_id=1, source_target_pairs={{0,16},{16,0},{32,48},{48,32},{64,80},{80,64},{96,112},{112,96},{1... | collective-permute-start | bytes 49160 | tf_op jit(solution)/shard_map/ppermute | solution.py:12
  203.4 3.2 %collective-permute-start.21 = (f32[16,256]{1,0:T(8,128)S(1)}, f32[16,256]{1,0:T(8,128)S(1)}, u32[]{:S(2)}, u32[]{:S(2)}) collective-permute-start(f32[16,256]{1,0:T(8,128)S(1)} %add.606), channel_id=1, source_target_pairs={{0,32},{16,48},{32,0},{48,16},{64,96},{80,112},{96,64},{112,80},{1... | collective-permute-start | bytes 49160 | tf_op jit(solution)/shard_map/ppermute | solution.py:12
  207.9 4.6 %collective-permute-start.22 = (f32[16,256]{1,0:T(8,128)S(1)}, f32[16,256]{1,0:T(8,128)S(1)}, u32[]{:S(2)}, u32[]{:S(2)}) collective-permute-start(f32[16,256]{1,0:T(8,128)S(1)} %add.607), channel_id=1, source_target_pairs={{0,64},{16,80},{32,96},{48,112},{64,0},{80,16},{96,32},{112,48},{1... | collective-permute-start | bytes 49160 | tf_op jit(solution)/shard_map/ppermute | solution.py:12
  213.8 2.6 %collective-permute-start.23 = (f32[16,256]{1,0:T(8,128)S(1)}, f32[16,256]{1,0:T(8,128)S(1)}, u32[]{:S(2)}, u32[]{:S(2)}) collective-permute-start(f32[16,256]{1,0:T(8,128)S(1)} %add.608), channel_id=1, source_target_pairs={{0,128},{16,144},{32,160},{48,176},{64,192},{80,208},{96,224},{112... | collective-permute-start | bytes 49160 | tf_op jit(solution)/shard_map/ppermute | solution.py:12
  216.5 5.7 %convolution_subtract_fusion.1 = f32[2048,256]{1,0:T(8,128)S(1)} fusion(f32[2048,256]{1,0:T(8,128)} %param.7, f32[256,2048]{1,0:T(8,128)} %all-gather.5.cloned.1.call-done, f32[256,256]{1,0:T(8,128)S(1)} %copy-done), kind=kOutput, calls=%fused_computation.10 | convolution fusion | flops 1611137024 | bytes 6553600 | tf_op jit(solution)/shard_map/dot_general | solution.py:95
  222.2 4.8 %collective-permute-start.24 = (f32[16,256]{1,0:T(8,128)S(1)}, f32[16,256]{1,0:T(8,128)S(1)}, u32[]{:S(2)}, u32[]{:S(2)}) collective-permute-start(f32[16,256]{1,0:T(8,128)S(1)} %add.609), channel_id=1, source_target_pairs={{0,256},{16,272},{32,288},{48,304},{64,320},{80,336},{96,352},{112... | collective-permute-start | bytes 49160 | tf_op jit(solution)/shard_map/ppermute | solution.py:12
  227.0 4.9 %convolution_subtract_fusion = f32[2048,256]{1,0:T(8,128)} fusion(f32[2048,256]{1,0:T(8,128)S(1)} %convolution_subtract_fusion.1, f32[256,2048]{1,0:T(8,128)S(1)} %fusion.62, f32[256,256]{1,0:T(8,128)S(1)} %fusion.69), kind=kOutput, calls=%fused_computation.9 | convolution fusion | flops 1611137024 | bytes 6553600 | tf_op jit(solution)/shard_map/dot_general | solution.py:95
  (141 shorter events, 51.5 us)
Async XLA Ops:
  7.2 199.4 %copy-start = (f32[256,256]{1,0:T(8,128)S(1)}, f32[256,256]{1,0:T(8,128)}, u32[]{:S(2)}) copy-start(f32[256,256]{1,0:T(8,128)} %param.9) | copy-start | bytes 786436
  7.2 185.7 %all-gather.3.cloned.1.call-start = ((), (), s32[]{:S(2)}) async-start(), calls=%async_computation | async-start | bytes 2228224 | tf_op jit(solution)/shard_map/all_gather | solution.py:179
  7.9 208.5 %all-gather.5.cloned.1.call-start = ((), (), s32[]{:S(2)}) async-start(), calls=%async_computation.1 | async-start | bytes 2228224 | tf_op jit(solution)/shard_map/all_gather | solution.py:177
  10.5 9.6 %copy-start.7 = (f32[16,2048]{1,0:T(8,128)S(1)}, f32[16,2048]{1,0:T(8,128)}, u32[]{:S(2)}) copy-start(f32[16,2048]{1,0:T(8,128)} %param.6) | copy-start | bytes 393220
  10.5 9.6 %copy-start.8 = (f32[16,2048]{1,0:T(8,128)S(1)}, f32[16,2048]{1,0:T(8,128)}, u32[]{:S(2)}) copy-start(f32[16,2048]{1,0:T(8,128)} %param.8) | copy-start | bytes 393220
  20.9 25.3 %copy-start.3 = (f32[2048,256]{1,0:T(8,128)S(1)}, f32[2048,256]{1,0:T(8,128)}, u32[]{:S(2)}) copy-start(f32[2048,256]{1,0:T(8,128)} %param.7) | copy-start | bytes 6291460
  27.2 9.8 %collective-permute-start = (f32[32,256]{0,1:T(8,128)S(1)}, f32[32,256]{0,1:T(8,128)S(1)}, u32[]{:S(2)}, u32[]{:S(2)}) collective-permute-start(f32[32,256]{0,1:T(8,128)S(1)} %fusion.19), channel_id=1, source_target_pairs={{0,16},{16,0},{32,48},{48,32},{64,80},{80,64},{96,112},{112,96},{1... | collective-permute-start | bytes 98312 | tf_op jit(solution)/shard_map/ppermute | solution.py:119
  37.1 10.6 %collective-permute-start.3 = (f32[32,256]{1,0:T(8,128)S(1)}, f32[32,256]{1,0:T(8,128)S(1)}, u32[]{:S(2)}, u32[]{:S(2)}) collective-permute-start(f32[32,256]{1,0:T(8,128)S(1)} %bitcast.149), channel_id=1, source_target_pairs={{0,96},{16,112},{32,64},{48,80},{64,32},{80,48},{96,0},{112,16},{1... | collective-permute-start | bytes 98312 | tf_op jit(solution)/shard_map/ppermute | solution.py:119
  39.0 8.7 %collective-permute-start.2 = (f32[32,256]{1,0:T(8,128)S(1)}, f32[32,256]{1,0:T(8,128)S(1)}, u32[]{:S(2)}, u32[]{:S(2)}) collective-permute-start(f32[32,256]{1,0:T(8,128)S(1)} %bitcast.150), channel_id=1, source_target_pairs={{0,64},{16,80},{32,96},{48,112},{64,0},{80,16},{96,32},{112,48},{1... | collective-permute-start | bytes 98312 | tf_op jit(solution)/shard_map/ppermute | solution.py:119
  40.9 6.8 %collective-permute-start.1 = (f32[32,256]{1,0:T(8,128)S(1)}, f32[32,256]{1,0:T(8,128)S(1)}, u32[]{:S(2)}, u32[]{:S(2)}) collective-permute-start(f32[32,256]{1,0:T(8,128)S(1)} %bitcast.151), channel_id=1, source_target_pairs={{0,32},{16,48},{32,0},{48,16},{64,96},{80,112},{96,64},{112,80},{1... | collective-permute-start | bytes 98312 | tf_op jit(solution)/shard_map/ppermute | solution.py:119
  47.8 9.0 %collective-permute-start.6 = (f32[32,256]{1,0:T(8,128)S(1)}, f32[32,256]{1,0:T(8,128)S(1)}, u32[]{:S(2)}, u32[]{:S(2)}) collective-permute-start(f32[32,256]{1,0:T(8,128)S(1)} %fusion.123), channel_id=1, source_target_pairs={{0,384},{16,400},{32,416},{48,432},{64,448},{80,464},{96,480},{112... | collective-permute-start | bytes 98312 | tf_op jit(solution)/shard_map/ppermute | solution.py:119
  49.7 7.1 %collective-permute-start.5 = (f32[32,256]{1,0:T(8,128)S(1)}, f32[32,256]{1,0:T(8,128)S(1)}, u32[]{:S(2)}, u32[]{:S(2)}) collective-permute-start(f32[32,256]{1,0:T(8,128)S(1)} %fusion.123), channel_id=1, source_target_pairs={{0,256},{16,272},{32,288},{48,304},{64,320},{80,336},{96,352},{112... | collective-permute-start | bytes 98312 | tf_op jit(solution)/shard_map/ppermute | solution.py:119
  51.7 7.0 %collective-permute-start.4 = (f32[32,256]{1,0:T(8,128)S(1)}, f32[32,256]{1,0:T(8,128)S(1)}, u32[]{:S(2)}, u32[]{:S(2)}) collective-permute-start(f32[32,256]{1,0:T(8,128)S(1)} %fusion.123), channel_id=1, source_target_pairs={{0,128},{16,144},{32,160},{48,176},{64,192},{80,208},{96,224},{112... | collective-permute-start | bytes 98312 | tf_op jit(solution)/shard_map/ppermute | solution.py:119
  58.7 9.3 %collective-permute-start.9 = (f32[1,32,256]{2,1,0:T(8,128)S(1)}, f32[1,32,256]{2,1,0:T(8,128)S(1)}, u32[]{:S(2)}, u32[]{:S(2)}) collective-permute-start(f32[1,32,256]{2,1,0:T(8,128)S(1)} %dynamic-slice_add_fusion.1), channel_id=1, source_target_pairs={{0,3},{1,2},{2,1},{3,0},{4,7},{5,6},{6,5},{7,4},{8,11},{9,10},{10,... | collective-permute-start | bytes 98312 | tf_op jit(solution)/shard_map/ppermute | solution.py:119
  61.5 7.0 %collective-permute-start.8 = (f32[1,32,256]{2,1,0:T(8,128)S(1)}, f32[1,32,256]{2,1,0:T(8,128)S(1)}, u32[]{:S(2)}, u32[]{:S(2)}) collective-permute-start(f32[1,32,256]{2,1,0:T(8,128)S(1)} %dynamic-slice_add_fusion.1), channel_id=1, source_target_pairs={{0,2},{1,3},{2,0},{3,1},{4,6},{5,7},{6,4},{7,5},{8,10},{9,11},{10,... | collective-permute-start | bytes 98312 | tf_op jit(solution)/shard_map/ppermute | solution.py:119
  63.4 6.2 %collective-permute-start.7 = (f32[1,32,256]{2,1,0:T(8,128)S(1)}, f32[1,32,256]{2,1,0:T(8,128)S(1)}, u32[]{:S(2)}, u32[]{:S(2)}) collective-permute-start(f32[1,32,256]{2,1,0:T(8,128)S(1)} %dynamic-slice_add_fusion.1), channel_id=1, source_target_pairs={{0,1},{1,0},{2,3},{3,2},{4,5},{5,4},{6,7},{7,6},{8,9},{9,8},{10,11... | collective-permute-start | bytes 98312 | tf_op jit(solution)/shard_map/ppermute | solution.py:119
  69.7 25.5 %collective-permute-start.12 = (f32[4,32,256]{2,1,0:T(8,128)S(1)}, f32[4,32,256]{2,1,0:T(8,128)S(1)}, u32[]{:S(2)}, u32[]{:S(2)}) collective-permute-start(f32[4,32,256]{2,1,0:T(8,128)S(1)} %get-tuple-element.31), channel_id=1, source_target_pairs={{0,12},{1,13},{2,14},{3,15},{4,8},{5,9},{6,10},{7,11},{8,4},{9,5},... | collective-permute-start | bytes 393224 | tf_op jit(solution)/shard_map/ppermute | solution.py:119
  79.5 19.5 %collective-permute-start.11 = (f32[4,32,256]{2,1,0:T(8,128)S(1)}, f32[4,32,256]{2,1,0:T(8,128)S(1)}, u32[]{:S(2)}, u32[]{:S(2)}) collective-permute-start(f32[4,32,256]{2,1,0:T(8,128)S(1)} %get-tuple-element.31), channel_id=1, source_target_pairs={{0,8},{1,9},{2,10},{3,11},{4,12},{5,13},{6,14},{7,15},{8,0},{9,1},... | collective-permute-start | bytes 393224 | tf_op jit(solution)/shard_map/ppermute | solution.py:119
  85.0 27.6 %collective-permute-start.10 = (f32[4,32,256]{2,1,0:T(8,128)S(1)}, f32[4,32,256]{2,1,0:T(8,128)S(1)}, u32[]{:S(2)}, u32[]{:S(2)}) collective-permute-start(f32[4,32,256]{2,1,0:T(8,128)S(1)} %get-tuple-element.31), channel_id=1, source_target_pairs={{0,4},{1,5},{2,6},{3,7},{4,0},{5,1},{6,2},{7,3},{8,12},{9,13},{10,... | collective-permute-start | bytes 393224 | tf_op jit(solution)/shard_map/ppermute | solution.py:119
  158.7 5.3 %collective-permute-start.13 = (f32[256,256]{0,1:T(8,128)S(1)}, f32[256,256]{0,1:T(8,128)S(1)}, u32[]{:S(2)}, u32[]{:S(2)}) collective-permute-start(f32[256,256]{0,1:T(8,128)S(1)} %select_select_fusion), channel_id=1, source_target_pairs={{0,16},{16,0},{32,48},{48,32},{64,80},{80,64},{96,112},{112,96},{1... | collective-permute-start | bytes 786440 | tf_op jit(solution)/shard_map/ppermute | solution.py:119
  164.1 16.6 %collective-permute-start.16 = (f32[256,256]{0,1:T(8,128)S(1)}, f32[256,256]{0,1:T(8,128)S(1)}, u32[]{:S(2)}, u32[]{:S(2)}) collective-permute-start(f32[256,256]{0,1:T(8,128)S(1)} %bitcast.141), channel_id=1, source_target_pairs={{0,96},{16,112},{32,64},{48,80},{64,32},{80,48},{96,0},{112,16},{1... | collective-permute-start | bytes 786440 | tf_op jit(solution)/shard_map/ppermute | solution.py:119
  167.8 13.0 %collective-permute-start.15 = (f32[256,256]{0,1:T(8,128)S(1)}, f32[256,256]{0,1:T(8,128)S(1)}, u32[]{:S(2)}, u32[]{:S(2)}) collective-permute-start(f32[256,256]{0,1:T(8,128)S(1)} %bitcast.142), channel_id=1, source_target_pairs={{0,64},{16,80},{32,96},{48,112},{64,0},{80,16},{96,32},{112,48},{1... | collective-permute-start | bytes 786440 | tf_op jit(solution)/shard_map/ppermute | solution.py:119
  170.7 12.3 %collective-permute-start.14 = (f32[256,256]{0,1:T(8,128)S(1)}, f32[256,256]{0,1:T(8,128)S(1)}, u32[]{:S(2)}, u32[]{:S(2)}) collective-permute-start(f32[256,256]{0,1:T(8,128)S(1)} %bitcast.143), channel_id=1, source_target_pairs={{0,32},{16,48},{32,0},{48,16},{64,96},{80,112},{96,64},{112,80},{1... | collective-permute-start | bytes 786440 | tf_op jit(solution)/shard_map/ppermute | solution.py:119
  183.8 18.3 %collective-permute-start.19 = (f32[256,256]{0,1:T(8,128)}, f32[256,256]{0,1:T(8,128)}, u32[]{:S(2)}, u32[]{:S(2)}) collective-permute-start(f32[256,256]{0,1:T(8,128)} %fusion.121), channel_id=1, source_target_pairs={{0,384},{16,400},{32,416},{48,432},{64,448},{80,464},{96,480},{112... | collective-permute-start | bytes 786440 | tf_op jit(solution)/shard_map/ppermute | solution.py:119
  187.9 14.2 %collective-permute-start.18 = (f32[256,256]{0,1:T(8,128)}, f32[256,256]{0,1:T(8,128)}, u32[]{:S(2)}, u32[]{:S(2)}) collective-permute-start(f32[256,256]{0,1:T(8,128)} %fusion.121), channel_id=1, source_target_pairs={{0,256},{16,272},{32,288},{48,304},{64,320},{80,336},{96,352},{112... | collective-permute-start | bytes 786440 | tf_op jit(solution)/shard_map/ppermute | solution.py:119
  189.8 12.3 %collective-permute-start.17 = (f32[256,256]{0,1:T(8,128)}, f32[256,256]{0,1:T(8,128)}, u32[]{:S(2)}, u32[]{:S(2)}) collective-permute-start(f32[256,256]{0,1:T(8,128)} %fusion.121), channel_id=1, source_target_pairs={{0,128},{16,144},{32,160},{48,176},{64,192},{80,208},{96,224},{112... | collective-permute-start | bytes 786440 | tf_op jit(solution)/shard_map/ppermute | solution.py:119
  198.2 5.1 %collective-permute-start.20 = (f32[16,256]{1,0:T(8,128)S(1)}, f32[16,256]{1,0:T(8,128)S(1)}, u32[]{:S(2)}, u32[]{:S(2)}) collective-permute-start(f32[16,256]{1,0:T(8,128)S(1)} %fusion.70), channel_id=1, source_target_pairs={{0,16},{16,0},{32,48},{48,32},{64,80},{80,64},{96,112},{112,96},{1... | collective-permute-start | bytes 49160 | tf_op jit(solution)/shard_map/ppermute | solution.py:12
  203.4 4.5 %collective-permute-start.21 = (f32[16,256]{1,0:T(8,128)S(1)}, f32[16,256]{1,0:T(8,128)S(1)}, u32[]{:S(2)}, u32[]{:S(2)}) collective-permute-start(f32[16,256]{1,0:T(8,128)S(1)} %add.606), channel_id=1, source_target_pairs={{0,32},{16,48},{32,0},{48,16},{64,96},{80,112},{96,64},{112,80},{1... | collective-permute-start | bytes 49160 | tf_op jit(solution)/shard_map/ppermute | solution.py:12
  207.9 6.0 %collective-permute-start.22 = (f32[16,256]{1,0:T(8,128)S(1)}, f32[16,256]{1,0:T(8,128)S(1)}, u32[]{:S(2)}, u32[]{:S(2)}) collective-permute-start(f32[16,256]{1,0:T(8,128)S(1)} %add.607), channel_id=1, source_target_pairs={{0,64},{16,80},{32,96},{48,112},{64,0},{80,16},{96,32},{112,48},{1... | collective-permute-start | bytes 49160 | tf_op jit(solution)/shard_map/ppermute | solution.py:12
  212.9 14.1 %copy-start.5 = (f32[256,256]{1,0:T(8,128)}, f32[256,256]{1,0:T(8,128)S(1)}, u32[]{:S(2)}) copy-start(f32[256,256]{1,0:T(8,128)S(1)} %fusion.69) | copy-start | bytes 786436
  213.8 8.3 %collective-permute-start.23 = (f32[16,256]{1,0:T(8,128)S(1)}, f32[16,256]{1,0:T(8,128)S(1)}, u32[]{:S(2)}, u32[]{:S(2)}) collective-permute-start(f32[16,256]{1,0:T(8,128)S(1)} %add.608), channel_id=1, source_target_pairs={{0,128},{16,144},{32,160},{48,176},{64,192},{80,208},{96,224},{112... | collective-permute-start | bytes 49160 | tf_op jit(solution)/shard_map/ppermute | solution.py:12
  222.2 9.7 %collective-permute-start.24 = (f32[16,256]{1,0:T(8,128)S(1)}, f32[16,256]{1,0:T(8,128)S(1)}, u32[]{:S(2)}, u32[]{:S(2)}) collective-permute-start(f32[16,256]{1,0:T(8,128)S(1)} %add.609), channel_id=1, source_target_pairs={{0,256},{16,272},{32,288},{48,304},{64,320},{80,336},{96,352},{112... | collective-permute-start | bytes 49160 | tf_op jit(solution)/shard_map/ppermute | solution.py:12
  (7 other events, 30.4 us)
Sparse Core Ops, SparseCore 0:
  10.1 69.9 all-gather.2
  82.1 86.7 all-gather.4

commit v5 on v2

--- a/solution.py
+++ b/solution.py
@@ -53,7 +53,7 @@
 def elimination_kernel(matrix_ref, reduced_ref):
     order = matrix_ref.shape[0]
     reduced_ref[...] = matrix_ref[...]
-    phase = 32
+    phase = 64
     for first_row in range(0, order - 1, phase):
         first_col = (first_row // 128) * 128
         height = order - first_row
@@ -120,14 +120,13 @@
     leaf_group, leaf_slot = trace_pivots(merge_picks, row_devices)
     owner_mask = leaf_group == own_row
     local_rows = jnp.take(leaf_picks[0], leaf_slot)
+    own_columns = jnp.take(jnp.concatenate([panel_t, prev_lower_t], 0), local_rows, axis=1)
+    pivot_part = butterfly_sum(jnp.where(owner_mask[None, :], own_columns, 0.0), "rows")
+    pivot_columns = lax.all_gather(pivot_part, "cols", axis=0, tiled=False)
     own_trailing = jnp.take(trailing, local_rows, axis=0)
-    own_columns = jnp.take(jnp.concatenate([panel_t, prev_lower_t], 0), local_rows, axis=1)
-    own_pivots = jnp.concatenate([own_trailing, own_columns.T], 1)
-    pivot_data = butterfly_sum(jnp.where(owner_mask[:, None], own_pivots, 0.0), "rows")
-    pivot_trailing = pivot_data[:, : own_trailing.shape[1]]
-    pivot_columns = lax.all_gather(
-        pivot_data[:, own_trailing.shape[1] :].T, "cols", axis=0, tiled=False
-    )
+    own_trailing = jnp.where(owner_mask[:, None], own_trailing, 0.0)
+    own_trailing, pivot_columns = lax.optimization_barrier((own_trailing, pivot_columns))
+    pivot_trailing = butterfly_sum(own_trailing, "rows")
     block_t = pivot_columns[:, :slab_rows].reshape(order, order)
     prev_pivots = pivot_columns[:, slab_rows:].reshape(order, order)
     middle_pivots = pivot_trailing - contract_first(prev_pivots, prev_upper)
@@ -135,14 +134,16 @@
         lax.all_gather(prev_lower_t, "cols", axis=0, tiled=True), prev_upper
     )
     panel_full = lax.all_gather(panel_t, "cols", axis=0, tiled=True)
+    panel_gram = butterfly_sum(contract_second(panel_full, panel_full), "rows")
     lower_left, upper_left = factor(block_t.T)
     inverse = upper_inverse(upper_left)
     upper_right = product(unit_lower_inverse(lower_left), middle_pivots)
     lower_full = jnp.dot(inverse.T, panel_full, precision=full_precision)
     lower_tile = lax.dynamic_slice_in_dim(lower_full, own_column * slab_rows, slab_rows, 0)
     updated = middle - contract_first(lower_full, upper_right)
-    gram_rows = contract_second(lower_tile, lower_full)
-    gram = butterfly_sum(gram_rows, "rows") / (rows_here * row_devices)
+    inverse_tile = lax.dynamic_slice_in_dim(inverse, own_column * slab_rows, slab_rows, 1)
+    gram_rows = contract_first(inverse_tile, product(panel_gram, inverse))
+    gram = gram_rows / (rows_here * row_devices)
     return (lower_tile, upper_left, upper_right, updated, gram)
 
 

time: 219 us -> 236 us (1.078)
  starting transfers between devices: 45.9 us -> 58.2 us
  blocking collectives: 26.8 us -> 29.3 us
    ppermute x10 -> x15, starting transfers between devices: 45.8 us -> 58.1 us  [from_partner(): lax.ppermute(shard, axis, [(i, i ^ 1 << apart) for i in range(lax.axis_si...]
    all_gather x1, blocking collectives: 26.8 us -> 29.3 us  [body(): pivot_columns = lax.all_gather(pivot_part, 'cols', axis=0, tiled=False)]
    dot_general x3 -> x4, matrix products: 11.3 us -> 12.3 us  [contract_first(): lax.dot_general(left_side, right_side, (((0,), (0,)), ((), ())), precisio...]
    dot_general x29 -> x30, matrix products: 12.3 us -> 11.8 us  [product(): return jnp.dot(left_side, right_side, precision=full_precision)]
    ppermute x10 -> x15, waiting for transfers between devices: 41.1 us -> 40.9 us  [from_partner(): lax.ppermute(shard, axis, [(i, i ^ 1 << apart) for i in range(lax.axis_si...]
  transfers between devices with their start and end apart: 12 -> 17, of which waited for: 7 -> 10; matrix products, arithmetic and copies ran while one was open for 25% -> 23% of each run, Pallas kernels for 15% -> 14%
where the time goes in v5:
time: 236 us; the launch traced here: 234 us
  starting transfers between devices  58.2 us (25%)
  waiting for transfers between devices  41.7 us (18%)
  Pallas kernels  33.5 us (14%)
  matrix products  30.1 us (13%)
  blocking collectives  29.3 us (12%)
  local copies, waits for them, and re-layouts  23.8 us (10%)
  between operations  14.9 us (6%)
    ppermute x15, starting transfers between devices, from_partner(): lax.ppermute(shard, axis, [(i, i ^ 1 << apart) for i in range(lax.axis_si...  58.1 us
    ppermute x15, waiting for transfers between devices, from_partner(): lax.ppermute(shard, axis, [(i, i ^ 1 << apart) for i in range(lax.axis_si...  40.9 us
    pallas_call x1, Pallas kernels, factor(): pl.pallas_call(elimination_kernel, out_shape=jax.ShapeDtypeStruct(matrix....  33.5 us
    all_gather x1, blocking collectives, body(): pivot_columns = lax.all_gather(pivot_part, 'cols', axis=0, tiled=False)  29.3 us
    dot_general x4, matrix products, contract_first(): lax.dot_general(left_side, right_side, (((0,), (0,)), ((), ())), precisio...  12.3 us
    gather x5, local copies, waits for them, and re-layouts, trace_pivots(): position = merge_picks[offset_rows + leaf_group, leaf_slot]  12 us
    dot_general x30, matrix products, product(): return jnp.dot(left_side, right_side, precision=full_precision)  11.8 us
  transfers between devices with their start and end apart: 17, of which 10 were waited for; matrix products, arithmetic and copies ran while one was open for 23% of the time, Pallas kernels for 14%

profile of v5, /device:TPU:1, one launch (start us, length us, event | category | flops | bytes accessed | tf_op | source)
XLA Modules:
  0.0 233.7 jit_solution(16536229534072184138)
XLA Ops:
  8.0 2.5 %gather_fusion = s32[256]{0:T(256)S(1)} fusion(s32[31,256]{1,0:T(8,128)} %param.11, s32[256]{0:T(256)} %constant.187), kind=kCustom, calls=%fused_computation | custom fusion | bytes 4096 | tf_op jit(solution)/shard_map/gather | solution.py:22
  10.5 2.4 %gather_fusion.1 = s32[256]{0:T(256)S(1)} fusion(s32[31,256]{1,0:T(8,128)} %param.11, s32[256]{0:T(256)S(1)} %bitcast.82), kind=kCustom, calls=%fused_computation.1 | custom fusion | bytes 4096 | tf_op jit(solution)/shard_map/gather | solution.py:22
  13.0 2.3 %gather_fusion.2 = s32[256]{0:T(256)S(1)} fusion(s32[31,256]{1,0:T(8,128)S(1)} %copy-done.2, s32[256]{0:T(256)S(1)} %bitcast.80), kind=kCustom, calls=%fused_computation.2 | custom fusion | bytes 4096 | tf_op jit(solution)/shard_map/gather | solution.py:22
  15.4 2.3 %gather_fusion.3 = s32[256]{0:T(256)S(1)} fusion(s32[31,256]{1,0:T(8,128)S(1)} %copy-done.2, s32[256]{0:T(256)S(1)} %bitcast.83), kind=kCustom, calls=%fused_computation.3 | custom fusion | bytes 4096 | tf_op jit(solution)/shard_map/gather | solution.py:22
  17.8 2.3 %gather_fusion.4 = s32[256]{0:T(256)S(1)} fusion(s32[31,256]{1,0:T(8,128)S(1)} %copy-done.2, s32[256]{0:T(256)S(1)} %bitcast.81), kind=kCustom, calls=%fused_computation.4 | custom fusion | bytes 4096 | tf_op jit(solution)/shard_map/gather | solution.py:22
  22.2 1.9 gather_fusion.5
  26.3 8.8 %collective-permute-start = (f32[32,256]{0,1:T(8,128)S(1)}, f32[32,256]{0,1:T(8,128)S(1)}, u32[]{:S(2)}, u32[]{:S(2)}) collective-permute-start(f32[32,256]{0,1:T(8,128)S(1)} %select_bitcast_fusion), channel_id=1, source_target_pairs={{0,16},{16,0},{32,48},{48,32},{64,80},{80,64},{96,112},{112,96},{1... | collective-permute-start | bytes 98312 | tf_op jit(solution)/shard_map/ppermute | solution.py:12
  36.6 1.9 collective-permute-start.1
  38.6 5.1 %collective-permute-done.1 = f32[32,256]{0,1:T(8,128)S(1)} collective-permute-done((f32[32,256]{0,1:T(8,128)S(1)}, f32[32,256]{0,1:T(8,128)S(1)}, u32[]{:S(2)}, u32[]{:S(2)}) %collective-permute-start.1) | collective-permute-done | bytes 32800 | tf_op jit(solution)/shard_map/ppermute | solution.py:12
  45.7 5.8 %collective-permute-done.2 = f32[32,256]{0,1:T(8,128)S(1)} collective-permute-done((f32[32,256]{0,1:T(8,128)S(1)}, f32[32,256]{0,1:T(8,128)S(1)}, u32[]{:S(2)}, u32[]{:S(2)}) %collective-permute-start.2) | collective-permute-done | bytes 32800 | tf_op jit(solution)/shard_map/ppermute | solution.py:12
  53.5 3.7 %collective-permute-done.3 = f32[32,256]{0,1:T(8,128)S(1)} collective-permute-done((f32[32,256]{0,1:T(8,128)S(1)}, f32[32,256]{0,1:T(8,128)S(1)}, u32[]{:S(2)}, u32[]{:S(2)}) %collective-permute-start.3) | collective-permute-done | bytes 32800 | tf_op jit(solution)/shard_map/ppermute | solution.py:12
  59.3 5.1 %collective-permute-done.4 = f32[32,256]{0,1:T(8,128)S(1)} collective-permute-done((f32[32,256]{0,1:T(8,128)S(1)}, f32[32,256]{0,1:T(8,128)S(1)}, u32[]{:S(2)}, u32[]{:S(2)}) %collective-permute-start.4) | collective-permute-done | bytes 32800 | tf_op jit(solution)/shard_map/ppermute | solution.py:12
  64.5 29.3 %all-gather = f32[512,256]{1,0:T(8,128)S(1)} all-gather(f32[32,256]{1,0:T(8,128)S(1)} %copy.29), channel_id=2, replica_groups=mesh['rows'=32,'cols'=16] {'cols'}, dimensions={0}, use_global_device_ids=true | all-gather | bytes 557056 | tf_op jit(solution)/shard_map/all_gather | solution.py:125
  94.6 33.5 %shard_map.101 = f32[256,256]{1,0:T(8,128)} custom-call(f32[256,256]{1,0:T(8,128)} %bitcast.87), custom_call_target="tpu_custom_call" | custom-call | tf_op jit(solution)/shard_map/pallas_call | solution.py:86
  129.3 2.4 %gather_fusion.8 = f32[256]{0:T(256)S(1)} fusion(f32[256,256]{0,1:T(8,128)S(1)} %broadcast_select_fusion, s32[256]{0:T(256)S(1)} %bitcast.84), kind=kCustom, calls=%fused_computation.8 | custom fusion | bytes 4096 | tf_op jit(solution)/shard_map/jit(diagonal)/cond/branch_0_fun/gather | solution.py:47
  137.8 10.2 %collective-permute-start.5 = (f32[256,256]{0,1:T(8,128)S(1)}, f32[256,256]{0,1:T(8,128)S(1)}, u32[]{:S(2)}, u32[]{:S(2)}) collective-permute-start(f32[256,256]{0,1:T(8,128)S(1)} %select_select_fusion), channel_id=1, source_target_pairs={{0,16},{16,0},{32,48},{48,32},{64,80},{80,64},{96,112},{112,96},{1... | collective-permute-start | bytes 786440 | tf_op jit(solution)/shard_map/ppermute | solution.py:12
  150.8 3.0 %collective-permute-start.6 = (f32[256,256]{0,1:T(8,128)S(1)}, f32[256,256]{0,1:T(8,128)S(1)}, u32[]{:S(2)}, u32[]{:S(2)}) collective-permute-start(f32[256,256]{0,1:T(8,128)S(1)} %add.434), channel_id=1, source_target_pairs={{0,32},{16,48},{32,0},{48,16},{64,96},{80,112},{96,64},{112,80},{1... | collective-permute-start | bytes 786440 | tf_op jit(solution)/shard_map/ppermute | solution.py:12
  154.6 6.0 %collective-permute-done.6 = f32[256,256]{0,1:T(8,128)S(1)} collective-permute-done((f32[256,256]{0,1:T(8,128)S(1)}, f32[256,256]{0,1:T(8,128)S(1)}, u32[]{:S(2)}, u32[]{:S(2)}) %collective-permute-start.6) | collective-permute-done | bytes 262176 | tf_op jit(solution)/shard_map/ppermute | solution.py:12
  160.6 4.5 %collective-permute-start.7 = (f32[256,256]{0,1:T(8,128)S(1)}, f32[256,256]{0,1:T(8,128)S(1)}, u32[]{:S(2)}, u32[]{:S(2)}) collective-permute-start(f32[256,256]{0,1:T(8,128)S(1)} %add.435), channel_id=1, source_target_pairs={{0,64},{16,80},{32,96},{48,112},{64,0},{80,16},{96,32},{112,48},{1... | collective-permute-start | bytes 786440 | tf_op jit(solution)/shard_map/ppermute | solution.py:12
  166.0 5.1 %collective-permute-done.7 = f32[256,256]{0,1:T(8,128)S(1)} collective-permute-done((f32[256,256]{0,1:T(8,128)S(1)}, f32[256,256]{0,1:T(8,128)S(1)}, u32[]{:S(2)}, u32[]{:S(2)}) %collective-permute-start.7) | collective-permute-done | bytes 262176 | tf_op jit(solution)/shard_map/ppermute | solution.py:12
  171.1 3.8 %collective-permute-start.8 = (f32[256,256]{0,1:T(8,128)S(1)}, f32[256,256]{0,1:T(8,128)S(1)}, u32[]{:S(2)}, u32[]{:S(2)}) collective-permute-start(f32[256,256]{0,1:T(8,128)S(1)} %add.436), channel_id=1, source_target_pairs={{0,128},{16,144},{32,160},{48,176},{64,192},{80,208},{96,224},{112... | collective-permute-start | bytes 786440 | tf_op jit(solution)/shard_map/ppermute | solution.py:12
  174.9 4.1 %fusion.68 = f32[256,256]{1,0:T(8,128)S(1)} fusion(f32[256,2048]{1,0:T(8,128)} %all-gather.4.cloned.1.call-done), kind=kOutput, calls=%fused_computation.138 | convolution fusion | flops 1610612736 | bytes 2359296 | tf_op jit(solution)/shard_map/dot_general | solution.py:101
  179.0 3.7 %collective-permute-start.10 = (f32[256,256]{1,0:T(8,128)S(1)}, f32[256,256]{1,0:T(8,128)S(1)}, u32[]{:S(2)}, u32[]{:S(2)}) collective-permute-start(f32[256,256]{1,0:T(8,128)S(1)} %fusion.68), channel_id=1, source_target_pairs={{0,16},{16,0},{32,48},{48,32},{64,80},{80,64},{96,112},{112,96},{1... | collective-permute-start | bytes 786440 | tf_op jit(solution)/shard_map/ppermute | solution.py:12
  183.1 4.6 %collective-permute-start.9 = (f32[256,256]{0,1:T(8,128)S(1)}, f32[256,256]{0,1:T(8,128)S(1)}, u32[]{:S(2)}, u32[]{:S(2)}) collective-permute-start(f32[256,256]{0,1:T(8,128)S(1)} %add.437), channel_id=1, source_target_pairs={{0,256},{16,272},{32,288},{48,304},{64,320},{80,336},{96,352},{112... | collective-permute-start | bytes 786440 | tf_op jit(solution)/shard_map/ppermute | solution.py:12
  188.1 2.6 %collective-permute-start.11 = (f32[256,256]{1,0:T(8,128)S(1)}, f32[256,256]{1,0:T(8,128)S(1)}, u32[]{:S(2)}, u32[]{:S(2)}) collective-permute-start(f32[256,256]{1,0:T(8,128)S(1)} %add.439), channel_id=1, source_target_pairs={{0,32},{16,48},{32,0},{48,16},{64,96},{80,112},{96,64},{112,80},{1... | collective-permute-start | bytes 786440 | tf_op jit(solution)/shard_map/ppermute | solution.py:12
  192.2 2.2 collective-permute-done.9
  194.9 2.8 %collective-permute-done.11 = f32[256,256]{1,0:T(8,128)S(1)} collective-permute-done((f32[256,256]{1,0:T(8,128)S(1)}, f32[256,256]{1,0:T(8,128)S(1)}, u32[]{:S(2)}, u32[]{:S(2)}) %collective-permute-start.11) | collective-permute-done | bytes 262176 | tf_op jit(solution)/shard_map/ppermute | solution.py:12
  197.7 5.0 %collective-permute-start.12 = (f32[256,256]{1,0:T(8,128)S(1)}, f32[256,256]{1,0:T(8,128)S(1)}, u32[]{:S(2)}, u32[]{:S(2)}) collective-permute-start(f32[256,256]{1,0:T(8,128)S(1)} %add.440), channel_id=1, source_target_pairs={{0,64},{16,80},{32,96},{48,112},{64,0},{80,16},{96,32},{112,48},{1... | collective-permute-start | bytes 786440 | tf_op jit(solution)/shard_map/ppermute | solution.py:12
  202.7 5.9 %convolution_subtract_fusion.1 = f32[2048,256]{1,0:T(8,128)S(1)} fusion(f32[2048,256]{1,0:T(8,128)} %param.7, f32[256,2048]{1,0:T(8,128)} %all-gather.6.cloned.1.call-done, f32[256,256]{1,0:T(8,128)S(1)} %copy-done), kind=kOutput, calls=%fused_computation.10 | convolution fusion | flops 1611137024 | bytes 6553600 | tf_op jit(solution)/shard_map/dot_general | solution.py:95
  212.5 4.4 %collective-permute-done.13 = f32[256,256]{1,0:T(8,128)S(1)} collective-permute-done((f32[256,256]{1,0:T(8,128)S(1)}, f32[256,256]{1,0:T(8,128)S(1)}, u32[]{:S(2)}, u32[]{:S(2)}) %collective-permute-start.13) | collective-permute-done | bytes 262176 | tf_op jit(solution)/shard_map/ppermute | solution.py:12
  217.0 2.4 %collective-permute-start.14 = (f32[256,256]{1,0:T(8,128)S(1)}, f32[256,256]{1,0:T(8,128)S(1)}, u32[]{:S(2)}, u32[]{:S(2)}) collective-permute-start(f32[256,256]{1,0:T(8,128)S(1)} %add.442), channel_id=1, source_target_pairs={{0,256},{16,272},{32,288},{48,304},{64,320},{80,336},{96,352},{112... | collective-permute-start | bytes 786440 | tf_op jit(solution)/shard_map/ppermute | solution.py:12
  219.4 5.0 %convolution_subtract_fusion = f32[2048,256]{1,0:T(8,128)} fusion(f32[2048,256]{1,0:T(8,128)S(1)} %convolution_subtract_fusion.1, f32[256,2048]{1,0:T(8,128)S(1)} %fusion.60, f32[256,256]{1,0:T(8,128)S(1)} %fusion.14), kind=kOutput, calls=%fused_computation.9 | convolution fusion | flops 1611137024 | bytes 6553600 | tf_op jit(solution)/shard_map/dot_general | solution.py:95
  (115 shorter events, 34.1 us)
Async XLA Ops:
  7.2 183.6 %copy-start = (f32[256,256]{1,0:T(8,128)S(1)}, f32[256,256]{1,0:T(8,128)}, u32[]{:S(2)}) copy-start(f32[256,256]{1,0:T(8,128)} %param.9) | copy-start | bytes 786436
  7.2 5.8 %copy-start.2 = (s32[31,256]{1,0:T(8,128)S(1)}, s32[31,256]{1,0:T(8,128)}, u32[]{:S(2)}) copy-start(s32[31,256]{1,0:T(8,128)} %param.11) | copy-start | bytes 95236
  7.2 167.7 %all-gather.4.cloned.1.call-start = ((), (), s32[]{:S(2)}) async-start(), calls=%async_computation | async-start | bytes 2228224 | tf_op jit(solution)/shard_map/all_gather | solution.py:136
  7.9 194.8 %all-gather.6.cloned.1.call-start = ((), (), s32[]{:S(2)}) async-start(), calls=%async_computation.1 | async-start | bytes 2228224 | tf_op jit(solution)/shard_map/all_gather | solution.py:134
  10.5 9.6 %copy-start.7 = (f32[16,2048]{1,0:T(8,128)S(1)}, f32[16,2048]{1,0:T(8,128)}, u32[]{:S(2)}) copy-start(f32[16,2048]{1,0:T(8,128)} %param.6) | copy-start | bytes 393220
  10.5 9.6 %copy-start.8 = (f32[16,2048]{1,0:T(8,128)S(1)}, f32[16,2048]{1,0:T(8,128)}, u32[]{:S(2)}) copy-start(f32[16,2048]{1,0:T(8,128)} %param.8) | copy-start | bytes 393220
  15.3 4.8 %copy-start.9 = (s32[256]{0:T(256)}, s32[256]{0:T(256)S(1)}, u32[]{:S(2)}) copy-start(s32[256]{0:T(256)S(1)} %gather_fusion.2) | copy-start | bytes 3076
  15.4 6.8 %copy-start.1 = (s32[1,256]{1,0:T(1,128)S(1)}, s32[1,256]{1,0:T(1,128)}, u32[]{:S(2)}) copy-start(s32[1,256]{1,0:T(1,128)} %param.10) | copy-start | bytes 3076
  17.7 2.4 %copy-start.11 = (s32[256]{0:T(256)}, s32[256]{0:T(256)S(1)}, u32[]{:S(2)}) copy-start(s32[256]{0:T(256)S(1)} %gather_fusion.3) | copy-start | bytes 3076
  20.1 15.1 %copy-start.4 = (f32[2048,256]{1,0:T(8,128)S(1)}, f32[2048,256]{1,0:T(8,128)}, u32[]{:S(2)}) copy-start(f32[2048,256]{1,0:T(8,128)} %param.7) | copy-start | bytes 6291460
  24.2 0.6 copy-start.12
  24.7 10.4 %copy-start.10 = (s32[1024]{0:T(1024)}, s32[1024]{0:T(1024)S(1)}, u32[]{:S(2)}) copy-start(s32[1024]{0:T(1024)S(1)} %pad_clamp_fusion) | copy-start | bytes 12292
  26.3 10.1 %collective-permute-start = (f32[32,256]{0,1:T(8,128)S(1)}, f32[32,256]{0,1:T(8,128)S(1)}, u32[]{:S(2)}, u32[]{:S(2)}) collective-permute-start(f32[32,256]{0,1:T(8,128)S(1)} %select_bitcast_fusion), channel_id=1, source_target_pairs={{0,16},{16,0},{32,48},{48,32},{64,80},{80,64},{96,112},{112,96},{1... | collective-permute-start | bytes 98312 | tf_op jit(solution)/shard_map/ppermute | solution.py:12
  36.6 7.1 %collective-permute-start.1 = (f32[32,256]{0,1:T(8,128)S(1)}, f32[32,256]{0,1:T(8,128)S(1)}, u32[]{:S(2)}, u32[]{:S(2)}) collective-permute-start(f32[32,256]{0,1:T(8,128)S(1)} %fusion.120), channel_id=1, source_target_pairs={{0,32},{16,48},{32,0},{48,16},{64,96},{80,112},{96,64},{112,80},{1... | collective-permute-start | bytes 98312 | tf_op jit(solution)/shard_map/ppermute | solution.py:12
  43.7 7.7 %collective-permute-start.2 = (f32[32,256]{0,1:T(8,128)S(1)}, f32[32,256]{0,1:T(8,128)S(1)}, u32[]{:S(2)}, u32[]{:S(2)}) collective-permute-start(f32[32,256]{0,1:T(8,128)S(1)} %add.412), channel_id=1, source_target_pairs={{0,64},{16,80},{32,96},{48,112},{64,0},{80,16},{96,32},{112,48},{1... | collective-permute-start | bytes 98312 | tf_op jit(solution)/shard_map/ppermute | solution.py:12
  51.5 5.7 %collective-permute-start.3 = (f32[32,256]{0,1:T(8,128)S(1)}, f32[32,256]{0,1:T(8,128)S(1)}, u32[]{:S(2)}, u32[]{:S(2)}) collective-permute-start(f32[32,256]{0,1:T(8,128)S(1)} %add.413), channel_id=1, source_target_pairs={{0,128},{16,144},{32,160},{48,176},{64,192},{80,208},{96,224},{112... | collective-permute-start | bytes 98312 | tf_op jit(solution)/shard_map/ppermute | solution.py:12
  57.2 7.2 %collective-permute-start.4 = (f32[32,256]{0,1:T(8,128)S(1)}, f32[32,256]{0,1:T(8,128)S(1)}, u32[]{:S(2)}, u32[]{:S(2)}) collective-permute-start(f32[32,256]{0,1:T(8,128)S(1)} %add.414), channel_id=1, source_target_pairs={{0,256},{16,272},{32,288},{48,304},{64,320},{80,336},{96,352},{112... | collective-permute-start | bytes 98312 | tf_op jit(solution)/shard_map/ppermute | solution.py:12
  129.3 3.6 %copy-start.5 = (f32[256,256]{1,0:T(8,128)S(1)}, f32[256,256]{1,0:T(8,128)}, u32[]{:S(2)}) copy-start(f32[256,256]{1,0:T(8,128)} %shard_map.101) | copy-start | bytes 786436
  137.8 13.0 %collective-permute-start.5 = (f32[256,256]{0,1:T(8,128)S(1)}, f32[256,256]{0,1:T(8,128)S(1)}, u32[]{:S(2)}, u32[]{:S(2)}) collective-permute-start(f32[256,256]{0,1:T(8,128)S(1)} %select_select_fusion), channel_id=1, source_target_pairs={{0,16},{16,0},{32,48},{48,32},{64,80},{80,64},{96,112},{112,96},{1... | collective-permute-start | bytes 786440 | tf_op jit(solution)/shard_map/ppermute | solution.py:12
  150.8 9.8 %collective-permute-start.6 = (f32[256,256]{0,1:T(8,128)S(1)}, f32[256,256]{0,1:T(8,128)S(1)}, u32[]{:S(2)}, u32[]{:S(2)}) collective-permute-start(f32[256,256]{0,1:T(8,128)S(1)} %add.434), channel_id=1, source_target_pairs={{0,32},{16,48},{32,0},{48,16},{64,96},{80,112},{96,64},{112,80},{1... | collective-permute-start | bytes 786440 | tf_op jit(solution)/shard_map/ppermute | solution.py:12
  160.6 10.4 %collective-permute-start.7 = (f32[256,256]{0,1:T(8,128)S(1)}, f32[256,256]{0,1:T(8,128)S(1)}, u32[]{:S(2)}, u32[]{:S(2)}) collective-permute-start(f32[256,256]{0,1:T(8,128)S(1)} %add.435), channel_id=1, source_target_pairs={{0,64},{16,80},{32,96},{48,112},{64,0},{80,16},{96,32},{112,48},{1... | collective-permute-start | bytes 786440 | tf_op jit(solution)/shard_map/ppermute | solution.py:12
  171.1 12.0 %collective-permute-start.8 = (f32[256,256]{0,1:T(8,128)S(1)}, f32[256,256]{0,1:T(8,128)S(1)}, u32[]{:S(2)}, u32[]{:S(2)}) collective-permute-start(f32[256,256]{0,1:T(8,128)S(1)} %add.436), channel_id=1, source_target_pairs={{0,128},{16,144},{32,160},{48,176},{64,192},{80,208},{96,224},{112... | collective-permute-start | bytes 786440 | tf_op jit(solution)/shard_map/ppermute | solution.py:12
  179.0 9.1 %collective-permute-start.10 = (f32[256,256]{1,0:T(8,128)S(1)}, f32[256,256]{1,0:T(8,128)S(1)}, u32[]{:S(2)}, u32[]{:S(2)}) collective-permute-start(f32[256,256]{1,0:T(8,128)S(1)} %fusion.68), channel_id=1, source_target_pairs={{0,16},{16,0},{32,48},{48,32},{64,80},{80,64},{96,112},{112,96},{1... | collective-permute-start | bytes 786440 | tf_op jit(solution)/shard_map/ppermute | solution.py:12
  183.1 11.3 %collective-permute-start.9 = (f32[256,256]{0,1:T(8,128)S(1)}, f32[256,256]{0,1:T(8,128)S(1)}, u32[]{:S(2)}, u32[]{:S(2)}) collective-permute-start(f32[256,256]{0,1:T(8,128)S(1)} %add.437), channel_id=1, source_target_pairs={{0,256},{16,272},{32,288},{48,304},{64,320},{80,336},{96,352},{112... | collective-permute-start | bytes 786440 | tf_op jit(solution)/shard_map/ppermute | solution.py:12
  188.1 9.5 %collective-permute-start.11 = (f32[256,256]{1,0:T(8,128)S(1)}, f32[256,256]{1,0:T(8,128)S(1)}, u32[]{:S(2)}, u32[]{:S(2)}) collective-permute-start(f32[256,256]{1,0:T(8,128)S(1)} %add.439), channel_id=1, source_target_pairs={{0,32},{16,48},{32,0},{48,16},{64,96},{80,112},{96,64},{112,80},{1... | collective-permute-start | bytes 786440 | tf_op jit(solution)/shard_map/ppermute | solution.py:12
  194.9 24.5 %copy-start.6 = (f32[256,256]{1,0:T(8,128)}, f32[256,256]{1,0:T(8,128)S(1)}, u32[]{:S(2)}) copy-start(f32[256,256]{1,0:T(8,128)S(1)} %fusion.14) | copy-start | bytes 786436
  197.7 12.9 %copy-start.3 = (f32[256,2048]{1,0:T(8,128)S(1)}, f32[256,2048]{1,0:T(8,128)}, u32[]{:S(2)}) copy-start(f32[256,2048]{1,0:T(8,128)} %all-gather.4.cloned.1.call-done) | copy-start | bytes 6291460
  197.7 10.9 %collective-permute-start.12 = (f32[256,256]{1,0:T(8,128)S(1)}, f32[256,256]{1,0:T(8,128)S(1)}, u32[]{:S(2)}, u32[]{:S(2)}) collective-permute-start(f32[256,256]{1,0:T(8,128)S(1)} %add.440), channel_id=1, source_target_pairs={{0,64},{16,80},{32,96},{48,112},{64,0},{80,16},{96,32},{112,48},{1... | collective-permute-start | bytes 786440 | tf_op jit(solution)/shard_map/ppermute | solution.py:12
  208.6 8.3 %collective-permute-start.13 = (f32[256,256]{1,0:T(8,128)S(1)}, f32[256,256]{1,0:T(8,128)S(1)}, u32[]{:S(2)}, u32[]{:S(2)}) collective-permute-start(f32[256,256]{1,0:T(8,128)S(1)} %add.441), channel_id=1, source_target_pairs={{0,128},{16,144},{32,160},{48,176},{64,192},{80,208},{96,224},{112... | collective-permute-start | bytes 786440 | tf_op jit(solution)/shard_map/ppermute | solution.py:12
  217.0 8.6 %collective-permute-start.14 = (f32[256,256]{1,0:T(8,128)S(1)}, f32[256,256]{1,0:T(8,128)S(1)}, u32[]{:S(2)}, u32[]{:S(2)}) collective-permute-start(f32[256,256]{1,0:T(8,128)S(1)} %add.442), channel_id=1, source_target_pairs={{0,256},{16,272},{32,288},{48,304},{64,320},{80,336},{96,352},{112... | collective-permute-start | bytes 786440 | tf_op jit(solution)/shard_map/ppermute | solution.py:12
Sparse Core Ops, SparseCore 0:
  10.1 70.0 all-gather.3
  82.3 69.7 all-gather.5

commit v6 on v2

--- a/solution.py
+++ b/solution.py
@@ -12,6 +12,15 @@
     return lax.ppermute(shard, axis, [(i, i ^ 1 << apart) for i in range(lax.axis_size(axis))])
 
 
+def lookup(table, group, slot):
+    width = table.shape[1]
+    slot_hit = slot[:, None] == lax.broadcasted_iota(jnp.int32, (slot.shape[0], width), 1)
+    chosen = jnp.zeros((slot.shape[0], width), table.dtype)
+    for index in range(table.shape[0]):
+        chosen = jnp.where((group == index)[:, None], table[index][None, :], chosen)
+    return jnp.sum(jnp.where(slot_hit, chosen, 0), axis=1)
+
+
 def trace_pivots(merge_picks, row_devices):
     list_width = merge_picks.shape[1]
     leaf_group = jnp.zeros((list_width,), jnp.int32)
@@ -19,7 +28,8 @@
     levels = row_devices.bit_length() - 1
     for section in reversed(range(levels)):
         offset_rows = row_devices - (row_devices >> section)
-        position = merge_picks[offset_rows + leaf_group, leaf_slot]
+        groups = 1 << levels - 1 - section
+        position = lookup(merge_picks[offset_rows : offset_rows + groups], leaf_group, leaf_slot)
         right_side = (position >= list_width).astype(jnp.int32)
         leaf_group = 2 * leaf_group + right_side
         leaf_slot = position - list_width * right_side
@@ -119,7 +129,7 @@
     own_column = lax.axis_index("cols")
     leaf_group, leaf_slot = trace_pivots(merge_picks, row_devices)
     owner_mask = leaf_group == own_row
-    local_rows = jnp.take(leaf_picks[0], leaf_slot)
+    local_rows = lookup(leaf_picks, jnp.zeros_like(leaf_slot), leaf_slot)
     own_trailing = jnp.take(trailing, local_rows, axis=0)
     own_columns = jnp.take(jnp.concatenate([panel_t, prev_lower_t], 0), local_rows, axis=1)
     own_pivots = jnp.concatenate([own_trailing, own_columns.T], 1)

time: 219 us -> 210 us (0.959)
  local copies, waits for them, and re-layouts: 22.8 us -> 11.4 us
  other arithmetic: 2.31 us -> 6.24 us
    gather x6 -> x0, local copies, waits for them, and re-layouts: 13.8 us -> none  [the longest x5 11.9 us: trace_pivots(): position = merge_picks[offset_rows + leaf_group, leaf_slot]]
    reduce_sum x0 -> x6, other arithmetic: none -> 3.2 us  [lookup(): return jnp.sum(jnp.where(slot_hit, chosen, 0), axis=1)]
  transfers between devices with their start and end apart: 12 -> 12, of which waited for: 7 -> 7; matrix products, arithmetic and copies ran while one was open for 25% -> 22% of each run, Pallas kernels for 15% -> 16%
where the time goes in v6:
time: 210 us; the launch traced here: 208 us
  starting transfers between devices  44.2 us (21%)
  waiting for transfers between devices  42.2 us (20%)
  Pallas kernels  32.9 us (16%)
  matrix products  29.1 us (14%)
  blocking collectives  27.1 us (13%)
  between operations  14.7 us (7%)
  local copies, waits for them, and re-layouts  11.4 us (5%)
  other arithmetic  6.24 us (3%)
    ppermute x10, starting transfers between devices, from_partner(): lax.ppermute(shard, axis, [(i, i ^ 1 << apart) for i in range(lax.axis_si...  44.1 us
    ppermute x10, waiting for transfers between devices, from_partner(): lax.ppermute(shard, axis, [(i, i ^ 1 << apart) for i in range(lax.axis_si...  41.5 us
    pallas_call x1, Pallas kernels, factor(): pl.pallas_call(elimination_kernel, out_shape=jax.ShapeDtypeStruct(matrix....  32.9 us
    all_gather x1, blocking collectives, body(): lax.all_gather(pivot_data[:, own_trailing.shape[1]:].T, 'cols', axis=0, t...  27.1 us
    dot_general x29, matrix products, product(): return jnp.dot(left_side, right_side, precision=full_precision)  12.3 us
    dot_general x3, matrix products, contract_first(): lax.dot_general(left_side, right_side, (((0,), (0,)), ((), ())), precisio...  11.3 us
  transfers between devices with their start and end apart: 12, of which 7 were waited for; matrix products, arithmetic and copies ran while one was open for 22% of the time, Pallas kernels for 16%

profile of v6, /device:TPU:1, one launch (start us, length us, event | category | flops | bytes accessed | tf_op | source)
XLA Modules:
  0.0 207.8 jit_solution(8485846635354705585)
XLA Ops:
  8.0 0.9 fusion.21
  8.9 1.2 fusion.20
  10.5 1.7 pad_maximum_fusion
  12.6 1.3 copy.25
  14.6 1.0 select_reduce_fusion.1
  15.6 0.9 select_reduce_fusion
  17.2 1.0 gather_fusion
  18.5 8.8 %collective-permute-start = (f32[256,288]{1,0:T(8,128)S(1)}, f32[256,288]{1,0:T(8,128)S(1)}, u32[]{:S(2)}, u32[]{:S(2)}) collective-permute-start(f32[256,288]{1,0:T(8,128)S(1)} %maximum_select_fusion), channel_id=1, source_target_pairs={{0,16},{16,0},{32,48},{48,32},{64,80},{80,64},{96,112},{112,96},{1... | collective-permute-start | bytes 884744 | tf_op jit(solution)/shard_map/ppermute | solution.py:12
  27.3 1.3 collective-permute-done
  28.7 1.9 collective-permute-start.1
  30.6 10.4 %collective-permute-done.1 = f32[256,288]{1,0:T(8,128)S(1)} collective-permute-done((f32[256,288]{1,0:T(8,128)S(1)}, f32[256,288]{1,0:T(8,128)S(1)}, u32[]{:S(2)}, u32[]{:S(2)}) %collective-permute-start.1) | collective-permute-done | bytes 294944 | tf_op jit(solution)/shard_map/ppermute | solution.py:12
  41.1 1.9 collective-permute-start.2
  43.0 11.0 %collective-permute-done.2 = f32[256,288]{1,0:T(8,128)S(1)} collective-permute-done((f32[256,288]{1,0:T(8,128)S(1)}, f32[256,288]{1,0:T(8,128)S(1)}, u32[]{:S(2)}, u32[]{:S(2)}) %collective-permute-start.2) | collective-permute-done | bytes 294944 | tf_op jit(solution)/shard_map/ppermute | solution.py:12
  54.0 1.9 collective-permute-start.3
  56.0 8.6 %collective-permute-done.3 = f32[256,288]{1,0:T(8,128)S(1)} collective-permute-done((f32[256,288]{1,0:T(8,128)S(1)}, f32[256,288]{1,0:T(8,128)S(1)}, u32[]{:S(2)}, u32[]{:S(2)}) %collective-permute-start.3) | collective-permute-done | bytes 294944 | tf_op jit(solution)/shard_map/ppermute | solution.py:12
  64.7 1.9 collective-permute-start.4
  66.8 9.0 %collective-permute-done.4 = f32[256,288]{1,0:T(8,128)S(1)} collective-permute-done((f32[256,288]{1,0:T(8,128)S(1)}, f32[256,288]{1,0:T(8,128)S(1)}, u32[]{:S(2)}, u32[]{:S(2)}) %collective-permute-start.4) | collective-permute-done | bytes 294944 | tf_op jit(solution)/shard_map/ppermute | solution.py:12
  76.0 27.1 %all-gather = f32[512,256]{1,0:T(8,128)S(1)} all-gather(f32[32,256]{1,0:T(8,128)S(1)} %copy.26), channel_id=2, replica_groups=mesh['rows'=32,'cols'=16] {'cols'}, dimensions={0}, use_global_device_ids=true | all-gather | bytes 557056 | tf_op jit(solution)/shard_map/all_gather | solution.py:138
  104.7 32.9 %shard_map.101 = f32[256,256]{1,0:T(8,128)} custom-call(f32[256,256]{1,0:T(8,128)} %bitcast.99), custom_call_target="tpu_custom_call" | custom-call | tf_op jit(solution)/shard_map/pallas_call | solution.py:96
  137.6 1.1 copy.28
  138.7 2.5 %gather_fusion.2 = f32[256]{0:T(256)S(1)} fusion(f32[256,256]{0,1:T(8,128)S(1)} %broadcast_select_fusion.1, s32[256]{0:T(256)S(1)} %bitcast.96), kind=kCustom, calls=%fused_computation.2 | custom fusion | bytes 4096 | tf_op jit(solution)/shard_map/jit(diagonal)/cond/branch_0_fun/gather | solution.py:57
  151.7 1.3 convolution_divide_fusion
  153.0 3.6 %fusion.27 = f32[256,2048]{1,0:T(8,128)S(1)} fusion(f32[256,256]{1,0:T(8,128)} %convolution_divide_fusion, f32[256,2048]{1,0:T(8,128)} %all-gather.4.cloned.1.call-done), kind=kOutput, calls=%fused_computation.124 | convolution fusion | flops 1610612736 | bytes 4456448 | tf_op jit(solution)/shard_map/dot_general | solution.py:151
  156.6 1.9 fusion.35
  158.6 11.4 %collective-permute-start.5 = (f32[16,256]{1,0:T(8,128)S(1)}, f32[16,256]{1,0:T(8,128)S(1)}, u32[]{:S(2)}, u32[]{:S(2)}) collective-permute-start(f32[16,256]{1,0:T(8,128)S(1)} %fusion.35), channel_id=1, source_target_pairs={{0,16},{16,0},{32,48},{48,32},{64,80},{80,64},{96,112},{112,96},{1... | collective-permute-start | bytes 49160 | tf_op jit(solution)/shard_map/ppermute | solution.py:12
  170.8 3.2 %collective-permute-start.6 = (f32[16,256]{1,0:T(8,128)S(1)}, f32[16,256]{1,0:T(8,128)S(1)}, u32[]{:S(2)}, u32[]{:S(2)}) collective-permute-start(f32[16,256]{1,0:T(8,128)S(1)} %add.393), channel_id=1, source_target_pairs={{0,32},{16,48},{32,0},{48,16},{64,96},{80,112},{96,64},{112,80},{1... | collective-permute-start | bytes 49160 | tf_op jit(solution)/shard_map/ppermute | solution.py:12
  175.3 5.7 %collective-permute-start.7 = (f32[16,256]{1,0:T(8,128)S(1)}, f32[16,256]{1,0:T(8,128)S(1)}, u32[]{:S(2)}, u32[]{:S(2)}) collective-permute-start(f32[16,256]{1,0:T(8,128)S(1)} %add.394), channel_id=1, source_target_pairs={{0,64},{16,80},{32,96},{48,112},{64,0},{80,16},{96,32},{112,48},{1... | collective-permute-start | bytes 49160 | tf_op jit(solution)/shard_map/ppermute | solution.py:12
  181.4 0.8 copy.31
  182.2 3.1 %collective-permute-start.8 = (f32[16,256]{1,0:T(8,128)S(1)}, f32[16,256]{1,0:T(8,128)S(1)}, u32[]{:S(2)}, u32[]{:S(2)}) collective-permute-start(f32[16,256]{1,0:T(8,128)S(1)} %add.395), channel_id=1, source_target_pairs={{0,128},{16,144},{32,160},{48,176},{64,192},{80,208},{96,224},{112... | collective-permute-start | bytes 49160 | tf_op jit(solution)/shard_map/ppermute | solution.py:12
  185.3 5.9 %convolution_subtract_fusion.1 = f32[2048,256]{1,0:T(8,128)S(1)} fusion(f32[2048,256]{1,0:T(8,128)} %param.7, f32[256,2048]{1,0:T(8,128)} %all-gather.6.cloned.1.call-done, f32[256,256]{1,0:T(8,128)S(1)} %copy-done), kind=kOutput, calls=%fused_computation.4 | convolution fusion | flops 1611137024 | bytes 6553600 | tf_op jit(solution)/shard_map/dot_general | solution.py:105
  191.2 4.3 %collective-permute-start.9 = (f32[16,256]{1,0:T(8,128)S(1)}, f32[16,256]{1,0:T(8,128)S(1)}, u32[]{:S(2)}, u32[]{:S(2)}) collective-permute-start(f32[16,256]{1,0:T(8,128)S(1)} %add.396), channel_id=1, source_target_pairs={{0,256},{16,272},{32,288},{48,304},{64,320},{80,336},{96,352},{112... | collective-permute-start | bytes 49160 | tf_op jit(solution)/shard_map/ppermute | solution.py:12
  195.6 4.8 %convolution_subtract_fusion = f32[2048,256]{1,0:T(8,128)} fusion(f32[2048,256]{1,0:T(8,128)S(1)} %convolution_subtract_fusion.1, f32[256,2048]{1,0:T(8,128)S(1)} %fusion.27, f32[256,256]{1,0:T(8,128)S(1)} %fusion.12), kind=kOutput, calls=%fused_computation.3 | convolution fusion | flops 1611137024 | bytes 6553600 | tf_op jit(solution)/shard_map/dot_general | solution.py:105
  (96 shorter events, 18.8 us)
Async XLA Ops:
  7.2 166.8 %copy-start = (f32[256,256]{1,0:T(8,128)S(1)}, f32[256,256]{1,0:T(8,128)}, u32[]{:S(2)}) copy-start(f32[256,256]{1,0:T(8,128)} %param.9) | copy-start | bytes 786436
  7.2 10.0 %copy-start.1 = (f32[2048,256]{1,0:T(8,128)S(1)}, f32[2048,256]{1,0:T(8,128)}, u32[]{:S(2)}) copy-start(f32[2048,256]{1,0:T(8,128)} %param.7) | copy-start | bytes 6291460
  7.2 145.8 %all-gather.4.cloned.1.call-start = ((), (), s32[]{:S(2)}) async-start(), calls=%async_computation | async-start | bytes 2228224 | tf_op jit(solution)/shard_map/all_gather | solution.py:147
  7.9 177.4 %all-gather.6.cloned.1.call-start = ((), (), s32[]{:S(2)}) async-start(), calls=%async_computation.1 | async-start | bytes 2228224 | tf_op jit(solution)/shard_map/all_gather | solution.py:145
  18.5 10.1 %collective-permute-start = (f32[256,288]{1,0:T(8,128)S(1)}, f32[256,288]{1,0:T(8,128)S(1)}, u32[]{:S(2)}, u32[]{:S(2)}) collective-permute-start(f32[256,288]{1,0:T(8,128)S(1)} %maximum_select_fusion), channel_id=1, source_target_pairs={{0,16},{16,0},{32,48},{48,32},{64,80},{80,64},{96,112},{112,96},{1... | collective-permute-start | bytes 884744 | tf_op jit(solution)/shard_map/ppermute | solution.py:12
  28.7 12.3 %collective-permute-start.1 = (f32[256,288]{1,0:T(8,128)S(1)}, f32[256,288]{1,0:T(8,128)S(1)}, u32[]{:S(2)}, u32[]{:S(2)}) collective-permute-start(f32[256,288]{1,0:T(8,128)S(1)} %add.370), channel_id=1, source_target_pairs={{0,32},{16,48},{32,0},{48,16},{64,96},{80,112},{96,64},{112,80},{1... | collective-permute-start | bytes 884744 | tf_op jit(solution)/shard_map/ppermute | solution.py:12
  41.1 12.9 %collective-permute-start.2 = (f32[256,288]{1,0:T(8,128)S(1)}, f32[256,288]{1,0:T(8,128)S(1)}, u32[]{:S(2)}, u32[]{:S(2)}) collective-permute-start(f32[256,288]{1,0:T(8,128)S(1)} %add.371), channel_id=1, source_target_pairs={{0,64},{16,80},{32,96},{48,112},{64,0},{80,16},{96,32},{112,48},{1... | collective-permute-start | bytes 884744 | tf_op jit(solution)/shard_map/ppermute | solution.py:12
  54.0 10.6 %collective-permute-start.3 = (f32[256,288]{1,0:T(8,128)S(1)}, f32[256,288]{1,0:T(8,128)S(1)}, u32[]{:S(2)}, u32[]{:S(2)}) collective-permute-start(f32[256,288]{1,0:T(8,128)S(1)} %add.372), channel_id=1, source_target_pairs={{0,128},{16,144},{32,160},{48,176},{64,192},{80,208},{96,224},{112... | collective-permute-start | bytes 884744 | tf_op jit(solution)/shard_map/ppermute | solution.py:12
  64.7 11.2 %collective-permute-start.4 = (f32[256,288]{1,0:T(8,128)S(1)}, f32[256,288]{1,0:T(8,128)S(1)}, u32[]{:S(2)}, u32[]{:S(2)}) collective-permute-start(f32[256,288]{1,0:T(8,128)S(1)} %add.373), channel_id=1, source_target_pairs={{0,256},{16,272},{32,288},{48,304},{64,320},{80,336},{96,352},{112... | collective-permute-start | bytes 884744 | tf_op jit(solution)/shard_map/ppermute | solution.py:12
  138.7 3.8 %copy-start.2 = (f32[256,256]{1,0:T(8,128)S(1)}, f32[256,256]{1,0:T(8,128)}, u32[]{:S(2)}) copy-start(f32[256,256]{1,0:T(8,128)} %shard_map.101) | copy-start | bytes 786436
  156.6 17.4 %copy-start.3 = (f32[16,16,256]{2,1,0:T(8,128)S(1)}, f32[16,16,256]{2,1,0:T(8,128)}, u32[]{:S(2)}) copy-start(f32[16,16,256]{2,1,0:T(8,128)} %get-tuple-element.26) | copy-start | bytes 786436
  156.6 18.6 %copy-start.5 = (f32[16,2048]{1,0:T(8,128)}, f32[16,2048]{1,0:T(8,128)S(1)}, u32[]{:S(2)}) copy-start(f32[16,2048]{1,0:T(8,128)S(1)} %constant_dynamic-slice_fusion) | copy-start | bytes 393220
  158.6 12.2 %collective-permute-start.5 = (f32[16,256]{1,0:T(8,128)S(1)}, f32[16,256]{1,0:T(8,128)S(1)}, u32[]{:S(2)}, u32[]{:S(2)}) collective-permute-start(f32[16,256]{1,0:T(8,128)S(1)} %fusion.35), channel_id=1, source_target_pairs={{0,16},{16,0},{32,48},{48,32},{64,80},{80,64},{96,112},{112,96},{1... | collective-permute-start | bytes 49160 | tf_op jit(solution)/shard_map/ppermute | solution.py:12
  170.8 4.5 %collective-permute-start.6 = (f32[16,256]{1,0:T(8,128)S(1)}, f32[16,256]{1,0:T(8,128)S(1)}, u32[]{:S(2)}, u32[]{:S(2)}) collective-permute-start(f32[16,256]{1,0:T(8,128)S(1)} %add.393), channel_id=1, source_target_pairs={{0,32},{16,48},{32,0},{48,16},{64,96},{80,112},{96,64},{112,80},{1... | collective-permute-start | bytes 49160 | tf_op jit(solution)/shard_map/ppermute | solution.py:12
  175.3 6.9 %collective-permute-start.7 = (f32[16,256]{1,0:T(8,128)S(1)}, f32[16,256]{1,0:T(8,128)S(1)}, u32[]{:S(2)}, u32[]{:S(2)}) collective-permute-start(f32[16,256]{1,0:T(8,128)S(1)} %add.394), channel_id=1, source_target_pairs={{0,64},{16,80},{32,96},{48,112},{64,0},{80,16},{96,32},{112,48},{1... | collective-permute-start | bytes 49160 | tf_op jit(solution)/shard_map/ppermute | solution.py:12
  181.3 14.2 %copy-start.4 = (f32[256,256]{1,0:T(8,128)}, f32[256,256]{1,0:T(8,128)S(1)}, u32[]{:S(2)}) copy-start(f32[256,256]{1,0:T(8,128)S(1)} %fusion.12) | copy-start | bytes 786436
  182.2 9.0 %collective-permute-start.8 = (f32[16,256]{1,0:T(8,128)S(1)}, f32[16,256]{1,0:T(8,128)S(1)}, u32[]{:S(2)}, u32[]{:S(2)}) collective-permute-start(f32[16,256]{1,0:T(8,128)S(1)} %add.395), channel_id=1, source_target_pairs={{0,128},{16,144},{32,160},{48,176},{64,192},{80,208},{96,224},{112... | collective-permute-start | bytes 49160 | tf_op jit(solution)/shard_map/ppermute | solution.py:12
  191.2 9.2 %collective-permute-start.9 = (f32[16,256]{1,0:T(8,128)S(1)}, f32[16,256]{1,0:T(8,128)S(1)}, u32[]{:S(2)}, u32[]{:S(2)}) collective-permute-start(f32[16,256]{1,0:T(8,128)S(1)} %add.396), channel_id=1, source_target_pairs={{0,256},{16,272},{32,288},{48,304},{64,320},{80,336},{96,352},{112... | collective-permute-start | bytes 49160 | tf_op jit(solution)/shard_map/ppermute | solution.py:12
Sparse Core Ops, SparseCore 0:
  10.1 69.8 all-gather.3
  82.1 70.2 all-gather.5

commit v7 on v6

--- a/solution.py
+++ b/solution.py
@@ -54,7 +54,11 @@
 
 
 def upper_inverse(upper):
-    diagonal = jnp.diagonal(upper)
+    order = upper.shape[0]
+    on_diagonal = lax.broadcasted_iota(jnp.int32, (order, order), 0) == lax.broadcasted_iota(
+        jnp.int32, (order, order), 1
+    )
+    diagonal = jnp.sum(jnp.where(on_diagonal, upper, 0.0), axis=0)
     scaled = upper / diagonal[:, None]
     unit_inverse = unit_lower_inverse(scaled.T).T
     return unit_inverse / diagonal[None, :]
@@ -64,31 +68,56 @@
     order = matrix_ref.shape[0]
     reduced_ref[...] = matrix_ref[...]
     phase = 32
-    for first_row in range(0, order - 1, phase):
+    for first_row in range(0, order, phase):
         first_col = (first_row // 128) * 128
         height = order - first_row
         width = order - first_col
-        row_index = lax.broadcasted_iota(jnp.int32, (height, width), 0) + first_row
-        col_index = lax.broadcasted_iota(jnp.int32, (height, width), 1) + first_col
-
-        def step(column_index, carry):
+        lanes = min(128, width)
+        row_index = lax.broadcasted_iota(jnp.int32, (height, 1), 0) + first_row
+        col_index = lax.broadcasted_iota(jnp.int32, (1, width), 1) + first_col
+        block_index = lax.broadcasted_iota(jnp.int32, (height, lanes), 1) + first_col
+
+        def step(pair, carry):
+            first = first_row + 2 * pair
+            second = first + 1
             window = reduced_ref[first_row:, first_col:]
-            pivot_line = reduced_ref[pl.ds(column_index, 1), :][:, first_col:]
-            on_column = col_index == column_index
-            pivot_column = jnp.sum(jnp.where(on_column, window, 0.0), axis=1, keepdims=True)
-            pivot_value = jnp.sum(
-                jnp.where(on_column[0:1], pivot_line, 0.0), axis=1, keepdims=True
-            )
-            factors = pivot_column / pivot_value
-            below = row_index > column_index
-            window = jnp.where(
-                below & (col_index > column_index), window - factors * pivot_line, window
-            )
-            window = jnp.where(below & on_column, factors, window)
+            first_line = reduced_ref[pl.ds(first, 1), :][:, first_col:]
+            second_line = reduced_ref[pl.ds(second, 1), :][:, first_col:]
+            lead = window[:, :lanes]
+            on_first = block_index == first
+            on_second = block_index == second
+            first_column = jnp.sum(jnp.where(on_first, lead, 0.0), axis=1, keepdims=True)
+            second_column = jnp.sum(jnp.where(on_second, lead, 0.0), axis=1, keepdims=True)
+            first_pivot = jnp.sum(
+                jnp.where(col_index == first, first_line, 0.0), axis=1, keepdims=True
+            )
+            coupling = jnp.sum(
+                jnp.where(col_index == second, first_line, 0.0), axis=1, keepdims=True
+            )
+            second_lead = jnp.sum(
+                jnp.where(col_index == first, second_line, 0.0), axis=1, keepdims=True
+            )
+            below_first = row_index > first
+            below_second = row_index > second
+            first_factors = jnp.where(below_first, first_column / first_pivot, 0.0)
+            first_line = jnp.where(col_index > first, first_line, 0.0)
+            second_line = second_line - second_lead / first_pivot * first_line
+            second_column = second_column - first_factors * coupling
+            second_pivot = jnp.sum(
+                jnp.where(col_index == second, second_line, 0.0), axis=1, keepdims=True
+            )
+            second_factors = jnp.where(below_second, second_column / second_pivot, 0.0)
+            second_line = jnp.where(col_index > second, second_line, 0.0)
+            window = window - first_factors * first_line - second_factors * second_line
+            first_kept = jnp.where(below_first, first_factors, first_column)
+            second_kept = jnp.where(below_second, second_factors, second_column)
             reduced_ref[first_row:, first_col:] = window
+            reduced_ref[first_row:, first_col : first_col + lanes] = jnp.where(
+                on_first, first_kept, jnp.where(on_second, second_kept, window[:, :lanes])
+            )
             return carry
 
-        lax.fori_loop(first_row, min(first_row + phase, order - 1), step, 0)
+        lax.fori_loop(0, min(phase, order - first_row) // 2, step, 0)
 
 
 def factor(matrix):

time: 210 us -> 204 us (0.971)
  Pallas kernels: 32.9 us -> 29.5 us
  local copies, waits for them, and re-layouts: 11.4 us -> 9 us
    pallas_call x1, Pallas kernels: 32.9 us -> 29.5 us  [factor(): pl.pallas_call(elimination_kernel, out_shape=jax.ShapeDtypeStruct(matrix....]
    gather x1 -> x0, local copies, waits for them, and re-layouts: 2.55 us -> none  [upper_inverse(): diagonal = jnp.diagonal(upper)]
  transfers between devices with their start and end apart: 12 -> 12, of which waited for: 7 -> 8; matrix products, arithmetic and copies ran while one was open for 22% -> 22% of each run, Pallas kernels for 16% -> 15%
where the time goes in v7:
time: 204 us; the launch traced here: 202 us
  starting transfers between devices  43.3 us (21%)
  waiting for transfers between devices  42.9 us (21%)
  Pallas kernels  29.5 us (14%)
  matrix products  29.4 us (14%)
  blocking collectives  26.7 us (13%)
  between operations  14.7 us (7%)
  local copies, waits for them, and re-layouts  9 us (4%)
  other arithmetic  6.27 us (3%)
    ppermute x10, starting transfers between devices, from_partner(): lax.ppermute(shard, axis, [(i, i ^ 1 << apart) for i in range(lax.axis_si...  43.3 us
    ppermute x10, waiting for transfers between devices, from_partner(): lax.ppermute(shard, axis, [(i, i ^ 1 << apart) for i in range(lax.axis_si...  42.2 us
    pallas_call x1, Pallas kernels, factor(): pl.pallas_call(elimination_kernel, out_shape=jax.ShapeDtypeStruct(matrix....  29.5 us
    all_gather x1, blocking collectives, body(): lax.all_gather(pivot_data[:, own_trailing.shape[1]:].T, 'cols', axis=0, t...  26.7 us
    dot_general x29, matrix products, product(): return jnp.dot(left_side, right_side, precision=full_precision)  12.6 us
    dot_general x3, matrix products, contract_first(): lax.dot_general(left_side, right_side, (((0,), (0,)), ((), ())), precisio...  11.3 us
  transfers between devices with their start and end apart: 12, of which 8 were waited for; matrix products, arithmetic and copies ran while one was open for 22% of the time, Pallas kernels for 15%

profile of v7, /device:TPU:1, one launch (start us, length us, event | category | flops | bytes accessed | tf_op | source)
XLA Modules:
  0.0 201.7 jit_solution(8926897187183310555)
XLA Ops:
  8.0 0.9 fusion.21
  8.9 1.2 fusion.20
  10.4 1.7 pad_maximum_fusion
  12.4 1.3 copy.28
  14.9 0.8 select_reduce_fusion.1
  16.4 1.0 gather_fusion
  17.7 8.8 %collective-permute-start = (f32[256,288]{1,0:T(8,128)S(1)}, f32[256,288]{1,0:T(8,128)S(1)}, u32[]{:S(2)}, u32[]{:S(2)}) collective-permute-start(f32[256,288]{1,0:T(8,128)S(1)} %maximum_select_fusion), channel_id=1, source_target_pairs={{0,16},{16,0},{32,48},{48,32},{64,80},{80,64},{96,112},{112,96},{1... | collective-permute-start | bytes 884744 | tf_op jit(solution)/shard_map/ppermute | solution.py:12
  26.5 1.3 collective-permute-done
  27.9 1.9 collective-permute-start.1
  29.8 10.4 %collective-permute-done.1 = f32[256,288]{1,0:T(8,128)S(1)} collective-permute-done((f32[256,288]{1,0:T(8,128)S(1)}, f32[256,288]{1,0:T(8,128)S(1)}, u32[]{:S(2)}, u32[]{:S(2)}) %collective-permute-start.1) | collective-permute-done | bytes 294944 | tf_op jit(solution)/shard_map/ppermute | solution.py:12
  40.3 1.9 collective-permute-start.2
  42.2 11.0 %collective-permute-done.2 = f32[256,288]{1,0:T(8,128)S(1)} collective-permute-done((f32[256,288]{1,0:T(8,128)S(1)}, f32[256,288]{1,0:T(8,128)S(1)}, u32[]{:S(2)}, u32[]{:S(2)}) %collective-permute-start.2) | collective-permute-done | bytes 294944 | tf_op jit(solution)/shard_map/ppermute | solution.py:12
  53.2 1.9 collective-permute-start.3
  55.4 8.4 %collective-permute-done.3 = f32[256,288]{1,0:T(8,128)S(1)} collective-permute-done((f32[256,288]{1,0:T(8,128)S(1)}, f32[256,288]{1,0:T(8,128)S(1)}, u32[]{:S(2)}, u32[]{:S(2)}) %collective-permute-start.3) | collective-permute-done | bytes 294944 | tf_op jit(solution)/shard_map/ppermute | solution.py:12
  63.9 1.9 collective-permute-start.4
  66.0 9.0 %collective-permute-done.4 = f32[256,288]{1,0:T(8,128)S(1)} collective-permute-done((f32[256,288]{1,0:T(8,128)S(1)}, f32[256,288]{1,0:T(8,128)S(1)}, u32[]{:S(2)}, u32[]{:S(2)}) %collective-permute-start.4) | collective-permute-done | bytes 294944 | tf_op jit(solution)/shard_map/ppermute | solution.py:12
  75.2 26.7 %all-gather = f32[512,256]{1,0:T(8,128)S(1)} all-gather(f32[32,256]{1,0:T(8,128)S(1)} %copy.29), channel_id=2, replica_groups=mesh['rows'=32,'cols'=16] {'cols'}, dimensions={0}, use_global_device_ids=true | all-gather | bytes 557056 | tf_op jit(solution)/shard_map/all_gather | solution.py:167
  102.6 0.8 copy.30
  103.4 29.5 %shard_map.101 = f32[256,256]{1,0:T(8,128)} custom-call(f32[256,256]{1,0:T(8,128)} %bitcast.97), custom_call_target="tpu_custom_call" | custom-call | tf_op jit(solution)/shard_map/pallas_call | solution.py:125
  132.9 1.1 copy.31
  141.9 1.3 convolution_divide_fusion
  146.1 3.8 %fusion.27 = f32[256,2048]{1,0:T(8,128)S(1)} fusion(f32[256,256]{1,0:T(8,128)} %convolution_divide_fusion, f32[256,2048]{1,0:T(8,128)} %all-gather.4.cloned.1.call-done), kind=kOutput, calls=%fused_computation.123 | convolution fusion | flops 1610612736 | bytes 4456448 | tf_op jit(solution)/shard_map/dot_general | solution.py:180
  150.0 1.7 fusion.35
  151.7 12.6 %collective-permute-start.5 = (f32[16,256]{1,0:T(8,128)S(1)}, f32[16,256]{1,0:T(8,128)S(1)}, u32[]{:S(2)}, u32[]{:S(2)}) collective-permute-start(f32[16,256]{1,0:T(8,128)S(1)} %fusion.35), channel_id=1, source_target_pairs={{0,16},{16,0},{32,48},{48,32},{64,80},{80,64},{96,112},{112,96},{1... | collective-permute-start | bytes 49160 | tf_op jit(solution)/shard_map/ppermute | solution.py:12
  165.1 2.8 %collective-permute-start.6 = (f32[16,256]{1,0:T(8,128)S(1)}, f32[16,256]{1,0:T(8,128)S(1)}, u32[]{:S(2)}, u32[]{:S(2)}) collective-permute-start(f32[16,256]{1,0:T(8,128)S(1)} %add.389), channel_id=1, source_target_pairs={{0,32},{16,48},{32,0},{48,16},{64,96},{80,112},{96,64},{112,80},{1... | collective-permute-start | bytes 49160 | tf_op jit(solution)/shard_map/ppermute | solution.py:12
  168.5 1.0 collective-permute-done.6
  169.6 4.3 %collective-permute-start.7 = (f32[16,256]{1,0:T(8,128)S(1)}, f32[16,256]{1,0:T(8,128)}, u32[]{:S(2)}, u32[]{:S(2)}) collective-permute-start(f32[16,256]{1,0:T(8,128)S(1)} %add.390), channel_id=1, source_target_pairs={{0,64},{16,80},{32,96},{48,112},{64,0},{80,16},{96,32},{112,48},{1... | collective-permute-start | bytes 49160 | tf_op jit(solution)/shard_map/ppermute | solution.py:12
  174.3 0.8 copy.34
  176.4 2.8 %collective-permute-start.8 = (f32[16,256]{1,0:T(8,128)S(1)}, f32[16,256]{1,0:T(8,128)S(1)}, u32[]{:S(2)}, u32[]{:S(2)}) collective-permute-start(f32[16,256]{1,0:T(8,128)S(1)} %add.391), channel_id=1, source_target_pairs={{0,128},{16,144},{32,160},{48,176},{64,192},{80,208},{96,224},{112... | collective-permute-start | bytes 49160 | tf_op jit(solution)/shard_map/ppermute | solution.py:12
  179.2 5.9 %convolution_subtract_fusion.1 = f32[2048,256]{1,0:T(8,128)S(1)} fusion(f32[2048,256]{1,0:T(8,128)} %param.7, f32[256,2048]{1,0:T(8,128)} %all-gather.6.cloned.1.call-done, f32[256,256]{1,0:T(8,128)S(1)} %copy-done), kind=kOutput, calls=%fused_computation.3 | convolution fusion | flops 1611137024 | bytes 6553600 | tf_op jit(solution)/shard_map/dot_general | solution.py:134
  185.1 4.3 %collective-permute-start.9 = (f32[16,256]{1,0:T(8,128)S(1)}, f32[16,256]{1,0:T(8,128)S(1)}, u32[]{:S(2)}, u32[]{:S(2)}) collective-permute-start(f32[16,256]{1,0:T(8,128)S(1)} %add.392), channel_id=1, source_target_pairs={{0,256},{16,272},{32,288},{48,304},{64,320},{80,336},{96,352},{112... | collective-permute-start | bytes 49160 | tf_op jit(solution)/shard_map/ppermute | solution.py:12
  189.5 4.8 %convolution_subtract_fusion = f32[2048,256]{1,0:T(8,128)} fusion(f32[2048,256]{1,0:T(8,128)S(1)} %convolution_subtract_fusion.1, f32[256,2048]{1,0:T(8,128)S(1)} %fusion.27, f32[256,256]{1,0:T(8,128)S(1)} %fusion.12), kind=kOutput, calls=%fused_computation.2 | convolution fusion | flops 1611137024 | bytes 6553600 | tf_op jit(solution)/shard_map/dot_general | solution.py:134
  (96 shorter events, 19.3 us)
Async XLA Ops:
  7.2 160.8 %copy-start = (f32[256,256]{1,0:T(8,128)S(1)}, f32[256,256]{1,0:T(8,128)}, u32[]{:S(2)}) copy-start(f32[256,256]{1,0:T(8,128)} %param.9) | copy-start | bytes 786436
  7.2 9.2 %copy-start.1 = (f32[2048,256]{1,0:T(8,128)S(1)}, f32[2048,256]{1,0:T(8,128)}, u32[]{:S(2)}) copy-start(f32[2048,256]{1,0:T(8,128)} %param.7) | copy-start | bytes 6291460
  7.2 138.9 %all-gather.4.cloned.1.call-start = ((), (), s32[]{:S(2)}) async-start(), calls=%async_computation | async-start | bytes 2228224 | tf_op jit(solution)/shard_map/all_gather | solution.py:176
  7.9 171.3 %all-gather.6.cloned.1.call-start = ((), (), s32[]{:S(2)}) async-start(), calls=%async_computation.1 | async-start | bytes 2228224 | tf_op jit(solution)/shard_map/all_gather | solution.py:174
  17.7 10.1 %collective-permute-start = (f32[256,288]{1,0:T(8,128)S(1)}, f32[256,288]{1,0:T(8,128)S(1)}, u32[]{:S(2)}, u32[]{:S(2)}) collective-permute-start(f32[256,288]{1,0:T(8,128)S(1)} %maximum_select_fusion), channel_id=1, source_target_pairs={{0,16},{16,0},{32,48},{48,32},{64,80},{80,64},{96,112},{112,96},{1... | collective-permute-start | bytes 884744 | tf_op jit(solution)/shard_map/ppermute | solution.py:12
  27.9 12.3 %collective-permute-start.1 = (f32[256,288]{1,0:T(8,128)S(1)}, f32[256,288]{1,0:T(8,128)S(1)}, u32[]{:S(2)}, u32[]{:S(2)}) collective-permute-start(f32[256,288]{1,0:T(8,128)S(1)} %add.366), channel_id=1, source_target_pairs={{0,32},{16,48},{32,0},{48,16},{64,96},{80,112},{96,64},{112,80},{1... | collective-permute-start | bytes 884744 | tf_op jit(solution)/shard_map/ppermute | solution.py:12
  40.3 12.9 %collective-permute-start.2 = (f32[256,288]{1,0:T(8,128)S(1)}, f32[256,288]{1,0:T(8,128)S(1)}, u32[]{:S(2)}, u32[]{:S(2)}) collective-permute-start(f32[256,288]{1,0:T(8,128)S(1)} %add.367), channel_id=1, source_target_pairs={{0,64},{16,80},{32,96},{48,112},{64,0},{80,16},{96,32},{112,48},{1... | collective-permute-start | bytes 884744 | tf_op jit(solution)/shard_map/ppermute | solution.py:12
  53.2 10.6 %collective-permute-start.3 = (f32[256,288]{1,0:T(8,128)S(1)}, f32[256,288]{1,0:T(8,128)S(1)}, u32[]{:S(2)}, u32[]{:S(2)}) collective-permute-start(f32[256,288]{1,0:T(8,128)S(1)} %add.368), channel_id=1, source_target_pairs={{0,128},{16,144},{32,160},{48,176},{64,192},{80,208},{96,224},{112... | collective-permute-start | bytes 884744 | tf_op jit(solution)/shard_map/ppermute | solution.py:12
  63.9 11.2 %collective-permute-start.4 = (f32[256,288]{1,0:T(8,128)S(1)}, f32[256,288]{1,0:T(8,128)S(1)}, u32[]{:S(2)}, u32[]{:S(2)}) collective-permute-start(f32[256,288]{1,0:T(8,128)S(1)} %add.369), channel_id=1, source_target_pairs={{0,256},{16,272},{32,288},{48,304},{64,320},{80,336},{96,352},{112... | collective-permute-start | bytes 884744 | tf_op jit(solution)/shard_map/ppermute | solution.py:12
  136.9 2.1 %copy-start.2 = (f32[256,256]{1,0:T(8,128)S(1)}, f32[256,256]{1,0:T(8,128)}, u32[]{:S(2)}) copy-start(f32[256,256]{1,0:T(8,128)} %shard_map.101) | copy-start | bytes 786436
  150.0 18.0 %copy-start.3 = (f32[16,16,256]{2,1,0:T(8,128)S(1)}, f32[16,16,256]{2,1,0:T(8,128)}, u32[]{:S(2)}) copy-start(f32[16,16,256]{2,1,0:T(8,128)} %get-tuple-element.28) | copy-start | bytes 786436
  150.0 19.6 %copy-start.5 = (f32[16,2048]{1,0:T(8,128)}, f32[16,2048]{1,0:T(8,128)S(1)}, u32[]{:S(2)}) copy-start(f32[16,2048]{1,0:T(8,128)S(1)} %constant_dynamic-slice_fusion) | copy-start | bytes 393220
  151.7 13.4 %collective-permute-start.5 = (f32[16,256]{1,0:T(8,128)S(1)}, f32[16,256]{1,0:T(8,128)S(1)}, u32[]{:S(2)}, u32[]{:S(2)}) collective-permute-start(f32[16,256]{1,0:T(8,128)S(1)} %fusion.35), channel_id=1, source_target_pairs={{0,16},{16,0},{32,48},{48,32},{64,80},{80,64},{96,112},{112,96},{1... | collective-permute-start | bytes 49160 | tf_op jit(solution)/shard_map/ppermute | solution.py:12
  165.1 4.5 %collective-permute-start.6 = (f32[16,256]{1,0:T(8,128)S(1)}, f32[16,256]{1,0:T(8,128)S(1)}, u32[]{:S(2)}, u32[]{:S(2)}) collective-permute-start(f32[16,256]{1,0:T(8,128)S(1)} %add.389), channel_id=1, source_target_pairs={{0,32},{16,48},{32,0},{48,16},{64,96},{80,112},{96,64},{112,80},{1... | collective-permute-start | bytes 49160 | tf_op jit(solution)/shard_map/ppermute | solution.py:12
  169.6 6.1 %collective-permute-start.7 = (f32[16,256]{1,0:T(8,128)S(1)}, f32[16,256]{1,0:T(8,128)}, u32[]{:S(2)}, u32[]{:S(2)}) collective-permute-start(f32[16,256]{1,0:T(8,128)S(1)} %add.390), channel_id=1, source_target_pairs={{0,64},{16,80},{32,96},{48,112},{64,0},{80,16},{96,32},{112,48},{1... | collective-permute-start | bytes 49160 | tf_op jit(solution)/shard_map/ppermute | solution.py:12
  174.3 15.1 %copy-start.4 = (f32[256,256]{1,0:T(8,128)}, f32[256,256]{1,0:T(8,128)S(1)}, u32[]{:S(2)}) copy-start(f32[256,256]{1,0:T(8,128)S(1)} %fusion.12) | copy-start | bytes 786436
  176.4 8.7 %collective-permute-start.8 = (f32[16,256]{1,0:T(8,128)S(1)}, f32[16,256]{1,0:T(8,128)S(1)}, u32[]{:S(2)}, u32[]{:S(2)}) collective-permute-start(f32[16,256]{1,0:T(8,128)S(1)} %add.391), channel_id=1, source_target_pairs={{0,128},{16,144},{32,160},{48,176},{64,192},{80,208},{96,224},{112... | collective-permute-start | bytes 49160 | tf_op jit(solution)/shard_map/ppermute | solution.py:12
  185.1 9.2 %collective-permute-start.9 = (f32[16,256]{1,0:T(8,128)S(1)}, f32[16,256]{1,0:T(8,128)S(1)}, u32[]{:S(2)}, u32[]{:S(2)}) collective-permute-start(f32[16,256]{1,0:T(8,128)S(1)} %add.392), channel_id=1, source_target_pairs={{0,256},{16,272},{32,288},{48,304},{64,320},{80,336},{96,352},{112... | collective-permute-start | bytes 49160 | tf_op jit(solution)/shard_map/ppermute | solution.py:12
Sparse Core Ops, SparseCore 0:
  10.1 69.9 all-gather.3
  82.1 70.4 all-gather.5

commit v8 on v7

--- a/solution.py
+++ b/solution.py
@@ -170,18 +170,21 @@
     block_t = pivot_columns[:, :slab_rows].reshape(order, order)
     prev_pivots = pivot_columns[:, slab_rows:].reshape(order, order)
     middle_pivots = pivot_trailing - contract_first(prev_pivots, prev_upper)
-    middle = trailing - contract_first(
-        lax.all_gather(prev_lower_t, "cols", axis=0, tiled=True), prev_upper
-    )
+    prev_full = lax.all_gather(prev_lower_t, "cols", axis=0, tiled=True)
     panel_full = lax.all_gather(panel_t, "cols", axis=0, tiled=True)
+    gram_part, block_t = lax.optimization_barrier((contract_second(panel_full, panel_full), block_t))
+    panel_gram = butterfly_sum(gram_part, "rows")
     lower_left, upper_left = factor(block_t.T)
     inverse = upper_inverse(upper_left)
     upper_right = product(unit_lower_inverse(lower_left), middle_pivots)
     lower_full = jnp.dot(inverse.T, panel_full, precision=full_precision)
+    prev_full, lower_full = lax.optimization_barrier((prev_full, lower_full))
+    middle = trailing - contract_first(prev_full, prev_upper)
     lower_tile = lax.dynamic_slice_in_dim(lower_full, own_column * slab_rows, slab_rows, 0)
     updated = middle - contract_first(lower_full, upper_right)
-    gram_rows = contract_second(lower_tile, lower_full)
-    gram = butterfly_sum(gram_rows, "rows") / (rows_here * row_devices)
+    inverse_tile = lax.dynamic_slice_in_dim(inverse, own_column * slab_rows, slab_rows, 1)
+    gram_rows = contract_first(inverse_tile, product(panel_gram, inverse))
+    gram = gram_rows / (rows_here * row_devices)
     return (lower_tile, upper_left, upper_right, updated, gram)
 
 

time: 204 us -> 223 us (1.093)
  waiting for transfers between devices: 42.9 us -> 56.7 us
  matrix products: 29.4 us -> 33.5 us
    ppermute x10, waiting for transfers between devices: 42.2 us -> 55.9 us  [from_partner(): lax.ppermute(shard, axis, [(i, i ^ 1 << apart) for i in range(lax.axis_si...]
    dot_general x1, matrix products: 1.72 us -> 4.79 us  [contract_second(): lax.dot_general(left_side, right_side, (((1,), (1,)), ((), ())), precisio...]
    dot_general x3 -> x4, matrix products: 11.3 us -> 13.1 us  [contract_first(): lax.dot_general(left_side, right_side, (((0,), (0,)), ((), ())), precisio...]
    dot_general x29 -> x30, matrix products: 12.6 us -> 13.7 us  [product(): return jnp.dot(left_side, right_side, precision=full_precision)]
  transfers between devices with their start and end apart: 12 -> 12, of which waited for: 8 -> 8; matrix products, arithmetic and copies ran while one was open for 22% -> 21% of each run, Pallas kernels for 15% -> 13%
where the time goes in v8:
time: 223 us; the launch traced here: 221 us
  waiting for transfers between devices  56.7 us (25%)
  starting transfers between devices  44.1 us (20%)
  matrix products  33.5 us (15%)
  Pallas kernels  29.5 us (13%)
  blocking collectives  26.7 us (12%)
  between operations  14.8 us (7%)
  local copies, waits for them, and re-layouts  9.64 us (4%)
  other arithmetic  6.37 us (3%)
    ppermute x10, waiting for transfers between devices, from_partner(): lax.ppermute(shard, axis, [(i, i ^ 1 << apart) for i in range(lax.axis_si...  55.9 us
    ppermute x10, starting transfers between devices, from_partner(): lax.ppermute(shard, axis, [(i, i ^ 1 << apart) for i in range(lax.axis_si...  44 us
    pallas_call x1, Pallas kernels, factor(): pl.pallas_call(elimination_kernel, out_shape=jax.ShapeDtypeStruct(matrix....  29.5 us
    all_gather x1, blocking collectives, body(): lax.all_gather(pivot_data[:, own_trailing.shape[1]:].T, 'cols', axis=0, t...  26.7 us
    dot_general x30, matrix products, product(): return jnp.dot(left_side, right_side, precision=full_precision)  13.7 us
    dot_general x4, matrix products, contract_first(): lax.dot_general(left_side, right_side, (((0,), (0,)), ((), ())), precisio...  13.1 us
    dot_general x1, matrix products, contract_second(): lax.dot_general(left_side, right_side, (((1,), (1,)), ((), ())), precisio...  4.79 us
  transfers between devices with their start and end apart: 12, of which 8 were waited for; matrix products, arithmetic and copies ran while one was open for 21% of the time, Pallas kernels for 13%

profile of v8, /device:TPU:1, one launch (start us, length us, event | category | flops | bytes accessed | tf_op | source)
XLA Modules:
  0.0 221.2 jit_solution(7143544082880107228)
XLA Ops:
  8.0 1.2 fusion.24
  10.7 1.7 pad_maximum_fusion
  12.4 1.3 copy.28
  15.0 1.7 gather_fusion
  18.7 8.8 %collective-permute-start = (f32[256,288]{1,0:T(8,128)S(1)}, f32[256,288]{1,0:T(8,128)S(1)}, u32[]{:S(2)}, u32[]{:S(2)}) collective-permute-start(f32[256,288]{1,0:T(8,128)S(1)} %maximum_select_fusion), channel_id=1, source_target_pairs={{0,16},{16,0},{32,48},{48,32},{64,80},{80,64},{96,112},{112,96},{1... | collective-permute-start | bytes 884744 | tf_op jit(solution)/shard_map/ppermute | solution.py:12
  27.5 1.3 collective-permute-done
  28.9 1.9 collective-permute-start.1
  30.8 10.4 %collective-permute-done.1 = f32[256,288]{1,0:T(8,128)S(1)} collective-permute-done((f32[256,288]{1,0:T(8,128)S(1)}, f32[256,288]{1,0:T(8,128)S(1)}, u32[]{:S(2)}, u32[]{:S(2)}) %collective-permute-start.1) | collective-permute-done | bytes 294944 | tf_op jit(solution)/shard_map/ppermute | solution.py:12
  41.3 1.9 collective-permute-start.2
  43.2 11.0 %collective-permute-done.2 = f32[256,288]{1,0:T(8,128)S(1)} collective-permute-done((f32[256,288]{1,0:T(8,128)S(1)}, f32[256,288]{1,0:T(8,128)S(1)}, u32[]{:S(2)}, u32[]{:S(2)}) %collective-permute-start.2) | collective-permute-done | bytes 294944 | tf_op jit(solution)/shard_map/ppermute | solution.py:12
  54.2 1.9 collective-permute-start.3
  56.4 8.4 %collective-permute-done.3 = f32[256,288]{1,0:T(8,128)S(1)} collective-permute-done((f32[256,288]{1,0:T(8,128)S(1)}, f32[256,288]{1,0:T(8,128)S(1)}, u32[]{:S(2)}, u32[]{:S(2)}) %collective-permute-start.3) | collective-permute-done | bytes 294944 | tf_op jit(solution)/shard_map/ppermute | solution.py:12
  64.8 1.9 collective-permute-start.4
  67.0 9.0 %collective-permute-done.4 = f32[256,288]{1,0:T(8,128)S(1)} collective-permute-done((f32[256,288]{1,0:T(8,128)S(1)}, f32[256,288]{1,0:T(8,128)S(1)}, u32[]{:S(2)}, u32[]{:S(2)}) %collective-permute-start.4) | collective-permute-done | bytes 294944 | tf_op jit(solution)/shard_map/ppermute | solution.py:12
  76.1 26.7 %all-gather = f32[512,256]{1,0:T(8,128)S(1)} all-gather(f32[32,256]{1,0:T(8,128)S(1)} %copy.29), channel_id=2, replica_groups=mesh['rows'=32,'cols'=16] {'cols'}, dimensions={0}, use_global_device_ids=true | all-gather | bytes 557056 | tf_op jit(solution)/shard_map/all_gather | solution.py:167
  102.9 1.3 fusion.39
  104.2 4.8 %fusion.26 = f32[256,256]{1,0:T(8,128)} fusion(f32[256,2048]{1,0:T(8,128)} %all-gather.6.cloned.1.call-done), kind=kOutput, calls=%fused_computation.122 | convolution fusion | flops 1610612736 | bytes 2359296 | tf_op jit(solution)/shard_map/dot_general | solution.py:140
  109.0 12.4 %collective-permute-start.5 = (f32[256,256]{1,0:T(8,128)}, f32[256,256]{1,0:T(8,128)}, u32[]{:S(2)}, u32[]{:S(2)}) collective-permute-start(f32[256,256]{1,0:T(8,128)} %fusion.26), channel_id=1, source_target_pairs={{0,16},{16,0},{32,48},{48,32},{64,80},{80,64},{96,112},{112,96},{1... | collective-permute-start | bytes 786440 | tf_op jit(solution)/shard_map/ppermute | solution.py:12
  122.3 29.5 %shard_map.101 = f32[256,256]{1,0:T(8,128)} custom-call(f32[256,256]{1,0:T(8,128)} %bitcast.99), custom_call_target="tpu_custom_call" | custom-call | tf_op jit(solution)/shard_map/pallas_call | solution.py:125
  151.7 1.1 copy.31
  161.3 1.1 fusion.8
  162.4 1.9 fusion.32
  164.3 6.1 %convolution_subtract_fusion.1 = f32[2048,256]{1,0:T(8,128)S(1)} fusion(f32[2048,256]{1,0:T(8,128)} %param.7, f32[256,2048]{1,0:T(8,128)} %all-gather.4.cloned.1.call-done, f32[256,256]{1,0:T(8,128)S(1)} %copy-done), kind=kOutput, calls=%fused_computation.3 | convolution fusion | flops 1611137024 | bytes 6553600 | tf_op jit(solution)/shard_map/dot_general | solution.py:134
  172.3 3.6 %collective-permute-start.6 = (f32[256,256]{1,0:T(8,128)S(1)}, f32[256,256]{1,0:T(8,128)S(1)}, u32[]{:S(2)}, u32[]{:S(2)}) collective-permute-start(f32[256,256]{1,0:T(8,128)S(1)} %add.390), channel_id=1, source_target_pairs={{0,32},{16,48},{32,0},{48,16},{64,96},{80,112},{96,64},{112,80},{1... | collective-permute-start | bytes 786440 | tf_op jit(solution)/shard_map/ppermute | solution.py:12
  176.8 5.8 %collective-permute-done.6 = f32[256,256]{1,0:T(8,128)S(1)} collective-permute-done((f32[256,256]{1,0:T(8,128)S(1)}, f32[256,256]{1,0:T(8,128)S(1)}, u32[]{:S(2)}, u32[]{:S(2)}) %collective-permute-start.6) | collective-permute-done | bytes 262176 | tf_op jit(solution)/shard_map/ppermute | solution.py:12
  182.6 4.7 %collective-permute-start.7 = (f32[256,256]{1,0:T(8,128)S(1)}, f32[256,256]{1,0:T(8,128)S(1)}, u32[]{:S(2)}, u32[]{:S(2)}) collective-permute-start(f32[256,256]{1,0:T(8,128)S(1)} %add.391), channel_id=1, source_target_pairs={{0,64},{16,80},{32,96},{48,112},{64,0},{80,16},{96,32},{112,48},{1... | collective-permute-start | bytes 786440 | tf_op jit(solution)/shard_map/ppermute | solution.py:12
  188.1 5.2 %collective-permute-done.7 = f32[256,256]{1,0:T(8,128)S(1)} collective-permute-done((f32[256,256]{1,0:T(8,128)S(1)}, f32[256,256]{1,0:T(8,128)S(1)}, u32[]{:S(2)}, u32[]{:S(2)}) %collective-permute-start.7) | collective-permute-done | bytes 262176 | tf_op jit(solution)/shard_map/ppermute | solution.py:12
  193.3 2.6 %collective-permute-start.8 = (f32[256,256]{1,0:T(8,128)S(1)}, f32[256,256]{1,0:T(8,128)S(1)}, u32[]{:S(2)}, u32[]{:S(2)}) collective-permute-start(f32[256,256]{1,0:T(8,128)S(1)} %add.392), channel_id=1, source_target_pairs={{0,128},{16,144},{32,160},{48,176},{64,192},{80,208},{96,224},{112... | collective-permute-start | bytes 786440 | tf_op jit(solution)/shard_map/ppermute | solution.py:12
  196.7 4.8 %collective-permute-done.8 = f32[256,256]{1,0:T(8,128)S(1)} collective-permute-done((f32[256,256]{1,0:T(8,128)S(1)}, f32[256,256]{1,0:T(8,128)S(1)}, u32[]{:S(2)}, u32[]{:S(2)}) %collective-permute-start.8) | collective-permute-done | bytes 262176 | tf_op jit(solution)/shard_map/ppermute | solution.py:12
  201.6 4.3 %collective-permute-start.9 = (f32[256,256]{1,0:T(8,128)S(1)}, f32[256,256]{1,0:T(8,128)}, u32[]{:S(2)}, u32[]{:S(2)}) collective-permute-start(f32[256,256]{1,0:T(8,128)S(1)} %add.393), channel_id=1, source_target_pairs={{0,256},{16,272},{32,288},{48,304},{64,320},{80,336},{96,352},{112... | collective-permute-start | bytes 786440 | tf_op jit(solution)/shard_map/ppermute | solution.py:12
  205.8 4.8 %convolution_subtract_fusion = f32[2048,256]{1,0:T(8,128)} fusion(f32[2048,256]{1,0:T(8,128)S(1)} %convolution_subtract_fusion.1, f32[256,2048]{1,0:T(8,128)S(1)} %fusion.32, f32[256,256]{1,0:T(8,128)S(1)} %fusion.12), kind=kOutput, calls=%fused_computation.2 | convolution fusion | flops 1611137024 | bytes 6553600 | tf_op jit(solution)/shard_map/dot_general | solution.py:134
  212.2 1.4 fusion.13
  (105 shorter events, 22.0 us)
Async XLA Ops:
  7.2 95.8 %copy-start = (f32[256,256]{1,0:T(8,128)S(1)}, f32[256,256]{1,0:T(8,128)}, u32[]{:S(2)}) copy-start(f32[256,256]{1,0:T(8,128)} %param.9) | copy-start | bytes 786436
  7.2 7.7 %copy-start.9 = (s32[1,256]{1,0:T(1,128)S(1)}, s32[1,256]{1,0:T(1,128)}, u32[]{:S(2)}) copy-start(s32[1,256]{1,0:T(1,128)} %param.10) | copy-start | bytes 3076
  7.2 7.8 %copy-start.2 = (f32[2048,256]{1,0:T(8,128)S(1)}, f32[2048,256]{1,0:T(8,128)}, u32[]{:S(2)}) copy-start(f32[2048,256]{1,0:T(8,128)} %param.7) | copy-start | bytes 6291460
  7.2 97.0 %all-gather.6.cloned.1.call-start = ((), (), s32[]{:S(2)}) async-start(), calls=%async_computation.1 | async-start | bytes 2228224 | tf_op jit(solution)/shard_map/all_gather | solution.py:174
  7.9 156.4 %all-gather.4.cloned.1.call-start = ((), (), s32[]{:S(2)}) async-start(), calls=%async_computation | async-start | bytes 2228224 | tf_op jit(solution)/shard_map/all_gather | solution.py:173
  18.7 10.1 %collective-permute-start = (f32[256,288]{1,0:T(8,128)S(1)}, f32[256,288]{1,0:T(8,128)S(1)}, u32[]{:S(2)}, u32[]{:S(2)}) collective-permute-start(f32[256,288]{1,0:T(8,128)S(1)} %maximum_select_fusion), channel_id=1, source_target_pairs={{0,16},{16,0},{32,48},{48,32},{64,80},{80,64},{96,112},{112,96},{1... | collective-permute-start | bytes 884744 | tf_op jit(solution)/shard_map/ppermute | solution.py:12
  28.9 12.3 %collective-permute-start.1 = (f32[256,288]{1,0:T(8,128)S(1)}, f32[256,288]{1,0:T(8,128)S(1)}, u32[]{:S(2)}, u32[]{:S(2)}) collective-permute-start(f32[256,288]{1,0:T(8,128)S(1)} %add.367), channel_id=1, source_target_pairs={{0,32},{16,48},{32,0},{48,16},{64,96},{80,112},{96,64},{112,80},{1... | collective-permute-start | bytes 884744 | tf_op jit(solution)/shard_map/ppermute | solution.py:12
  41.3 12.9 %collective-permute-start.2 = (f32[256,288]{1,0:T(8,128)S(1)}, f32[256,288]{1,0:T(8,128)S(1)}, u32[]{:S(2)}, u32[]{:S(2)}) collective-permute-start(f32[256,288]{1,0:T(8,128)S(1)} %add.368), channel_id=1, source_target_pairs={{0,64},{16,80},{32,96},{48,112},{64,0},{80,16},{96,32},{112,48},{1... | collective-permute-start | bytes 884744 | tf_op jit(solution)/shard_map/ppermute | solution.py:12
  54.2 10.6 %collective-permute-start.3 = (f32[256,288]{1,0:T(8,128)S(1)}, f32[256,288]{1,0:T(8,128)S(1)}, u32[]{:S(2)}, u32[]{:S(2)}) collective-permute-start(f32[256,288]{1,0:T(8,128)S(1)} %add.369), channel_id=1, source_target_pairs={{0,128},{16,144},{32,160},{48,176},{64,192},{80,208},{96,224},{112... | collective-permute-start | bytes 884744 | tf_op jit(solution)/shard_map/ppermute | solution.py:12
  64.8 11.2 %collective-permute-start.4 = (f32[256,288]{1,0:T(8,128)S(1)}, f32[256,288]{1,0:T(8,128)S(1)}, u32[]{:S(2)}, u32[]{:S(2)}) collective-permute-start(f32[256,288]{1,0:T(8,128)S(1)} %add.370), channel_id=1, source_target_pairs={{0,256},{16,272},{32,288},{48,304},{64,320},{80,336},{96,352},{112... | collective-permute-start | bytes 884744 | tf_op jit(solution)/shard_map/ppermute | solution.py:12
  109.0 62.2 %collective-permute-start.5 = (f32[256,256]{1,0:T(8,128)}, f32[256,256]{1,0:T(8,128)}, u32[]{:S(2)}, u32[]{:S(2)}) collective-permute-start(f32[256,256]{1,0:T(8,128)} %fusion.26), channel_id=1, source_target_pairs={{0,16},{16,0},{32,48},{48,32},{64,80},{80,64},{96,112},{112,96},{1... | collective-permute-start | bytes 786440 | tf_op jit(solution)/shard_map/ppermute | solution.py:12
  152.9 4.1 %copy-start.5 = (f32[256,256]{0,1:T(8,128)}, f32[256,256]{0,1:T(8,128)S(1)}, u32[]{:S(2)}) copy-start(f32[256,256]{0,1:T(8,128)S(1)} %get-tuple-element.29) | copy-start | bytes 786436
  153.4 1.9 copy-start.3
  159.5 2.8 %copy-start.1 = (f32[256,2048]{1,0:T(8,128)S(1)}, f32[256,2048]{1,0:T(8,128)}, u32[]{:S(2)}) copy-start(f32[256,2048]{1,0:T(8,128)} %all-gather.6.cloned.1.call-done) | copy-start | bytes 6291460
  164.3 6.5 %copy-start.8 = (f32[256,256]{1,0:T(8,128)S(1)}, f32[256,256]{1,0:T(8,128)}, u32[]{:S(2)}) copy-start(f32[256,256]{1,0:T(8,128)} %fusion.8) | copy-start | bytes 786436
  172.3 10.2 %collective-permute-start.6 = (f32[256,256]{1,0:T(8,128)S(1)}, f32[256,256]{1,0:T(8,128)S(1)}, u32[]{:S(2)}, u32[]{:S(2)}) collective-permute-start(f32[256,256]{1,0:T(8,128)S(1)} %add.390), channel_id=1, source_target_pairs={{0,32},{16,48},{32,0},{48,16},{64,96},{80,112},{96,64},{112,80},{1... | collective-permute-start | bytes 786440 | tf_op jit(solution)/shard_map/ppermute | solution.py:12
  176.8 19.5 %copy-start.4 = (f32[256,256]{1,0:T(8,128)S(1)}, f32[256,256]{1,0:T(8,128)}, u32[]{:S(2)}) copy-start(f32[256,256]{1,0:T(8,128)} %fusion.39) | copy-start | bytes 786436
  182.6 10.6 %collective-permute-start.7 = (f32[256,256]{1,0:T(8,128)S(1)}, f32[256,256]{1,0:T(8,128)S(1)}, u32[]{:S(2)}, u32[]{:S(2)}) collective-permute-start(f32[256,256]{1,0:T(8,128)S(1)} %add.391), channel_id=1, source_target_pairs={{0,64},{16,80},{32,96},{48,112},{64,0},{80,16},{96,32},{112,48},{1... | collective-permute-start | bytes 786440 | tf_op jit(solution)/shard_map/ppermute | solution.py:12
  193.3 8.2 %collective-permute-start.8 = (f32[256,256]{1,0:T(8,128)S(1)}, f32[256,256]{1,0:T(8,128)S(1)}, u32[]{:S(2)}, u32[]{:S(2)}) collective-permute-start(f32[256,256]{1,0:T(8,128)S(1)} %add.392), channel_id=1, source_target_pairs={{0,128},{16,144},{32,160},{48,176},{64,192},{80,208},{96,224},{112... | collective-permute-start | bytes 786440 | tf_op jit(solution)/shard_map/ppermute | solution.py:12
  196.7 9.1 %copy-start.7 = (f32[256,256]{1,0:T(8,128)}, f32[256,256]{1,0:T(8,128)S(1)}, u32[]{:S(2)}) copy-start(f32[256,256]{1,0:T(8,128)S(1)} %fusion.12) | copy-start | bytes 786436
  201.5 9.1 %copy-start.6 = (f32[256,256]{0,1:T(8,128)S(1)}, f32[256,256]{0,1:T(8,128)}, u32[]{:S(2)}) copy-start(f32[256,256]{0,1:T(8,128)} %copy-done.5) | copy-start | bytes 786436
  201.6 10.6 %collective-permute-start.9 = (f32[256,256]{1,0:T(8,128)S(1)}, f32[256,256]{1,0:T(8,128)}, u32[]{:S(2)}, u32[]{:S(2)}) collective-permute-start(f32[256,256]{1,0:T(8,128)S(1)} %add.393), channel_id=1, source_target_pairs={{0,256},{16,272},{32,288},{48,304},{64,320},{80,336},{96,352},{112... | collective-permute-start | bytes 786440 | tf_op jit(solution)/shard_map/ppermute | solution.py:12
Sparse Core Ops, SparseCore 0:
  10.1 69.9 all-gather.5
  82.2 69.6 all-gather.3

commit v9 on v7

--- a/solution.py
+++ b/solution.py
@@ -176,12 +176,13 @@
     panel_full = lax.all_gather(panel_t, "cols", axis=0, tiled=True)
     lower_left, upper_left = factor(block_t.T)
     inverse = upper_inverse(upper_left)
-    upper_right = product(unit_lower_inverse(lower_left), middle_pivots)
     lower_full = jnp.dot(inverse.T, panel_full, precision=full_precision)
     lower_tile = lax.dynamic_slice_in_dim(lower_full, own_column * slab_rows, slab_rows, 0)
+    gram_rows = contract_second(lower_tile, lower_full)
+    lower_left, gram_rows = lax.optimization_barrier((lower_left, gram_rows))
+    gram = butterfly_sum(gram_rows, "rows") / (rows_here * row_devices)
+    upper_right = product(unit_lower_inverse(lower_left), middle_pivots)
     updated = middle - contract_first(lower_full, upper_right)
-    gram_rows = contract_second(lower_tile, lower_full)
-    gram = butterfly_sum(gram_rows, "rows") / (rows_here * row_devices)
     return (lower_tile, upper_left, upper_right, updated, gram)
 
 

time: 204 us -> 207 us (1.015)
  starting transfers between devices: 43.3 us -> 45.9 us
    ppermute x10, starting transfers between devices: 43.3 us -> 45.8 us  [from_partner(): lax.ppermute(shard, axis, [(i, i ^ 1 << apart) for i in range(lax.axis_si...]
  transfers between devices with their start and end apart: 12 -> 12, of which waited for: 8 -> 8; matrix products, arithmetic and copies ran while one was open for 22% -> 22% of each run, Pallas kernels for 15% -> 14%
where the time goes in v9:
time: 207 us; the launch traced here: 204 us
  starting transfers between devices  45.9 us (22%)
  waiting for transfers between devices  43.6 us (21%)
  matrix products  29.8 us (14%)
  Pallas kernels  29.3 us (14%)
  blocking collectives  26.2 us (13%)
  between operations  14.7 us (7%)
  local copies, waits for them, and re-layouts  9.02 us (4%)
  other arithmetic  5.9 us (3%)
    ppermute x10, starting transfers between devices, from_partner(): lax.ppermute(shard, axis, [(i, i ^ 1 << apart) for i in range(lax.axis_si...  45.8 us
    ppermute x10, waiting for transfers between devices, from_partner(): lax.ppermute(shard, axis, [(i, i ^ 1 << apart) for i in range(lax.axis_si...  42.9 us
    pallas_call x1, Pallas kernels, factor(): pl.pallas_call(elimination_kernel, out_shape=jax.ShapeDtypeStruct(matrix....  29.3 us
    all_gather x1, blocking collectives, body(): lax.all_gather(pivot_data[:, own_trailing.shape[1]:].T, 'cols', axis=0, t...  26.2 us
    dot_general x29, matrix products, product(): return jnp.dot(left_side, right_side, precision=full_precision)  12.5 us
    dot_general x3, matrix products, contract_first(): lax.dot_general(left_side, right_side, (((0,), (0,)), ((), ())), precisio...  12 us
  transfers between devices with their start and end apart: 12, of which 8 were waited for; matrix products, arithmetic and copies ran while one was open for 22% of the time, Pallas kernels for 14%

profile of v9, /device:TPU:1, one launch (start us, length us, event | category | flops | bytes accessed | tf_op | source)
XLA Modules:
  0.0 204.4 jit_solution(16348464013948821834)
XLA Ops:
  8.0 1.2 fusion.16
  9.3 0.9 fusion.17
  10.7 1.7 pad_maximum_fusion
  12.4 1.3 copy.28
  15.0 1.7 gather_fusion
  17.5 1.1 broadcast_select_fusion
  18.7 8.8 %collective-permute-start = (f32[256,288]{1,0:T(8,128)S(1)}, f32[256,288]{1,0:T(8,128)S(1)}, u32[]{:S(2)}, u32[]{:S(2)}) collective-permute-start(f32[256,288]{1,0:T(8,128)S(1)} %maximum_select_fusion), channel_id=1, source_target_pairs={{0,16},{16,0},{32,48},{48,32},{64,80},{80,64},{96,112},{112,96},{1... | collective-permute-start | bytes 884744 | tf_op jit(solution)/shard_map/ppermute | solution.py:12
  27.5 1.3 collective-permute-done
  28.9 1.9 collective-permute-start.1
  30.8 10.4 %collective-permute-done.1 = f32[256,288]{1,0:T(8,128)S(1)} collective-permute-done((f32[256,288]{1,0:T(8,128)S(1)}, f32[256,288]{1,0:T(8,128)S(1)}, u32[]{:S(2)}, u32[]{:S(2)}) %collective-permute-start.1) | collective-permute-done | bytes 294944 | tf_op jit(solution)/shard_map/ppermute | solution.py:12
  41.3 1.9 collective-permute-start.2
  43.2 11.0 %collective-permute-done.2 = f32[256,288]{1,0:T(8,128)S(1)} collective-permute-done((f32[256,288]{1,0:T(8,128)S(1)}, f32[256,288]{1,0:T(8,128)S(1)}, u32[]{:S(2)}, u32[]{:S(2)}) %collective-permute-start.2) | collective-permute-done | bytes 294944 | tf_op jit(solution)/shard_map/ppermute | solution.py:12
  54.2 1.9 collective-permute-start.3
  56.4 8.4 %collective-permute-done.3 = f32[256,288]{1,0:T(8,128)S(1)} collective-permute-done((f32[256,288]{1,0:T(8,128)S(1)}, f32[256,288]{1,0:T(8,128)S(1)}, u32[]{:S(2)}, u32[]{:S(2)}) %collective-permute-start.3) | collective-permute-done | bytes 294944 | tf_op jit(solution)/shard_map/ppermute | solution.py:12
  64.8 1.9 collective-permute-start.4
  67.0 9.0 %collective-permute-done.4 = f32[256,288]{1,0:T(8,128)S(1)} collective-permute-done((f32[256,288]{1,0:T(8,128)S(1)}, f32[256,288]{1,0:T(8,128)S(1)}, u32[]{:S(2)}, u32[]{:S(2)}) %collective-permute-start.4) | collective-permute-done | bytes 294944 | tf_op jit(solution)/shard_map/ppermute | solution.py:12
  76.1 26.2 %all-gather = f32[512,256]{1,0:T(8,128)S(1)} all-gather(f32[32,256]{1,0:T(8,128)S(1)} %copy.29), channel_id=2, replica_groups=mesh['rows'=32,'cols'=16] {'cols'}, dimensions={0}, use_global_device_ids=true | all-gather | bytes 557056 | tf_op jit(solution)/shard_map/all_gather | solution.py:167
  103.2 29.3 %shard_map.101 = f32[256,256]{1,0:T(8,128)} custom-call(f32[256,256]{1,0:T(8,128)} %bitcast.97), custom_call_target="tpu_custom_call" | custom-call | tf_op jit(solution)/shard_map/pallas_call | solution.py:125
  132.5 1.1 copy.31
  139.9 1.3 fusion.31
  141.9 3.5 %fusion.23 = f32[256,2048]{1,0:T(8,128)S(1)} fusion(f32[256,256]{1,0:T(8,128)S(1)} %convolution_divide_fusion, f32[256,2048]{1,0:T(8,128)} %all-gather.4.cloned.1.call-done), kind=kOutput, calls=%fused_computation.119 | convolution fusion | flops 1610612736 | bytes 4456448 | tf_op jit(solution)/shard_map/dot_general | solution.py:179
  145.5 1.7 fusion.24
  147.2 13.4 %collective-permute-start.5 = (f32[16,256]{1,0:T(8,128)S(1)}, f32[16,256]{1,0:T(8,128)S(1)}, u32[]{:S(2)}, u32[]{:S(2)}) collective-permute-start(f32[16,256]{1,0:T(8,128)S(1)} %fusion.24), channel_id=1, source_target_pairs={{0,16},{16,0},{32,48},{48,32},{64,80},{80,64},{96,112},{112,96},{1... | collective-permute-start | bytes 49160 | tf_op jit(solution)/shard_map/ppermute | solution.py:12
  164.6 1.1 fusion.10
  165.8 5.9 %convolution_subtract_fusion.1 = f32[2048,256]{1,0:T(8,128)S(1)} fusion(f32[2048,256]{1,0:T(8,128)} %param.7, f32[256,2048]{1,0:T(8,128)} %all-gather.6.cloned.1.call-done, f32[256,256]{1,0:T(8,128)S(1)} %copy-done), kind=kOutput, calls=%fused_computation.3 | convolution fusion | flops 1611137024 | bytes 6553600 | tf_op jit(solution)/shard_map/dot_general | solution.py:134
  172.1 3.1 %collective-permute-start.6 = (f32[16,256]{1,0:T(8,128)S(1)}, f32[16,256]{1,0:T(8,128)S(1)}, u32[]{:S(2)}, u32[]{:S(2)}) collective-permute-start(f32[16,256]{1,0:T(8,128)S(1)} %add.389), channel_id=1, source_target_pairs={{0,32},{16,48},{32,0},{48,16},{64,96},{80,112},{96,64},{112,80},{1... | collective-permute-start | bytes 49160 | tf_op jit(solution)/shard_map/ppermute | solution.py:12
  175.7 0.9 collective-permute-done.6
  176.6 4.6 %collective-permute-start.7 = (f32[16,256]{1,0:T(8,128)S(1)}, f32[16,256]{1,0:T(8,128)S(1)}, u32[]{:S(2)}, u32[]{:S(2)}) collective-permute-start(f32[16,256]{1,0:T(8,128)S(1)} %add.390), channel_id=1, source_target_pairs={{0,64},{16,80},{32,96},{48,112},{64,0},{80,16},{96,32},{112,48},{1... | collective-permute-start | bytes 49160 | tf_op jit(solution)/shard_map/ppermute | solution.py:12
  181.6 1.0 collective-permute-done.7
  182.6 3.2 %collective-permute-start.8 = (f32[16,256]{1,0:T(8,128)S(1)}, f32[16,256]{1,0:T(8,128)S(1)}, u32[]{:S(2)}, u32[]{:S(2)}) collective-permute-start(f32[16,256]{1,0:T(8,128)S(1)} %add.391), channel_id=1, source_target_pairs={{0,128},{16,144},{32,160},{48,176},{64,192},{80,208},{96,224},{112... | collective-permute-start | bytes 49160 | tf_op jit(solution)/shard_map/ppermute | solution.py:12
  187.1 5.1 %collective-permute-start.9 = (f32[16,256]{1,0:T(8,128)S(1)}, f32[16,256]{1,0:T(8,128)S(1)}, u32[]{:S(2)}, u32[]{:S(2)}) collective-permute-start(f32[16,256]{1,0:T(8,128)S(1)} %add.392), channel_id=1, source_target_pairs={{0,256},{16,272},{32,288},{48,304},{64,320},{80,336},{96,352},{112... | collective-permute-start | bytes 49160 | tf_op jit(solution)/shard_map/ppermute | solution.py:12
  192.1 4.8 %convolution_subtract_fusion = f32[2048,256]{1,0:T(8,128)} fusion(f32[2048,256]{1,0:T(8,128)S(1)} %convolution_subtract_fusion.1, f32[256,2048]{1,0:T(8,128)S(1)} %fusion.23, f32[256,256]{1,0:T(8,128)S(1)} %fusion.12), kind=kOutput, calls=%fused_computation.2 | convolution fusion | flops 1611137024 | bytes 6553600 | tf_op jit(solution)/shard_map/dot_general | solution.py:134
  (101 shorter events, 19.1 us)
Async XLA Ops:
  7.2 132.7 %copy-start = (f32[256,256]{1,0:T(8,128)S(1)}, f32[256,256]{1,0:T(8,128)}, u32[]{:S(2)}) copy-start(f32[256,256]{1,0:T(8,128)} %param.9) | copy-start | bytes 786436
  7.2 7.7 %copy-start.7 = (s32[1,256]{1,0:T(1,128)S(1)}, s32[1,256]{1,0:T(1,128)}, u32[]{:S(2)}) copy-start(s32[1,256]{1,0:T(1,128)} %param.10) | copy-start | bytes 3076
  7.2 7.8 %copy-start.1 = (f32[2048,256]{1,0:T(8,128)S(1)}, f32[2048,256]{1,0:T(8,128)}, u32[]{:S(2)}) copy-start(f32[2048,256]{1,0:T(8,128)} %param.7) | copy-start | bytes 6291460
  7.2 134.7 %all-gather.4.cloned.1.call-start = ((), (), s32[]{:S(2)}) async-start(), calls=%async_computation | async-start | bytes 2228224 | tf_op jit(solution)/shard_map/all_gather | solution.py:176
  7.9 157.8 %all-gather.6.cloned.1.call-start = ((), (), s32[]{:S(2)}) async-start(), calls=%async_computation.1 | async-start | bytes 2228224 | tf_op jit(solution)/shard_map/all_gather | solution.py:174
  18.7 10.1 %collective-permute-start = (f32[256,288]{1,0:T(8,128)S(1)}, f32[256,288]{1,0:T(8,128)S(1)}, u32[]{:S(2)}, u32[]{:S(2)}) collective-permute-start(f32[256,288]{1,0:T(8,128)S(1)} %maximum_select_fusion), channel_id=1, source_target_pairs={{0,16},{16,0},{32,48},{48,32},{64,80},{80,64},{96,112},{112,96},{1... | collective-permute-start | bytes 884744 | tf_op jit(solution)/shard_map/ppermute | solution.py:12
  28.9 12.3 %collective-permute-start.1 = (f32[256,288]{1,0:T(8,128)S(1)}, f32[256,288]{1,0:T(8,128)S(1)}, u32[]{:S(2)}, u32[]{:S(2)}) collective-permute-start(f32[256,288]{1,0:T(8,128)S(1)} %add.366), channel_id=1, source_target_pairs={{0,32},{16,48},{32,0},{48,16},{64,96},{80,112},{96,64},{112,80},{1... | collective-permute-start | bytes 884744 | tf_op jit(solution)/shard_map/ppermute | solution.py:12
  41.3 12.9 %collective-permute-start.2 = (f32[256,288]{1,0:T(8,128)S(1)}, f32[256,288]{1,0:T(8,128)S(1)}, u32[]{:S(2)}, u32[]{:S(2)}) collective-permute-start(f32[256,288]{1,0:T(8,128)S(1)} %add.367), channel_id=1, source_target_pairs={{0,64},{16,80},{32,96},{48,112},{64,0},{80,16},{96,32},{112,48},{1... | collective-permute-start | bytes 884744 | tf_op jit(solution)/shard_map/ppermute | solution.py:12
  54.2 10.6 %collective-permute-start.3 = (f32[256,288]{1,0:T(8,128)S(1)}, f32[256,288]{1,0:T(8,128)S(1)}, u32[]{:S(2)}, u32[]{:S(2)}) collective-permute-start(f32[256,288]{1,0:T(8,128)S(1)} %add.368), channel_id=1, source_target_pairs={{0,128},{16,144},{32,160},{48,176},{64,192},{80,208},{96,224},{112... | collective-permute-start | bytes 884744 | tf_op jit(solution)/shard_map/ppermute | solution.py:12
  64.8 11.2 %collective-permute-start.4 = (f32[256,288]{1,0:T(8,128)S(1)}, f32[256,288]{1,0:T(8,128)S(1)}, u32[]{:S(2)}, u32[]{:S(2)}) collective-permute-start(f32[256,288]{1,0:T(8,128)S(1)} %add.369), channel_id=1, source_target_pairs={{0,256},{16,272},{32,288},{48,304},{64,320},{80,336},{96,352},{112... | collective-permute-start | bytes 884744 | tf_op jit(solution)/shard_map/ppermute | solution.py:12
  138.3 3.0 %copy-start.2 = (f32[256,256]{1,0:T(8,128)S(1)}, f32[256,256]{1,0:T(8,128)}, u32[]{:S(2)}) copy-start(f32[256,256]{1,0:T(8,128)} %shard_map.101) | copy-start | bytes 786436
  145.4 16.3 %copy-start.6 = (f32[16,2048]{1,0:T(8,128)}, f32[16,2048]{1,0:T(8,128)S(1)}, u32[]{:S(2)}) copy-start(f32[16,2048]{1,0:T(8,128)S(1)} %constant_dynamic-slice_fusion) | copy-start | bytes 393220
  147.2 24.9 %collective-permute-start.5 = (f32[16,256]{1,0:T(8,128)S(1)}, f32[16,256]{1,0:T(8,128)S(1)}, u32[]{:S(2)}, u32[]{:S(2)}) collective-permute-start(f32[16,256]{1,0:T(8,128)S(1)} %fusion.24), channel_id=1, source_target_pairs={{0,16},{16,0},{32,48},{48,32},{64,80},{80,64},{96,112},{112,96},{1... | collective-permute-start | bytes 49160 | tf_op jit(solution)/shard_map/ppermute | solution.py:12
  165.8 9.5 %copy-start.5 = (f32[256,256]{1,0:T(8,128)S(1)}, f32[256,256]{1,0:T(8,128)}, u32[]{:S(2)}) copy-start(f32[256,256]{1,0:T(8,128)} %fusion.10) | copy-start | bytes 786436
  171.7 14.1 %copy-start.3 = (f32[256,256]{1,0:T(8,128)S(1)}, f32[256,256]{1,0:T(8,128)}, u32[]{:S(2)}) copy-start(f32[256,256]{1,0:T(8,128)} %fusion.31) | copy-start | bytes 786436
  172.1 4.5 %collective-permute-start.6 = (f32[16,256]{1,0:T(8,128)S(1)}, f32[16,256]{1,0:T(8,128)S(1)}, u32[]{:S(2)}, u32[]{:S(2)}) collective-permute-start(f32[16,256]{1,0:T(8,128)S(1)} %add.389), channel_id=1, source_target_pairs={{0,32},{16,48},{32,0},{48,16},{64,96},{80,112},{96,64},{112,80},{1... | collective-permute-start | bytes 49160 | tf_op jit(solution)/shard_map/ppermute | solution.py:12
  176.6 6.0 %collective-permute-start.7 = (f32[16,256]{1,0:T(8,128)S(1)}, f32[16,256]{1,0:T(8,128)S(1)}, u32[]{:S(2)}, u32[]{:S(2)}) collective-permute-start(f32[16,256]{1,0:T(8,128)S(1)} %add.390), channel_id=1, source_target_pairs={{0,64},{16,80},{32,96},{48,112},{64,0},{80,16},{96,32},{112,48},{1... | collective-permute-start | bytes 49160 | tf_op jit(solution)/shard_map/ppermute | solution.py:12
  182.6 4.5 %collective-permute-start.8 = (f32[16,256]{1,0:T(8,128)S(1)}, f32[16,256]{1,0:T(8,128)S(1)}, u32[]{:S(2)}, u32[]{:S(2)}) collective-permute-start(f32[16,256]{1,0:T(8,128)S(1)} %add.391), channel_id=1, source_target_pairs={{0,128},{16,144},{32,160},{48,176},{64,192},{80,208},{96,224},{112... | collective-permute-start | bytes 49160 | tf_op jit(solution)/shard_map/ppermute | solution.py:12
  186.2 10.7 %copy-start.4 = (f32[256,256]{1,0:T(8,128)}, f32[256,256]{1,0:T(8,128)S(1)}, u32[]{:S(2)}) copy-start(f32[256,256]{1,0:T(8,128)S(1)} %fusion.12) | copy-start | bytes 786436
  187.1 9.9 %collective-permute-start.9 = (f32[16,256]{1,0:T(8,128)S(1)}, f32[16,256]{1,0:T(8,128)S(1)}, u32[]{:S(2)}, u32[]{:S(2)}) collective-permute-start(f32[16,256]{1,0:T(8,128)S(1)} %add.392), channel_id=1, source_target_pairs={{0,256},{16,272},{32,288},{48,304},{64,320},{80,336},{96,352},{112... | collective-permute-start | bytes 49160 | tf_op jit(solution)/shard_map/ppermute | solution.py:12
Sparse Core Ops, SparseCore 0:
  10.1 69.9 all-gather.3
  82.2 70.0 all-gather.5

commit v10 on v7

--- a/solution.py
+++ b/solution.py
@@ -159,14 +159,13 @@
     leaf_group, leaf_slot = trace_pivots(merge_picks, row_devices)
     owner_mask = leaf_group == own_row
     local_rows = lookup(leaf_picks, jnp.zeros_like(leaf_slot), leaf_slot)
+    own_columns = jnp.take(jnp.concatenate([panel_t, prev_lower_t], 0), local_rows, axis=1)
+    pivot_part = butterfly_sum(jnp.where(owner_mask[None, :], own_columns, 0.0), "rows")
+    pivot_columns = lax.all_gather(pivot_part, "cols", axis=0, tiled=False)
     own_trailing = jnp.take(trailing, local_rows, axis=0)
-    own_columns = jnp.take(jnp.concatenate([panel_t, prev_lower_t], 0), local_rows, axis=1)
-    own_pivots = jnp.concatenate([own_trailing, own_columns.T], 1)
-    pivot_data = butterfly_sum(jnp.where(owner_mask[:, None], own_pivots, 0.0), "rows")
-    pivot_trailing = pivot_data[:, : own_trailing.shape[1]]
-    pivot_columns = lax.all_gather(
-        pivot_data[:, own_trailing.shape[1] :].T, "cols", axis=0, tiled=False
-    )
+    own_trailing = jnp.where(owner_mask[:, None], own_trailing, 0.0)
+    own_trailing, pivot_columns = lax.optimization_barrier((own_trailing, pivot_columns))
+    pivot_trailing = butterfly_sum(own_trailing, "rows")
     block_t = pivot_columns[:, :slab_rows].reshape(order, order)
     prev_pivots = pivot_columns[:, slab_rows:].reshape(order, order)
     middle_pivots = pivot_trailing - contract_first(prev_pivots, prev_upper)

time: 204 us -> 219 us (1.074)
  starting transfers between devices: 43.3 us -> 61.9 us
  waiting for transfers between devices: 42.9 us -> 35 us
  blocking collectives: 26.7 us -> 29.9 us
    ppermute x10 -> x15, starting transfers between devices: 43.3 us -> 61.8 us  [from_partner(): lax.ppermute(shard, axis, [(i, i ^ 1 << apart) for i in range(lax.axis_si...]
    ppermute x10 -> x15, waiting for transfers between devices: 42.2 us -> 34.2 us  [from_partner(): lax.ppermute(shard, axis, [(i, i ^ 1 << apart) for i in range(lax.axis_si...]
    all_gather x1, blocking collectives: 26.7 us -> 29.9 us  [body(): pivot_columns = lax.all_gather(pivot_part, 'cols', axis=0, tiled=False)]
  transfers between devices with their start and end apart: 12 -> 17, of which waited for: 8 -> 8; matrix products, arithmetic and copies ran while one was open for 22% -> 21% of each run, Pallas kernels for 15% -> 14%
where the time goes in v10:
time: 219 us; the launch traced here: 217 us
  starting transfers between devices  61.9 us (28%)
  waiting for transfers between devices  35 us (16%)
  matrix products  30.1 us (14%)
  blocking collectives  29.9 us (14%)
  Pallas kernels  29.3 us (13%)
  between operations  14.8 us (7%)
  local copies, waits for them, and re-layouts  10.1 us (5%)
  other arithmetic  5.53 us (3%)
    ppermute x15, starting transfers between devices, from_partner(): lax.ppermute(shard, axis, [(i, i ^ 1 << apart) for i in range(lax.axis_si...  61.8 us
    ppermute x15, waiting for transfers between devices, from_partner(): lax.ppermute(shard, axis, [(i, i ^ 1 << apart) for i in range(lax.axis_si...  34.2 us
    all_gather x1, blocking collectives, body(): pivot_columns = lax.all_gather(pivot_part, 'cols', axis=0, tiled=False)  29.9 us
    pallas_call x1, Pallas kernels, factor(): pl.pallas_call(elimination_kernel, out_shape=jax.ShapeDtypeStruct(matrix....  29.3 us
    dot_general x29, matrix products, product(): return jnp.dot(left_side, right_side, precision=full_precision)  13.5 us
    dot_general x3, matrix products, contract_first(): lax.dot_general(left_side, right_side, (((0,), (0,)), ((), ())), precisio...  11.3 us
  transfers between devices with their start and end apart: 17, of which 8 were waited for; matrix products, arithmetic and copies ran while one was open for 21% of the time, Pallas kernels for 14%

profile of v10, /device:TPU:1, one launch (start us, length us, event | category | flops | bytes accessed | tf_op | source)
XLA Modules:
  0.0 216.6 jit_solution(8234519965024330433)
XLA Ops:
  10.2 1.7 pad_maximum_fusion
  16.6 8.8 %collective-permute-start = (f32[32,256]{0,1:T(8,128)S(1)}, f32[32,256]{0,1:T(8,128)S(1)}, u32[]{:S(2)}, u32[]{:S(2)}) collective-permute-start(f32[32,256]{0,1:T(8,128)S(1)} %select_bitcast_fusion), channel_id=1, source_target_pairs={{0,16},{16,0},{32,48},{48,32},{64,80},{80,64},{96,112},{112,96},{1... | collective-permute-start | bytes 98312 | tf_op jit(solution)/shard_map/ppermute | solution.py:12
  26.7 1.9 collective-permute-start.1
  28.6 4.9 %collective-permute-done.1 = f32[32,256]{0,1:T(8,128)S(1)} collective-permute-done((f32[32,256]{0,1:T(8,128)S(1)}, f32[32,256]{0,1:T(8,128)S(1)}, u32[]{:S(2)}, u32[]{:S(2)}) %collective-permute-start.1) | collective-permute-done | bytes 32800 | tf_op jit(solution)/shard_map/ppermute | solution.py:12
  33.5 1.9 collective-permute-start.2
  35.4 5.3 %collective-permute-done.2 = f32[32,256]{0,1:T(8,128)S(1)} collective-permute-done((f32[32,256]{0,1:T(8,128)S(1)}, f32[32,256]{0,1:T(8,128)S(1)}, u32[]{:S(2)}, u32[]{:S(2)}) %collective-permute-start.2) | collective-permute-done | bytes 32800 | tf_op jit(solution)/shard_map/ppermute | solution.py:12
  40.7 1.9 collective-permute-start.3
  42.7 4.1 %collective-permute-done.3 = f32[32,256]{0,1:T(8,128)S(1)} collective-permute-done((f32[32,256]{0,1:T(8,128)S(1)}, f32[32,256]{0,1:T(8,128)S(1)}, u32[]{:S(2)}, u32[]{:S(2)}) %collective-permute-start.3) | collective-permute-done | bytes 32800 | tf_op jit(solution)/shard_map/ppermute | solution.py:12
  46.9 1.9 collective-permute-start.4
  49.1 4.9 %collective-permute-done.4 = f32[32,256]{0,1:T(8,128)S(1)} collective-permute-done((f32[32,256]{0,1:T(8,128)S(1)}, f32[32,256]{0,1:T(8,128)S(1)}, u32[]{:S(2)}, u32[]{:S(2)}) %collective-permute-start.4) | collective-permute-done | bytes 32800 | tf_op jit(solution)/shard_map/ppermute | solution.py:12
  54.2 29.9 %all-gather = f32[512,256]{1,0:T(8,128)S(1)} all-gather(f32[32,256]{1,0:T(8,128)S(1)} %copy.32), channel_id=2, replica_groups=mesh['rows'=32,'cols'=16] {'cols'}, dimensions={0}, use_global_device_ids=true | all-gather | bytes 557056 | tf_op jit(solution)/shard_map/all_gather | solution.py:164
  85.6 29.3 %shard_map.101 = f32[256,256]{1,0:T(8,128)} custom-call(f32[256,256]{1,0:T(8,128)} %bitcast.99), custom_call_target="tpu_custom_call" | custom-call | tf_op jit(solution)/shard_map/pallas_call | solution.py:125
  122.9 9.8 %collective-permute-start.5 = (f32[256,256]{0,1:T(8,128)S(1)}, f32[256,256]{0,1:T(8,128)S(1)}, u32[]{:S(2)}, u32[]{:S(2)}) collective-permute-start(f32[256,256]{0,1:T(8,128)S(1)} %select_select_fusion), channel_id=1, source_target_pairs={{0,16},{16,0},{32,48},{48,32},{64,80},{80,64},{96,112},{112,96},{1... | collective-permute-start | bytes 786440 | tf_op jit(solution)/shard_map/ppermute | solution.py:12
  134.8 3.7 %collective-permute-start.6 = (f32[256,256]{0,1:T(8,128)S(1)}, f32[256,256]{0,1:T(8,128)S(1)}, u32[]{:S(2)}, u32[]{:S(2)}) collective-permute-start(f32[256,256]{0,1:T(8,128)S(1)} %add.420), channel_id=1, source_target_pairs={{0,32},{16,48},{32,0},{48,16},{64,96},{80,112},{96,64},{112,80},{1... | collective-permute-start | bytes 786440 | tf_op jit(solution)/shard_map/ppermute | solution.py:12
  139.3 5.9 %collective-permute-done.6 = f32[256,256]{0,1:T(8,128)S(1)} collective-permute-done((f32[256,256]{0,1:T(8,128)S(1)}, f32[256,256]{0,1:T(8,128)S(1)}, u32[]{:S(2)}, u32[]{:S(2)}) %collective-permute-start.6) | collective-permute-done | bytes 262176 | tf_op jit(solution)/shard_map/ppermute | solution.py:12
  145.2 6.1 %collective-permute-start.7 = (f32[256,256]{0,1:T(8,128)S(1)}, f32[256,256]{0,1:T(8,128)S(1)}, u32[]{:S(2)}, u32[]{:S(2)}) collective-permute-start(f32[256,256]{0,1:T(8,128)S(1)} %add.421), channel_id=1, source_target_pairs={{0,64},{16,80},{32,96},{48,112},{64,0},{80,16},{96,32},{112,48},{1... | collective-permute-start | bytes 786440 | tf_op jit(solution)/shard_map/ppermute | solution.py:12
  152.1 5.2 %collective-permute-done.7 = f32[256,256]{0,1:T(8,128)S(1)} collective-permute-done((f32[256,256]{0,1:T(8,128)S(1)}, f32[256,256]{0,1:T(8,128)S(1)}, u32[]{:S(2)}, u32[]{:S(2)}) %collective-permute-start.7) | collective-permute-done | bytes 262176 | tf_op jit(solution)/shard_map/ppermute | solution.py:12
  157.3 3.1 %collective-permute-start.8 = (f32[256,256]{0,1:T(8,128)S(1)}, f32[256,256]{0,1:T(8,128)S(1)}, u32[]{:S(2)}, u32[]{:S(2)}) collective-permute-start(f32[256,256]{0,1:T(8,128)S(1)} %add.422), channel_id=1, source_target_pairs={{0,128},{16,144},{32,160},{48,176},{64,192},{80,208},{96,224},{112... | collective-permute-start | bytes 786440 | tf_op jit(solution)/shard_map/ppermute | solution.py:12
  160.4 1.3 convolution_divide_fusion
  162.1 3.5 %collective-permute-done.8 = f32[256,256]{0,1:T(8,128)S(1)} collective-permute-done((f32[256,256]{0,1:T(8,128)S(1)}, f32[256,256]{0,1:T(8,128)S(1)}, u32[]{:S(2)}, u32[]{:S(2)}) %collective-permute-start.8) | collective-permute-done | bytes 262176 | tf_op jit(solution)/shard_map/ppermute | solution.py:12
  165.7 6.3 %collective-permute-start.9 = (f32[256,256]{0,1:T(8,128)S(1)}, f32[256,256]{0,1:T(8,128)}, u32[]{:S(2)}, u32[]{:S(2)}) collective-permute-start(f32[256,256]{0,1:T(8,128)S(1)} %add.423), channel_id=1, source_target_pairs={{0,256},{16,272},{32,288},{48,304},{64,320},{80,336},{96,352},{112... | collective-permute-start | bytes 786440 | tf_op jit(solution)/shard_map/ppermute | solution.py:12
  172.1 3.6 %fusion.29 = f32[256,2048]{1,0:T(8,128)S(1)} fusion(f32[256,256]{1,0:T(8,128)} %convolution_divide_fusion, f32[256,2048]{1,0:T(8,128)} %all-gather.4.cloned.1.call-done), kind=kOutput, calls=%fused_computation.122 | convolution fusion | flops 1610612736 | bytes 4456448 | tf_op jit(solution)/shard_map/dot_general | solution.py:179
  175.7 1.7 fusion.37
  177.4 4.1 %collective-permute-start.10 = (f32[16,256]{1,0:T(8,128)S(1)}, f32[16,256]{1,0:T(8,128)S(1)}, u32[]{:S(2)}, u32[]{:S(2)}) collective-permute-start(f32[16,256]{1,0:T(8,128)S(1)} %fusion.37), channel_id=1, source_target_pairs={{0,16},{16,0},{32,48},{48,32},{64,80},{80,64},{96,112},{112,96},{1... | collective-permute-start | bytes 49160 | tf_op jit(solution)/shard_map/ppermute | solution.py:12
  182.3 2.3 %collective-permute-start.11 = (f32[16,256]{1,0:T(8,128)S(1)}, f32[16,256]{1,0:T(8,128)S(1)}, u32[]{:S(2)}, u32[]{:S(2)}) collective-permute-start(f32[16,256]{1,0:T(8,128)S(1)} %add.425), channel_id=1, source_target_pairs={{0,32},{16,48},{32,0},{48,16},{64,96},{80,112},{96,64},{112,80},{1... | collective-permute-start | bytes 49160 | tf_op jit(solution)/shard_map/ppermute | solution.py:12
  185.3 1.8 copy.38
  187.1 5.2 %collective-permute-start.12 = (f32[16,256]{1,0:T(8,128)S(1)}, f32[16,256]{1,0:T(8,128)S(1)}, u32[]{:S(2)}, u32[]{:S(2)}) collective-permute-start(f32[16,256]{1,0:T(8,128)S(1)} %add.426), channel_id=1, source_target_pairs={{0,64},{16,80},{32,96},{48,112},{64,0},{80,16},{96,32},{112,48},{1... | collective-permute-start | bytes 49160 | tf_op jit(solution)/shard_map/ppermute | solution.py:12
  192.3 1.4 fusion.12
  193.7 2.1 collective-permute-start.13
  195.8 5.9 %convolution_subtract_fusion.1 = f32[2048,256]{1,0:T(8,128)S(1)} fusion(f32[2048,256]{1,0:T(8,128)} %param.7, f32[256,2048]{1,0:T(8,128)} %all-gather.6.cloned.1.call-done, f32[256,256]{1,0:T(8,128)S(1)} %copy-done), kind=kOutput, calls=%fused_computation.3 | convolution fusion | flops 1611137024 | bytes 6553600 | tf_op jit(solution)/shard_map/dot_general | solution.py:134
  201.7 2.5 %collective-permute-start.14 = (f32[16,256]{1,0:T(8,128)S(1)}, f32[16,256]{1,0:T(8,128)S(1)}, u32[]{:S(2)}, u32[]{:S(2)}) collective-permute-start(f32[16,256]{1,0:T(8,128)S(1)} %add.428), channel_id=1, source_target_pairs={{0,256},{16,272},{32,288},{48,304},{64,320},{80,336},{96,352},{112... | collective-permute-start | bytes 49160 | tf_op jit(solution)/shard_map/ppermute | solution.py:12
  204.3 4.8 %convolution_subtract_fusion = f32[2048,256]{1,0:T(8,128)} fusion(f32[2048,256]{1,0:T(8,128)S(1)} %convolution_subtract_fusion.1, f32[256,2048]{1,0:T(8,128)S(1)} %fusion.29, f32[256,256]{1,0:T(8,128)S(1)} %fusion.12), kind=kOutput, calls=%fused_computation.2 | convolution fusion | flops 1611137024 | bytes 6553600 | tf_op jit(solution)/shard_map/dot_general | solution.py:134
  (110 shorter events, 24.9 us)
Async XLA Ops:
  7.2 177.5 %copy-start = (f32[256,256]{1,0:T(8,128)S(1)}, f32[256,256]{1,0:T(8,128)}, u32[]{:S(2)}) copy-start(f32[256,256]{1,0:T(8,128)} %param.9) | copy-start | bytes 786436
  7.2 18.2 %copy-start.1 = (f32[2048,256]{1,0:T(8,128)S(1)}, f32[2048,256]{1,0:T(8,128)}, u32[]{:S(2)}) copy-start(f32[2048,256]{1,0:T(8,128)} %param.7) | copy-start | bytes 6291460
  7.2 164.9 %all-gather.4.cloned.1.call-start = ((), (), s32[]{:S(2)}) async-start(), calls=%async_computation | async-start | bytes 2228224 | tf_op jit(solution)/shard_map/all_gather | solution.py:175
  7.9 187.9 %all-gather.6.cloned.1.call-start = ((), (), s32[]{:S(2)}) async-start(), calls=%async_computation.1 | async-start | bytes 2228224 | tf_op jit(solution)/shard_map/all_gather | solution.py:173
  16.6 9.9 %collective-permute-start = (f32[32,256]{0,1:T(8,128)S(1)}, f32[32,256]{0,1:T(8,128)S(1)}, u32[]{:S(2)}, u32[]{:S(2)}) collective-permute-start(f32[32,256]{0,1:T(8,128)S(1)} %select_bitcast_fusion), channel_id=1, source_target_pairs={{0,16},{16,0},{32,48},{48,32},{64,80},{80,64},{96,112},{112,96},{1... | collective-permute-start | bytes 98312 | tf_op jit(solution)/shard_map/ppermute | solution.py:12
  26.7 6.8 %collective-permute-start.1 = (f32[32,256]{0,1:T(8,128)S(1)}, f32[32,256]{0,1:T(8,128)S(1)}, u32[]{:S(2)}, u32[]{:S(2)}) collective-permute-start(f32[32,256]{0,1:T(8,128)S(1)} %fusion.87), channel_id=1, source_target_pairs={{0,32},{16,48},{32,0},{48,16},{64,96},{80,112},{96,64},{112,80},{1... | collective-permute-start | bytes 98312 | tf_op jit(solution)/shard_map/ppermute | solution.py:12
  33.5 7.2 %collective-permute-start.2 = (f32[32,256]{0,1:T(8,128)S(1)}, f32[32,256]{0,1:T(8,128)S(1)}, u32[]{:S(2)}, u32[]{:S(2)}) collective-permute-start(f32[32,256]{0,1:T(8,128)S(1)} %add.398), channel_id=1, source_target_pairs={{0,64},{16,80},{32,96},{48,112},{64,0},{80,16},{96,32},{112,48},{1... | collective-permute-start | bytes 98312 | tf_op jit(solution)/shard_map/ppermute | solution.py:12
  40.7 6.1 %collective-permute-start.3 = (f32[32,256]{0,1:T(8,128)S(1)}, f32[32,256]{0,1:T(8,128)S(1)}, u32[]{:S(2)}, u32[]{:S(2)}) collective-permute-start(f32[32,256]{0,1:T(8,128)S(1)} %add.399), channel_id=1, source_target_pairs={{0,128},{16,144},{32,160},{48,176},{64,192},{80,208},{96,224},{112... | collective-permute-start | bytes 98312 | tf_op jit(solution)/shard_map/ppermute | solution.py:12
  46.9 7.2 %collective-permute-start.4 = (f32[32,256]{0,1:T(8,128)S(1)}, f32[32,256]{0,1:T(8,128)S(1)}, u32[]{:S(2)}, u32[]{:S(2)}) collective-permute-start(f32[32,256]{0,1:T(8,128)S(1)} %add.400), channel_id=1, source_target_pairs={{0,256},{16,272},{32,288},{48,304},{64,320},{80,336},{96,352},{112... | collective-permute-start | bytes 98312 | tf_op jit(solution)/shard_map/ppermute | solution.py:12
  114.9 2.6 %copy-start.2 = (f32[256,256]{1,0:T(8,128)S(1)}, f32[256,256]{1,0:T(8,128)}, u32[]{:S(2)}) copy-start(f32[256,256]{1,0:T(8,128)} %shard_map.101) | copy-start | bytes 786436
  116.2 2.3 %copy-start.5 = (f32[256,256]{0,1:T(8,128)}, f32[256,256]{0,1:T(8,128)S(1)}, u32[]{:S(2)}) copy-start(f32[256,256]{0,1:T(8,128)S(1)} %get-tuple-element.25) | copy-start | bytes 786436
  122.9 11.9 %collective-permute-start.5 = (f32[256,256]{0,1:T(8,128)S(1)}, f32[256,256]{0,1:T(8,128)S(1)}, u32[]{:S(2)}, u32[]{:S(2)}) collective-permute-start(f32[256,256]{0,1:T(8,128)S(1)} %select_select_fusion), channel_id=1, source_target_pairs={{0,16},{16,0},{32,48},{48,32},{64,80},{80,64},{96,112},{112,96},{1... | collective-permute-start | bytes 786440 | tf_op jit(solution)/shard_map/ppermute | solution.py:12
  134.8 10.4 %collective-permute-start.6 = (f32[256,256]{0,1:T(8,128)S(1)}, f32[256,256]{0,1:T(8,128)S(1)}, u32[]{:S(2)}, u32[]{:S(2)}) collective-permute-start(f32[256,256]{0,1:T(8,128)S(1)} %add.420), channel_id=1, source_target_pairs={{0,32},{16,48},{32,0},{48,16},{64,96},{80,112},{96,64},{112,80},{1... | collective-permute-start | bytes 786440 | tf_op jit(solution)/shard_map/ppermute | solution.py:12
  145.2 12.1 %collective-permute-start.7 = (f32[256,256]{0,1:T(8,128)S(1)}, f32[256,256]{0,1:T(8,128)S(1)}, u32[]{:S(2)}, u32[]{:S(2)}) collective-permute-start(f32[256,256]{0,1:T(8,128)S(1)} %add.421), channel_id=1, source_target_pairs={{0,64},{16,80},{32,96},{48,112},{64,0},{80,16},{96,32},{112,48},{1... | collective-permute-start | bytes 786440 | tf_op jit(solution)/shard_map/ppermute | solution.py:12
  157.3 8.4 %collective-permute-start.8 = (f32[256,256]{0,1:T(8,128)S(1)}, f32[256,256]{0,1:T(8,128)S(1)}, u32[]{:S(2)}, u32[]{:S(2)}) collective-permute-start(f32[256,256]{0,1:T(8,128)S(1)} %add.422), channel_id=1, source_target_pairs={{0,128},{16,144},{32,160},{48,176},{64,192},{80,208},{96,224},{112... | collective-permute-start | bytes 786440 | tf_op jit(solution)/shard_map/ppermute | solution.py:12
  165.7 26.5 %collective-permute-start.9 = (f32[256,256]{0,1:T(8,128)S(1)}, f32[256,256]{0,1:T(8,128)}, u32[]{:S(2)}, u32[]{:S(2)}) collective-permute-start(f32[256,256]{0,1:T(8,128)S(1)} %add.423), channel_id=1, source_target_pairs={{0,256},{16,272},{32,288},{48,304},{64,320},{80,336},{96,352},{112... | collective-permute-start | bytes 786440 | tf_op jit(solution)/shard_map/ppermute | solution.py:12
  175.6 9.1 %copy-start.4 = (f32[16,16,256]{2,1,0:T(8,128)S(1)}, f32[16,16,256]{2,1,0:T(8,128)}, u32[]{:S(2)}) copy-start(f32[16,16,256]{2,1,0:T(8,128)} %get-tuple-element.32) | copy-start | bytes 786436
  175.7 11.4 %copy-start.6 = (f32[16,2048]{1,0:T(8,128)}, f32[16,2048]{1,0:T(8,128)S(1)}, u32[]{:S(2)}) copy-start(f32[16,2048]{1,0:T(8,128)S(1)} %constant_dynamic-slice_fusion) | copy-start | bytes 393220
  177.4 4.9 %collective-permute-start.10 = (f32[16,256]{1,0:T(8,128)S(1)}, f32[16,256]{1,0:T(8,128)S(1)}, u32[]{:S(2)}, u32[]{:S(2)}) collective-permute-start(f32[16,256]{1,0:T(8,128)S(1)} %fusion.37), channel_id=1, source_target_pairs={{0,16},{16,0},{32,48},{48,32},{64,80},{80,64},{96,112},{112,96},{1... | collective-permute-start | bytes 49160 | tf_op jit(solution)/shard_map/ppermute | solution.py:12
  182.3 4.7 %collective-permute-start.11 = (f32[16,256]{1,0:T(8,128)S(1)}, f32[16,256]{1,0:T(8,128)S(1)}, u32[]{:S(2)}, u32[]{:S(2)}) collective-permute-start(f32[16,256]{1,0:T(8,128)S(1)} %add.425), channel_id=1, source_target_pairs={{0,32},{16,48},{32,0},{48,16},{64,96},{80,112},{96,64},{112,80},{1... | collective-permute-start | bytes 49160 | tf_op jit(solution)/shard_map/ppermute | solution.py:12
  187.1 6.6 %collective-permute-start.12 = (f32[16,256]{1,0:T(8,128)S(1)}, f32[16,256]{1,0:T(8,128)S(1)}, u32[]{:S(2)}, u32[]{:S(2)}) collective-permute-start(f32[16,256]{1,0:T(8,128)S(1)} %add.426), channel_id=1, source_target_pairs={{0,64},{16,80},{32,96},{48,112},{64,0},{80,16},{96,32},{112,48},{1... | collective-permute-start | bytes 49160 | tf_op jit(solution)/shard_map/ppermute | solution.py:12
  193.6 10.6 %copy-start.3 = (f32[256,256]{1,0:T(8,128)}, f32[256,256]{1,0:T(8,128)S(1)}, u32[]{:S(2)}) copy-start(f32[256,256]{1,0:T(8,128)S(1)} %fusion.12) | copy-start | bytes 786436
  193.7 8.0 %collective-permute-start.13 = (f32[16,256]{1,0:T(8,128)S(1)}, f32[16,256]{1,0:T(8,128)S(1)}, u32[]{:S(2)}, u32[]{:S(2)}) collective-permute-start(f32[16,256]{1,0:T(8,128)S(1)} %add.427), channel_id=1, source_target_pairs={{0,128},{16,144},{32,160},{48,176},{64,192},{80,208},{96,224},{112... | collective-permute-start | bytes 49160 | tf_op jit(solution)/shard_map/ppermute | solution.py:12
  201.7 7.4 %collective-permute-start.14 = (f32[16,256]{1,0:T(8,128)S(1)}, f32[16,256]{1,0:T(8,128)S(1)}, u32[]{:S(2)}, u32[]{:S(2)}) collective-permute-start(f32[16,256]{1,0:T(8,128)S(1)} %add.428), channel_id=1, source_target_pairs={{0,256},{16,272},{32,288},{48,304},{64,320},{80,336},{96,352},{112... | collective-permute-start | bytes 49160 | tf_op jit(solution)/shard_map/ppermute | solution.py:12
Sparse Core Ops, SparseCore 0:
  10.1 71.5 all-gather.3
  83.8 69.3 all-gather.5

commit v11 on v7

--- a/solution.py
+++ b/solution.py
@@ -162,7 +162,8 @@
     own_trailing = jnp.take(trailing, local_rows, axis=0)
     own_columns = jnp.take(jnp.concatenate([panel_t, prev_lower_t], 0), local_rows, axis=1)
     own_pivots = jnp.concatenate([own_trailing, own_columns.T], 1)
-    pivot_data = butterfly_sum(jnp.where(owner_mask[:, None], own_pivots, 0.0), "rows")
+    own_pivots = jnp.where(owner_mask[:, None], own_pivots, 0.0)
+    pivot_data = butterfly_sum(own_pivots.reshape(-1, 128), "rows").reshape(own_pivots.shape)
     pivot_trailing = pivot_data[:, : own_trailing.shape[1]]
     pivot_columns = lax.all_gather(
         pivot_data[:, own_trailing.shape[1] :].T, "cols", axis=0, tiled=False

time: 204 us -> 196 us (0.961)
  waiting for transfers between devices: 42.9 us -> 33.9 us
    ppermute x10, waiting for transfers between devices: 42.2 us -> 33.1 us  [from_partner(): lax.ppermute(shard, axis, [(i, i ^ 1 << apart) for i in range(lax.axis_si...]
  transfers between devices with their start and end apart: 12 -> 12, of which waited for: 8 -> 8; matrix products, arithmetic and copies ran while one was open for 22% -> 23% of each run, Pallas kernels for 15% -> 15%
where the time goes in v11:
time: 196 us; the launch traced here: 194 us
  starting transfers between devices  42.2 us (22%)
  waiting for transfers between devices  33.9 us (17%)
  Pallas kernels  29.5 us (15%)
  matrix products  29.4 us (15%)
  blocking collectives  28.5 us (15%)
  between operations  14.7 us (8%)
  local copies, waits for them, and re-layouts  9.52 us (5%)
  other arithmetic  6.22 us (3%)
    ppermute x10, starting transfers between devices, from_partner(): lax.ppermute(shard, axis, [(i, i ^ 1 << apart) for i in range(lax.axis_si...  42.1 us
    ppermute x10, waiting for transfers between devices, from_partner(): lax.ppermute(shard, axis, [(i, i ^ 1 << apart) for i in range(lax.axis_si...  33.1 us
    pallas_call x1, Pallas kernels, factor(): pl.pallas_call(elimination_kernel, out_shape=jax.ShapeDtypeStruct(matrix....  29.5 us
    all_gather x1, blocking collectives, body(): lax.all_gather(pivot_data[:, own_trailing.shape[1]:].T, 'cols', axis=0, t...  28.5 us
    dot_general x29, matrix products, product(): return jnp.dot(left_side, right_side, precision=full_precision)  12.6 us
    dot_general x3, matrix products, contract_first(): lax.dot_general(left_side, right_side, (((0,), (0,)), ((), ())), precisio...  11.3 us
  transfers between devices with their start and end apart: 12, of which 8 were waited for; matrix products, arithmetic and copies ran while one was open for 23% of the time, Pallas kernels for 15%

profile of v11, /device:TPU:1, one launch (start us, length us, event | category | flops | bytes accessed | tf_op | source)
XLA Modules:
  0.0 193.9 jit_solution(1454827256708657266)
XLA Ops:
  8.0 0.9 fusion.21
  8.9 1.2 fusion.20
  10.4 1.7 pad_maximum_fusion
  12.4 1.3 copy.28
  14.9 0.8 select_reduce_fusion.1
  16.4 1.0 gather_fusion
  18.1 8.8 %collective-permute-start = (f32[576,128]{1,0:T(8,128)S(1)}, f32[576,128]{1,0:T(8,128)S(1)}, u32[]{:S(2)}, u32[]{:S(2)}) collective-permute-start(f32[576,128]{1,0:T(8,128)S(1)} %select_n.209), channel_id=1, source_target_pairs={{0,16},{16,0},{32,48},{48,32},{64,80},{80,64},{96,112},{112,96},{1... | collective-permute-start | bytes 884744 | tf_op jit(solution)/shard_map/ppermute | solution.py:12
  26.8 1.2 collective-permute-done
  28.1 1.9 collective-permute-start.1
  30.0 8.3 %collective-permute-done.1 = f32[576,128]{1,0:T(8,128)S(1)} collective-permute-done((f32[576,128]{1,0:T(8,128)S(1)}, f32[576,128]{1,0:T(8,128)S(1)}, u32[]{:S(2)}, u32[]{:S(2)}) %collective-permute-start.1) | collective-permute-done | bytes 294944 | tf_op jit(solution)/shard_map/ppermute | solution.py:12
  38.3 1.9 collective-permute-start.2
  40.3 8.9 %collective-permute-done.2 = f32[576,128]{1,0:T(8,128)S(1)} collective-permute-done((f32[576,128]{1,0:T(8,128)S(1)}, f32[576,128]{1,0:T(8,128)S(1)}, u32[]{:S(2)}, u32[]{:S(2)}) %collective-permute-start.2) | collective-permute-done | bytes 294944 | tf_op jit(solution)/shard_map/ppermute | solution.py:12
  49.2 1.9 collective-permute-start.3
  51.3 6.2 %collective-permute-done.3 = f32[576,128]{1,0:T(8,128)S(1)} collective-permute-done((f32[576,128]{1,0:T(8,128)S(1)}, f32[576,128]{1,0:T(8,128)S(1)}, u32[]{:S(2)}, u32[]{:S(2)}) %collective-permute-start.3) | collective-permute-done | bytes 294944 | tf_op jit(solution)/shard_map/ppermute | solution.py:12
  57.6 1.9 collective-permute-start.4
  59.7 6.8 %collective-permute-done.4 = f32[576,128]{1,0:T(8,128)S(1)} collective-permute-done((f32[576,128]{1,0:T(8,128)S(1)}, f32[576,128]{1,0:T(8,128)S(1)}, u32[]{:S(2)}, u32[]{:S(2)}) %collective-permute-start.4) | collective-permute-done | bytes 294944 | tf_op jit(solution)/shard_map/ppermute | solution.py:12
  66.9 28.5 %all-gather = f32[512,256]{1,0:T(8,128)S(1)} all-gather(f32[32,256]{1,0:T(8,128)S(1)} %copy.29), channel_id=2, replica_groups=mesh['rows'=32,'cols'=16] {'cols'}, dimensions={0}, use_global_device_ids=true | all-gather | bytes 557056 | tf_op jit(solution)/shard_map/all_gather | solution.py:168
  96.1 0.8 copy.30
  97.0 29.5 %shard_map.101 = f32[256,256]{1,0:T(8,128)} custom-call(f32[256,256]{1,0:T(8,128)} %bitcast.97), custom_call_target="tpu_custom_call" | custom-call | tf_op jit(solution)/shard_map/pallas_call | solution.py:125
  126.4 1.1 copy.31
  135.4 1.3 convolution_divide_fusion
  139.7 3.8 %fusion.27 = f32[256,2048]{1,0:T(8,128)S(1)} fusion(f32[256,256]{1,0:T(8,128)} %convolution_divide_fusion, f32[256,2048]{1,0:T(8,128)} %all-gather.4.cloned.1.call-done), kind=kOutput, calls=%fused_computation.123 | convolution fusion | flops 1610612736 | bytes 4456448 | tf_op jit(solution)/shard_map/dot_general | solution.py:181
  143.6 1.7 fusion.35
  145.3 11.3 %collective-permute-start.5 = (f32[16,256]{1,0:T(8,128)S(1)}, f32[16,256]{1,0:T(8,128)S(1)}, u32[]{:S(2)}, u32[]{:S(2)}) collective-permute-start(f32[16,256]{1,0:T(8,128)S(1)} %fusion.35), channel_id=1, source_target_pairs={{0,16},{16,0},{32,48},{48,32},{64,80},{80,64},{96,112},{112,96},{1... | collective-permute-start | bytes 49160 | tf_op jit(solution)/shard_map/ppermute | solution.py:12
  157.4 2.8 %collective-permute-start.6 = (f32[16,256]{1,0:T(8,128)S(1)}, f32[16,256]{1,0:T(8,128)S(1)}, u32[]{:S(2)}, u32[]{:S(2)}) collective-permute-start(f32[16,256]{1,0:T(8,128)S(1)} %add.389), channel_id=1, source_target_pairs={{0,32},{16,48},{32,0},{48,16},{64,96},{80,112},{96,64},{112,80},{1... | collective-permute-start | bytes 49160 | tf_op jit(solution)/shard_map/ppermute | solution.py:12
  160.9 1.0 collective-permute-done.6
  161.9 4.6 %collective-permute-start.7 = (f32[16,256]{1,0:T(8,128)S(1)}, f32[16,256]{1,0:T(8,128)}, u32[]{:S(2)}, u32[]{:S(2)}) collective-permute-start(f32[16,256]{1,0:T(8,128)S(1)} %add.390), channel_id=1, source_target_pairs={{0,64},{16,80},{32,96},{48,112},{64,0},{80,16},{96,32},{112,48},{1... | collective-permute-start | bytes 49160 | tf_op jit(solution)/shard_map/ppermute | solution.py:12
  166.9 0.8 copy.34
  168.7 3.0 %collective-permute-start.8 = (f32[16,256]{1,0:T(8,128)S(1)}, f32[16,256]{1,0:T(8,128)S(1)}, u32[]{:S(2)}, u32[]{:S(2)}) collective-permute-start(f32[16,256]{1,0:T(8,128)S(1)} %add.391), channel_id=1, source_target_pairs={{0,128},{16,144},{32,160},{48,176},{64,192},{80,208},{96,224},{112... | collective-permute-start | bytes 49160 | tf_op jit(solution)/shard_map/ppermute | solution.py:12
  171.7 5.9 %convolution_subtract_fusion.1 = f32[2048,256]{1,0:T(8,128)S(1)} fusion(f32[2048,256]{1,0:T(8,128)} %param.7, f32[256,2048]{1,0:T(8,128)} %all-gather.6.cloned.1.call-done, f32[256,256]{1,0:T(8,128)S(1)} %copy-done), kind=kOutput, calls=%fused_computation.3 | convolution fusion | flops 1611137024 | bytes 6553600 | tf_op jit(solution)/shard_map/dot_general | solution.py:134
  177.6 4.0 %collective-permute-start.9 = (f32[16,256]{1,0:T(8,128)S(1)}, f32[16,256]{1,0:T(8,128)S(1)}, u32[]{:S(2)}, u32[]{:S(2)}) collective-permute-start(f32[16,256]{1,0:T(8,128)S(1)} %add.392), channel_id=1, source_target_pairs={{0,256},{16,272},{32,288},{48,304},{64,320},{80,336},{96,352},{112... | collective-permute-start | bytes 49160 | tf_op jit(solution)/shard_map/ppermute | solution.py:12
  181.6 4.8 %convolution_subtract_fusion = f32[2048,256]{1,0:T(8,128)} fusion(f32[2048,256]{1,0:T(8,128)S(1)} %convolution_subtract_fusion.1, f32[256,2048]{1,0:T(8,128)S(1)} %fusion.27, f32[256,256]{1,0:T(8,128)S(1)} %fusion.12), kind=kOutput, calls=%fused_computation.2 | convolution fusion | flops 1611137024 | bytes 6553600 | tf_op jit(solution)/shard_map/dot_general | solution.py:134
  (98 shorter events, 19.5 us)
Async XLA Ops:
  7.2 153.1 %copy-start = (f32[256,256]{1,0:T(8,128)S(1)}, f32[256,256]{1,0:T(8,128)}, u32[]{:S(2)}) copy-start(f32[256,256]{1,0:T(8,128)} %param.9) | copy-start | bytes 786436
  7.2 9.2 %copy-start.1 = (f32[2048,256]{1,0:T(8,128)S(1)}, f32[2048,256]{1,0:T(8,128)}, u32[]{:S(2)}) copy-start(f32[2048,256]{1,0:T(8,128)} %param.7) | copy-start | bytes 6291460
  7.2 132.5 %all-gather.4.cloned.1.call-start = ((), (), s32[]{:S(2)}) async-start(), calls=%async_computation | async-start | bytes 2228224 | tf_op jit(solution)/shard_map/all_gather | solution.py:177
  7.9 163.8 %all-gather.6.cloned.1.call-start = ((), (), s32[]{:S(2)}) async-start(), calls=%async_computation.1 | async-start | bytes 2228224 | tf_op jit(solution)/shard_map/all_gather | solution.py:175
  18.1 10.0 %collective-permute-start = (f32[576,128]{1,0:T(8,128)S(1)}, f32[576,128]{1,0:T(8,128)S(1)}, u32[]{:S(2)}, u32[]{:S(2)}) collective-permute-start(f32[576,128]{1,0:T(8,128)S(1)} %select_n.209), channel_id=1, source_target_pairs={{0,16},{16,0},{32,48},{48,32},{64,80},{80,64},{96,112},{112,96},{1... | collective-permute-start | bytes 884744 | tf_op jit(solution)/shard_map/ppermute | solution.py:12
  28.1 10.2 %collective-permute-start.1 = (f32[576,128]{1,0:T(8,128)S(1)}, f32[576,128]{1,0:T(8,128)S(1)}, u32[]{:S(2)}, u32[]{:S(2)}) collective-permute-start(f32[576,128]{1,0:T(8,128)S(1)} %add.366), channel_id=1, source_target_pairs={{0,32},{16,48},{32,0},{48,16},{64,96},{80,112},{96,64},{112,80},{1... | collective-permute-start | bytes 884744 | tf_op jit(solution)/shard_map/ppermute | solution.py:12
  38.3 10.8 %collective-permute-start.2 = (f32[576,128]{1,0:T(8,128)S(1)}, f32[576,128]{1,0:T(8,128)S(1)}, u32[]{:S(2)}, u32[]{:S(2)}) collective-permute-start(f32[576,128]{1,0:T(8,128)S(1)} %add.367), channel_id=1, source_target_pairs={{0,64},{16,80},{32,96},{48,112},{64,0},{80,16},{96,32},{112,48},{1... | collective-permute-start | bytes 884744 | tf_op jit(solution)/shard_map/ppermute | solution.py:12
  49.2 8.4 %collective-permute-start.3 = (f32[576,128]{1,0:T(8,128)S(1)}, f32[576,128]{1,0:T(8,128)S(1)}, u32[]{:S(2)}, u32[]{:S(2)}) collective-permute-start(f32[576,128]{1,0:T(8,128)S(1)} %add.368), channel_id=1, source_target_pairs={{0,128},{16,144},{32,160},{48,176},{64,192},{80,208},{96,224},{112... | collective-permute-start | bytes 884744 | tf_op jit(solution)/shard_map/ppermute | solution.py:12
  57.6 9.0 %collective-permute-start.4 = (f32[576,128]{1,0:T(8,128)S(1)}, f32[576,128]{1,0:T(8,128)S(1)}, u32[]{:S(2)}, u32[]{:S(2)}) collective-permute-start(f32[576,128]{1,0:T(8,128)S(1)} %add.369), channel_id=1, source_target_pairs={{0,256},{16,272},{32,288},{48,304},{64,320},{80,336},{96,352},{112... | collective-permute-start | bytes 884744 | tf_op jit(solution)/shard_map/ppermute | solution.py:12
  130.5 2.1 %copy-start.2 = (f32[256,256]{1,0:T(8,128)S(1)}, f32[256,256]{1,0:T(8,128)}, u32[]{:S(2)}) copy-start(f32[256,256]{1,0:T(8,128)} %shard_map.101) | copy-start | bytes 786436
  143.5 16.7 %copy-start.3 = (f32[16,16,256]{2,1,0:T(8,128)S(1)}, f32[16,16,256]{2,1,0:T(8,128)}, u32[]{:S(2)}) copy-start(f32[16,16,256]{2,1,0:T(8,128)} %get-tuple-element.28) | copy-start | bytes 786436
  143.5 18.4 %copy-start.5 = (f32[16,2048]{1,0:T(8,128)}, f32[16,2048]{1,0:T(8,128)S(1)}, u32[]{:S(2)}) copy-start(f32[16,2048]{1,0:T(8,128)S(1)} %constant_dynamic-slice_fusion) | copy-start | bytes 393220
  145.3 12.1 %collective-permute-start.5 = (f32[16,256]{1,0:T(8,128)S(1)}, f32[16,256]{1,0:T(8,128)S(1)}, u32[]{:S(2)}, u32[]{:S(2)}) collective-permute-start(f32[16,256]{1,0:T(8,128)S(1)} %fusion.35), channel_id=1, source_target_pairs={{0,16},{16,0},{32,48},{48,32},{64,80},{80,64},{96,112},{112,96},{1... | collective-permute-start | bytes 49160 | tf_op jit(solution)/shard_map/ppermute | solution.py:12
  157.4 4.5 %collective-permute-start.6 = (f32[16,256]{1,0:T(8,128)S(1)}, f32[16,256]{1,0:T(8,128)S(1)}, u32[]{:S(2)}, u32[]{:S(2)}) collective-permute-start(f32[16,256]{1,0:T(8,128)S(1)} %add.389), channel_id=1, source_target_pairs={{0,32},{16,48},{32,0},{48,16},{64,96},{80,112},{96,64},{112,80},{1... | collective-permute-start | bytes 49160 | tf_op jit(solution)/shard_map/ppermute | solution.py:12
  161.9 6.1 %collective-permute-start.7 = (f32[16,256]{1,0:T(8,128)S(1)}, f32[16,256]{1,0:T(8,128)}, u32[]{:S(2)}, u32[]{:S(2)}) collective-permute-start(f32[16,256]{1,0:T(8,128)S(1)} %add.390), channel_id=1, source_target_pairs={{0,64},{16,80},{32,96},{48,112},{64,0},{80,16},{96,32},{112,48},{1... | collective-permute-start | bytes 49160 | tf_op jit(solution)/shard_map/ppermute | solution.py:12
  166.9 14.7 %copy-start.4 = (f32[256,256]{1,0:T(8,128)}, f32[256,256]{1,0:T(8,128)S(1)}, u32[]{:S(2)}) copy-start(f32[256,256]{1,0:T(8,128)S(1)} %fusion.12) | copy-start | bytes 786436
  168.7 8.9 %collective-permute-start.8 = (f32[16,256]{1,0:T(8,128)S(1)}, f32[16,256]{1,0:T(8,128)S(1)}, u32[]{:S(2)}, u32[]{:S(2)}) collective-permute-start(f32[16,256]{1,0:T(8,128)S(1)} %add.391), channel_id=1, source_target_pairs={{0,128},{16,144},{32,160},{48,176},{64,192},{80,208},{96,224},{112... | collective-permute-start | bytes 49160 | tf_op jit(solution)/shard_map/ppermute | solution.py:12
  177.6 8.8 %collective-permute-start.9 = (f32[16,256]{1,0:T(8,128)S(1)}, f32[16,256]{1,0:T(8,128)S(1)}, u32[]{:S(2)}, u32[]{:S(2)}) collective-permute-start(f32[16,256]{1,0:T(8,128)S(1)} %add.392), channel_id=1, source_target_pairs={{0,256},{16,272},{32,288},{48,304},{64,320},{80,336},{96,352},{112... | collective-permute-start | bytes 49160 | tf_op jit(solution)/shard_map/ppermute | solution.py:12
Sparse Core Ops, SparseCore 0:
  10.1 70.5 all-gather.3
  82.7 69.5 all-gather.5

commit v12 on v11

--- a/solution.py
+++ b/solution.py
@@ -160,7 +160,9 @@
     owner_mask = leaf_group == own_row
     local_rows = lookup(leaf_picks, jnp.zeros_like(leaf_slot), leaf_slot)
     own_trailing = jnp.take(trailing, local_rows, axis=0)
-    own_columns = jnp.take(jnp.concatenate([panel_t, prev_lower_t], 0), local_rows, axis=1)
+    own_columns = jnp.concatenate(
+        [jnp.take(panel_t, local_rows, axis=1), jnp.take(prev_lower_t, local_rows, axis=1)], 0
+    )
     own_pivots = jnp.concatenate([own_trailing, own_columns.T], 1)
     own_pivots = jnp.where(owner_mask[:, None], own_pivots, 0.0)
     pivot_data = butterfly_sum(own_pivots.reshape(-1, 128), "rows").reshape(own_pivots.shape)

time: 196 us -> 198 us (1.010)
  local copies, waits for them, and re-layouts: 9.52 us -> 13.6 us
  other arithmetic: 6.22 us -> 3.96 us
    unnamed x13 -> x17, local copies, waits for them, and re-layouts: 0.88 us -> 4.33 us
  transfers between devices with their start and end apart: 12 -> 12, of which waited for: 8 -> 8; matrix products, arithmetic and copies ran while one was open for 23% -> 24% of each run, Pallas kernels for 15% -> 15%
where the time goes in v12:
time: 198 us; the launch traced here: 196 us
  starting transfers between devices  42.6 us (22%)
  waiting for transfers between devices  34.1 us (17%)
  Pallas kernels  29.5 us (15%)
  matrix products  29.4 us (15%)
  blocking collectives  27.9 us (14%)
  between operations  14.8 us (7%)
  local copies, waits for them, and re-layouts  13.6 us (7%)
  other arithmetic  3.96 us (2%)
    ppermute x10, starting transfers between devices, from_partner(): lax.ppermute(shard, axis, [(i, i ^ 1 << apart) for i in range(lax.axis_si...  42.5 us
    ppermute x10, waiting for transfers between devices, from_partner(): lax.ppermute(shard, axis, [(i, i ^ 1 << apart) for i in range(lax.axis_si...  33.3 us
    pallas_call x1, Pallas kernels, factor(): pl.pallas_call(elimination_kernel, out_shape=jax.ShapeDtypeStruct(matrix....  29.5 us
    all_gather x1, blocking collectives, body(): lax.all_gather(pivot_data[:, own_trailing.shape[1]:].T, 'cols', axis=0, t...  27.9 us
    dot_general x29, matrix products, product(): return jnp.dot(left_side, right_side, precision=full_precision)  12.6 us
    dot_general x3, matrix products, contract_first(): lax.dot_general(left_side, right_side, (((0,), (0,)), ((), ())), precisio...  11.3 us
    unnamed x17, local copies, waits for them, and re-layouts  4.33 us
  transfers between devices with their start and end apart: 12, of which 8 were waited for; matrix products, arithmetic and copies ran while one was open for 24% of the time, Pallas kernels for 15%

profile of v12, /device:TPU:1, one launch (start us, length us, event | category | flops | bytes accessed | tf_op | source)
XLA Modules:
  0.0 195.8 jit_solution(10758045900312514015)
XLA Ops:
  8.0 1.2 copy.40
  9.2 0.9 fusion.21
  10.2 1.2 fusion.20
  12.3 2.2 %copy.41 = f32[16,2048]{0,1:T(8,128)} copy(f32[16,2048]{1,0:T(8,128)} %param.10) | data formatting | bytes 262144 | tf_op args[2]
  16.2 1.9 gather_fusion.2
  18.2 1.0 gather_fusion
  19.9 8.8 %collective-permute-start = (f32[576,128]{1,0:T(8,128)S(1)}, f32[576,128]{1,0:T(8,128)S(1)}, u32[]{:S(2)}, u32[]{:S(2)}) collective-permute-start(f32[576,128]{1,0:T(8,128)S(1)} %select_n.203), channel_id=1, source_target_pairs={{0,16},{16,0},{32,48},{48,32},{64,80},{80,64},{96,112},{112,96},{1... | collective-permute-start | bytes 884744 | tf_op jit(solution)/shard_map/ppermute | solution.py:12
  28.7 1.2 collective-permute-done
  30.0 1.9 collective-permute-start.1
  31.9 8.3 %collective-permute-done.1 = f32[576,128]{1,0:T(8,128)S(1)} collective-permute-done((f32[576,128]{1,0:T(8,128)S(1)}, f32[576,128]{1,0:T(8,128)S(1)}, u32[]{:S(2)}, u32[]{:S(2)}) %collective-permute-start.1) | collective-permute-done | bytes 294944 | tf_op jit(solution)/shard_map/ppermute | solution.py:12
  40.2 1.9 collective-permute-start.2
  42.1 8.9 %collective-permute-done.2 = f32[576,128]{1,0:T(8,128)S(1)} collective-permute-done((f32[576,128]{1,0:T(8,128)S(1)}, f32[576,128]{1,0:T(8,128)S(1)}, u32[]{:S(2)}, u32[]{:S(2)}) %collective-permute-start.2) | collective-permute-done | bytes 294944 | tf_op jit(solution)/shard_map/ppermute | solution.py:12
  51.1 1.9 collective-permute-start.3
  53.2 6.3 %collective-permute-done.3 = f32[576,128]{1,0:T(8,128)S(1)} collective-permute-done((f32[576,128]{1,0:T(8,128)S(1)}, f32[576,128]{1,0:T(8,128)S(1)}, u32[]{:S(2)}, u32[]{:S(2)}) %collective-permute-start.3) | collective-permute-done | bytes 294944 | tf_op jit(solution)/shard_map/ppermute | solution.py:12
  59.6 1.9 collective-permute-start.4
  61.7 6.8 %collective-permute-done.4 = f32[576,128]{1,0:T(8,128)S(1)} collective-permute-done((f32[576,128]{1,0:T(8,128)S(1)}, f32[576,128]{1,0:T(8,128)S(1)}, u32[]{:S(2)}, u32[]{:S(2)}) %collective-permute-start.4) | collective-permute-done | bytes 294944 | tf_op jit(solution)/shard_map/ppermute | solution.py:12
  68.9 27.9 %all-gather = f32[512,256]{1,0:T(8,128)S(1)} all-gather(f32[32,256]{1,0:T(8,128)S(1)} %copy.42), channel_id=2, replica_groups=mesh['rows'=32,'cols'=16] {'cols'}, dimensions={0}, use_global_device_ids=true | all-gather | bytes 557056 | tf_op jit(solution)/shard_map/all_gather | solution.py:170
  97.5 0.8 copy.43
  98.4 29.5 %shard_map.101 = f32[256,256]{1,0:T(8,128)} custom-call(f32[256,256]{1,0:T(8,128)} %bitcast.103), custom_call_target="tpu_custom_call" | custom-call | tf_op jit(solution)/shard_map/pallas_call | solution.py:125
  127.8 1.1 copy.44
  136.8 1.3 convolution_divide_fusion
  141.1 3.8 %fusion.27 = f32[256,2048]{1,0:T(8,128)S(1)} fusion(f32[256,256]{1,0:T(8,128)} %convolution_divide_fusion, f32[256,2048]{1,0:T(8,128)} %all-gather.4.cloned.1.call-done), kind=kOutput, calls=%fused_computation.126 | convolution fusion | flops 1610612736 | bytes 4456448 | tf_op jit(solution)/shard_map/dot_general | solution.py:183
  144.9 1.7 fusion.35
  146.7 11.3 %collective-permute-start.5 = (f32[16,256]{1,0:T(8,128)S(1)}, f32[16,256]{1,0:T(8,128)S(1)}, u32[]{:S(2)}, u32[]{:S(2)}) collective-permute-start(f32[16,256]{1,0:T(8,128)S(1)} %fusion.35), channel_id=1, source_target_pairs={{0,16},{16,0},{32,48},{48,32},{64,80},{80,64},{96,112},{112,96},{1... | collective-permute-start | bytes 49160 | tf_op jit(solution)/shard_map/ppermute | solution.py:12
  158.8 2.9 %collective-permute-start.6 = (f32[16,256]{1,0:T(8,128)S(1)}, f32[16,256]{1,0:T(8,128)S(1)}, u32[]{:S(2)}, u32[]{:S(2)}) collective-permute-start(f32[16,256]{1,0:T(8,128)S(1)} %add.391), channel_id=1, source_target_pairs={{0,32},{16,48},{32,0},{48,16},{64,96},{80,112},{96,64},{112,80},{1... | collective-permute-start | bytes 49160 | tf_op jit(solution)/shard_map/ppermute | solution.py:12
  162.4 1.0 collective-permute-done.6
  163.3 4.4 %collective-permute-start.7 = (f32[16,256]{1,0:T(8,128)S(1)}, f32[16,256]{1,0:T(8,128)}, u32[]{:S(2)}, u32[]{:S(2)}) collective-permute-start(f32[16,256]{1,0:T(8,128)S(1)} %add.392), channel_id=1, source_target_pairs={{0,64},{16,80},{32,96},{48,112},{64,0},{80,16},{96,32},{112,48},{1... | collective-permute-start | bytes 49160 | tf_op jit(solution)/shard_map/ppermute | solution.py:12
  168.2 0.8 copy.47
  170.1 3.1 %collective-permute-start.8 = (f32[16,256]{1,0:T(8,128)S(1)}, f32[16,256]{1,0:T(8,128)S(1)}, u32[]{:S(2)}, u32[]{:S(2)}) collective-permute-start(f32[16,256]{1,0:T(8,128)S(1)} %add.393), channel_id=1, source_target_pairs={{0,128},{16,144},{32,160},{48,176},{64,192},{80,208},{96,224},{112... | collective-permute-start | bytes 49160 | tf_op jit(solution)/shard_map/ppermute | solution.py:12
  173.3 5.9 %convolution_subtract_fusion.1 = f32[2048,256]{1,0:T(8,128)S(1)} fusion(f32[2048,256]{1,0:T(8,128)} %param.9, f32[256,2048]{1,0:T(8,128)} %all-gather.6.cloned.1.call-done, f32[256,256]{1,0:T(8,128)S(1)} %copy-done), kind=kOutput, calls=%fused_computation.4 | convolution fusion | flops 1611137024 | bytes 6553600 | tf_op jit(solution)/shard_map/dot_general | solution.py:134
  179.2 4.2 %collective-permute-start.9 = (f32[16,256]{1,0:T(8,128)S(1)}, f32[16,256]{1,0:T(8,128)S(1)}, u32[]{:S(2)}, u32[]{:S(2)}) collective-permute-start(f32[16,256]{1,0:T(8,128)S(1)} %add.394), channel_id=1, source_target_pairs={{0,256},{16,272},{32,288},{48,304},{64,320},{80,336},{96,352},{112... | collective-permute-start | bytes 49160 | tf_op jit(solution)/shard_map/ppermute | solution.py:12
  183.5 4.8 %convolution_subtract_fusion = f32[2048,256]{1,0:T(8,128)} fusion(f32[2048,256]{1,0:T(8,128)S(1)} %convolution_subtract_fusion.1, f32[256,2048]{1,0:T(8,128)S(1)} %fusion.27, f32[256,256]{1,0:T(8,128)S(1)} %fusion.12), kind=kOutput, calls=%fused_computation.3 | convolution fusion | flops 1611137024 | bytes 6553600 | tf_op jit(solution)/shard_map/dot_general | solution.py:134
  (104 shorter events, 19.9 us)
Async XLA Ops:
  7.2 154.6 %copy-start = (f32[256,256]{1,0:T(8,128)S(1)}, f32[256,256]{1,0:T(8,128)}, u32[]{:S(2)}) copy-start(f32[256,256]{1,0:T(8,128)} %param.11) | copy-start | bytes 786436
  7.2 8.2 %copy-start.6 = (s32[1,256]{1,0:T(1,128)S(1)}, s32[1,256]{1,0:T(1,128)}, u32[]{:S(2)}) copy-start(s32[1,256]{1,0:T(1,128)} %param.12) | copy-start | bytes 3076
  7.2 11.0 %copy-start.1 = (f32[2048,256]{1,0:T(8,128)S(1)}, f32[2048,256]{1,0:T(8,128)}, u32[]{:S(2)}) copy-start(f32[2048,256]{1,0:T(8,128)} %param.9) | copy-start | bytes 6291460
  7.2 133.9 %all-gather.4.cloned.1.call-start = ((), (), s32[]{:S(2)}) async-start(), calls=%async_computation | async-start | bytes 2228224 | tf_op jit(solution)/shard_map/all_gather | solution.py:179
  7.9 165.4 %all-gather.6.cloned.1.call-start = ((), (), s32[]{:S(2)}) async-start(), calls=%async_computation.1 | async-start | bytes 2228224 | tf_op jit(solution)/shard_map/all_gather | solution.py:177
  19.9 10.0 %collective-permute-start = (f32[576,128]{1,0:T(8,128)S(1)}, f32[576,128]{1,0:T(8,128)S(1)}, u32[]{:S(2)}, u32[]{:S(2)}) collective-permute-start(f32[576,128]{1,0:T(8,128)S(1)} %select_n.203), channel_id=1, source_target_pairs={{0,16},{16,0},{32,48},{48,32},{64,80},{80,64},{96,112},{112,96},{1... | collective-permute-start | bytes 884744 | tf_op jit(solution)/shard_map/ppermute | solution.py:12
  30.0 10.2 %collective-permute-start.1 = (f32[576,128]{1,0:T(8,128)S(1)}, f32[576,128]{1,0:T(8,128)S(1)}, u32[]{:S(2)}, u32[]{:S(2)}) collective-permute-start(f32[576,128]{1,0:T(8,128)S(1)} %add.368), channel_id=1, source_target_pairs={{0,32},{16,48},{32,0},{48,16},{64,96},{80,112},{96,64},{112,80},{1... | collective-permute-start | bytes 884744 | tf_op jit(solution)/shard_map/ppermute | solution.py:12
  40.2 10.8 %collective-permute-start.2 = (f32[576,128]{1,0:T(8,128)S(1)}, f32[576,128]{1,0:T(8,128)S(1)}, u32[]{:S(2)}, u32[]{:S(2)}) collective-permute-start(f32[576,128]{1,0:T(8,128)S(1)} %add.369), channel_id=1, source_target_pairs={{0,64},{16,80},{32,96},{48,112},{64,0},{80,16},{96,32},{112,48},{1... | collective-permute-start | bytes 884744 | tf_op jit(solution)/shard_map/ppermute | solution.py:12
  51.1 8.5 %collective-permute-start.3 = (f32[576,128]{1,0:T(8,128)S(1)}, f32[576,128]{1,0:T(8,128)S(1)}, u32[]{:S(2)}, u32[]{:S(2)}) collective-permute-start(f32[576,128]{1,0:T(8,128)S(1)} %add.370), channel_id=1, source_target_pairs={{0,128},{16,144},{32,160},{48,176},{64,192},{80,208},{96,224},{112... | collective-permute-start | bytes 884744 | tf_op jit(solution)/shard_map/ppermute | solution.py:12
  59.6 9.0 %collective-permute-start.4 = (f32[576,128]{1,0:T(8,128)S(1)}, f32[576,128]{1,0:T(8,128)S(1)}, u32[]{:S(2)}, u32[]{:S(2)}) collective-permute-start(f32[576,128]{1,0:T(8,128)S(1)} %add.371), channel_id=1, source_target_pairs={{0,256},{16,272},{32,288},{48,304},{64,320},{80,336},{96,352},{112... | collective-permute-start | bytes 884744 | tf_op jit(solution)/shard_map/ppermute | solution.py:12
  131.9 2.1 %copy-start.2 = (f32[256,256]{1,0:T(8,128)S(1)}, f32[256,256]{1,0:T(8,128)}, u32[]{:S(2)}) copy-start(f32[256,256]{1,0:T(8,128)} %shard_map.101) | copy-start | bytes 786436
  144.9 16.9 %copy-start.3 = (f32[16,16,256]{2,1,0:T(8,128)S(1)}, f32[16,16,256]{2,1,0:T(8,128)}, u32[]{:S(2)}) copy-start(f32[16,16,256]{2,1,0:T(8,128)} %get-tuple-element.34) | copy-start | bytes 786436
  144.9 18.4 %copy-start.5 = (f32[16,2048]{1,0:T(8,128)}, f32[16,2048]{1,0:T(8,128)S(1)}, u32[]{:S(2)}) copy-start(f32[16,2048]{1,0:T(8,128)S(1)} %constant_dynamic-slice_fusion) | copy-start | bytes 393220
  146.7 12.2 %collective-permute-start.5 = (f32[16,256]{1,0:T(8,128)S(1)}, f32[16,256]{1,0:T(8,128)S(1)}, u32[]{:S(2)}, u32[]{:S(2)}) collective-permute-start(f32[16,256]{1,0:T(8,128)S(1)} %fusion.35), channel_id=1, source_target_pairs={{0,16},{16,0},{32,48},{48,32},{64,80},{80,64},{96,112},{112,96},{1... | collective-permute-start | bytes 49160 | tf_op jit(solution)/shard_map/ppermute | solution.py:12
  158.8 4.5 %collective-permute-start.6 = (f32[16,256]{1,0:T(8,128)S(1)}, f32[16,256]{1,0:T(8,128)S(1)}, u32[]{:S(2)}, u32[]{:S(2)}) collective-permute-start(f32[16,256]{1,0:T(8,128)S(1)} %add.391), channel_id=1, source_target_pairs={{0,32},{16,48},{32,0},{48,16},{64,96},{80,112},{96,64},{112,80},{1... | collective-permute-start | bytes 49160 | tf_op jit(solution)/shard_map/ppermute | solution.py:12
  163.3 6.1 %collective-permute-start.7 = (f32[16,256]{1,0:T(8,128)S(1)}, f32[16,256]{1,0:T(8,128)}, u32[]{:S(2)}, u32[]{:S(2)}) collective-permute-start(f32[16,256]{1,0:T(8,128)S(1)} %add.392), channel_id=1, source_target_pairs={{0,64},{16,80},{32,96},{48,112},{64,0},{80,16},{96,32},{112,48},{1... | collective-permute-start | bytes 49160 | tf_op jit(solution)/shard_map/ppermute | solution.py:12
  168.2 15.3 %copy-start.4 = (f32[256,256]{1,0:T(8,128)}, f32[256,256]{1,0:T(8,128)S(1)}, u32[]{:S(2)}) copy-start(f32[256,256]{1,0:T(8,128)S(1)} %fusion.12) | copy-start | bytes 786436
  170.1 9.1 %collective-permute-start.8 = (f32[16,256]{1,0:T(8,128)S(1)}, f32[16,256]{1,0:T(8,128)S(1)}, u32[]{:S(2)}, u32[]{:S(2)}) collective-permute-start(f32[16,256]{1,0:T(8,128)S(1)} %add.393), channel_id=1, source_target_pairs={{0,128},{16,144},{32,160},{48,176},{64,192},{80,208},{96,224},{112... | collective-permute-start | bytes 49160 | tf_op jit(solution)/shard_map/ppermute | solution.py:12
  179.2 9.1 %collective-permute-start.9 = (f32[16,256]{1,0:T(8,128)S(1)}, f32[16,256]{1,0:T(8,128)S(1)}, u32[]{:S(2)}, u32[]{:S(2)}) collective-permute-start(f32[16,256]{1,0:T(8,128)S(1)} %add.394), channel_id=1, source_target_pairs={{0,256},{16,272},{32,288},{48,304},{64,320},{80,336},{96,352},{112... | collective-permute-start | bytes 49160 | tf_op jit(solution)/shard_map/ppermute | solution.py:12
Sparse Core Ops, SparseCore 0:
  10.1 69.9 all-gather.3
  82.2 70.3 all-gather.5
